TPU v7x, 256 devices: a whole 4x4x8 slice. The times are simulated.
256 devices in a mesh: ctx: 32 (over y, z), tp: 8 (over x, core).
Axes of the slice: x: 4, y: 4, z: 8, core: 2. Of those that a mesh axis runs over, the one named last changes fastest.
Arguments:
- tokens: bfloat16 [16384, 4096], P('ctx', 'tp'), may hold values from -6 to 6
- qkv_blocks: bfloat16 [3, 4, 1024, 1024], P(None, None, None, 'tp'), may hold values from -0.046875 to 0.046875
- out_blocks: bfloat16 [4, 1024, 1024], P(None, 'tp'), may hold values from -0.046875 to 0.046875
- mix_factors: float32 [4, 4, 4, 4], replicated, may hold values from -4 to 4
- head_gain: float32 [4, 1024], P(None, 'tp'), may hold values from 0.1 to 1.9
Outputs:
- layer_out: bfloat16 [16384, 4096], P('ctx', 'tp')
All inputs are finite; a program needn't handle non-finite values.
Results may differ from a plain program's by a relative error of at most 0.025.
Values may be sent and summed in bfloat16 or wider, within the bound.
No kernel may reach another device: no remote copies, remote signals or barrier semaphores. Data moves between devices by JAX's collectives and lax.ppermute only.
A program may use at most 128 MiB of HBM per device.

v0:
```python
import functools

import jax
import jax.numpy as jnp
from jax import lax
from jax.sharding import PartitionSpec as P

PHM = 4
SPAN = 128
HEAD = 128
BLOCK = 1024


epsilon = 1e-06


def exclusive_prefix(value, axis, devices):
    acc = value
    shift = 1
    while shift < devices:
        pairs = [(i, i + shift) for i in range(devices - shift)]
        acc = acc + lax.ppermute(acc, axis, pairs)
        shift *= 2
    return acc - value


def fold_weights(blocks, mixing):
    terms, rows, cols = blocks.shape
    folded = None
    for term_index in range(terms):
        part = (
            mixing[term_index][:, None, :, None]
            * blocks[term_index].astype(jnp.float32)[None, :, None, :]
        )
        folded = part if folded is None else folded + part
    return folded.astype(jnp.bfloat16).reshape(PHM * rows, PHM * cols)


def on_device(ctx_devices, tokens, qkv_blocks, out_blocks, mix_factors, head_gain):
    col_width = qkv_blocks.shape[-1]
    w_qkv = [fold_weights(qkv_blocks[p], mix_factors[p]) for p in range(3)]
    w_out = fold_weights(out_blocks, mix_factors[3])

    whole = lax.all_gather(tokens, "tp", axis=1, tiled=True)
    tok_rows = whole.shape[0]
    local_heads = PHM * col_width // HEAD
    nblk = tok_rows // SPAN

    def project(p):
        out = jnp.dot(whole, w_qkv[p], preferred_element_type=jnp.float32)
        return out.astype(jnp.bfloat16).reshape(nblk, SPAN, local_heads, HEAD)

    key_heads = project(1)
    value_heads = project(2)
    states = jnp.einsum(
        "nshd,nshe->nhde", key_heads, value_heads, preferred_element_type=jnp.float32
    )
    totals = jnp.sum(states, axis=0)
    earlier_sum = exclusive_prefix(totals, "ctx", ctx_devices)

    query_heads = project(0)
    scores = jnp.einsum(
        "nshd,nthd->nhst", query_heads, key_heads, preferred_element_type=jnp.float32
    )
    causal = jnp.arange(SPAN)[:, None] >= jnp.arange(SPAN)[None, :]
    scores = jnp.where(causal[None, None], scores, 0.0).astype(jnp.bfloat16)
    within = jnp.einsum("nhst,nthe->nshe", scores, value_heads, preferred_element_type=jnp.float32)

    prefixes = [earlier_sum]
    for n in range(1, nblk):
        prefixes.append(prefixes[-1] + states[n - 1])
    prefix = jnp.stack(prefixes, axis=0)
    prefix_hi = prefix.astype(jnp.bfloat16)
    prefix_lo = (prefix - prefix_hi.astype(jnp.float32)).astype(jnp.bfloat16)
    carried_out = jnp.einsum(
        "nshd,nhde->nshe", query_heads, prefix_hi, preferred_element_type=jnp.float32
    ) + jnp.einsum(
        "nshd,nhde->nshe", query_heads, prefix_lo, preferred_element_type=jnp.float32
    )
    combined = within + carried_out
    mean_sq = jnp.mean(combined * combined, axis=-1, keepdims=True)
    normed = combined * lax.rsqrt(mean_sq + epsilon) * head_gain
    attn = normed.astype(jnp.bfloat16).reshape(tok_rows, PHM * col_width)
    partial_value = jnp.dot(attn, w_out, preferred_element_type=jnp.float32)
    reduced = lax.psum_scatter(
        partial_value.astype(jnp.bfloat16),
        "tp",
        scatter_dimension=1,
        tiled=True,
    )
    return reduced


def solution(mesh):
    placed = (P("ctx", "tp"), P(None, None, None, "tp"), P(None, "tp", None), P(), P(None, "tp"))
    return jax.shard_map(
        functools.partial(on_device, mesh.shape["ctx"]),
        mesh=mesh,
        in_specs=placed,
        out_specs=P("ctx", "tp"),
        check_vma=False,
    )
```

profile of v0, /device:TPU:8, one launch (start us, length us, event | category | flops | bytes accessed | tf_op | source)
XLA Modules:
  0.0 184.3 jit_solution(11684833220325055081)
XLA Ops:
  6.5 0.0 all-gather.2.cloned.1.call-start
  6.5 0.7 all-gather.2.cloned.1.call-update
  7.3 0.0 reduce-scatter.2.cloned.1.call-start
  7.3 0.9 slice_bitcast_fusion.10
  8.2 2.4 %bitcast_convert_fusion.7 = (f32[1024,128]{1,0:T(8,128)S(1)}, f32[1024,128]{1,0:T(8,128)S(1)}, f32[1024,128]{1,0:T(8,128)S(1)}, f32[1024,128]{1,0:T(8,128)S(1)},...) fusion(bf16[3,4,1024,128]{3,2,1,0:T(8,128)(2,1)} %param.6), kind=kLoop, calls=%fused_computation.53 | loop fusion | flops 1572864 | bytes 9437184 | tf_op jit(solution)/shard_map/convert_element_type | solution.py:33
  10.6 5.6 %add_convert_fusion.3 = bf16[4,1024,4,128]{3,2,1,0:T(4,128)(2,1)} fusion(f32[1024,128]{1,0:T(8,128)S(1)} %get-tuple-element.13, f32[4,4]{1,0:T(4,128)S(1)} %get-tuple-element.35, f32[1024,128]{1,0:T(8,128)S(1)} %get-tuple-element.14, f32[4,4]{1,0:T(4,128)S(1)} %get-tuple-element.36, f32[1024,128]{1,0:T(8,128)S(1)} %get-tuple-element.15, ...), kind=kLoop, calls=%fused_computation.3 | loop fusion | flops 16777216 | bytes 6291712 | tf_op jit(solution)/shard_map/convert.18
  16.2 10.3 %add_convert_fusion.1 = (bf16[4,1024,4,128]{3,2,1,0:T(4,128)(2,1)}, bf16[4,1024,4,128]{3,2,1,0:T(4,128)(2,1)}) fusion(f32[1024,128]{1,0:T(8,128)S(1)} %get-tuple-element.17, f32[4,4]{1,0:T(4,128)S(1)} %get-tuple-element.28, f32[1024,128]{1,0:T(8,128)S(1)} %get-tuple-element.18, f32[4,4]{1,0:T(4,128)S(1)} %get-tuple-element.29, ...), kind=kLoop, calls=%fused_computation.1 | loop fusion | flops 33554432 | bytes 12583424 | tf_op jit(solution)/shard_map/convert.16
  26.5 20.2 %all-gather.2.cloned.1.call-done = bf16[512,4096]{1,0:T(8,128)(2,1)} async-done(((bf16[512,512]{1,0:T(8,128)(2,1)}), bf16[512,4096]{1,0:T(8,128)(2,1)}) %all-gather.2.cloned.1.call-update) | async-done | bytes 4194320 | tf_op jit(solution)/shard_map/all_gather | solution.py:44
  46.7 5.8 %fusion.22 = bf16[512,512]{0,1:T(8,128)(2,1)S(1)} fusion(bf16[512,4096]{1,0:T(8,128)(2,1)} %all-gather.2.cloned.1.call-done, bf16[512,8,4,128]{3,2,1,0:T(4,128)(2,1)} %bitcast.175), kind=kOutput, calls=%fused_computation.23 | convolution fusion | flops 2147745792 | bytes 8912896 | tf_op jit(solution)/shard_map/dot_general | solution.py:50
  52.5 0.1 reshape.307
  52.6 5.8 %fusion.28 = bf16[512,512]{0,1:T(8,128)(2,1)S(1)} fusion(bf16[512,4096]{1,0:T(8,128)(2,1)} %all-gather.2.cloned.1.call-done, bf16[512,8,4,128]{3,2,1,0:T(4,128)(2,1)} %bitcast.172), kind=kOutput, calls=%fused_computation.25 | convolution fusion | flops 2147745792 | bytes 8912896 | tf_op jit(solution)/shard_map/dot_general | solution.py:50
  58.5 0.0 copy-start.2
  58.5 0.1 reshape.305
  58.6 0.4 copy.15
  59.0 0.3 fusion.52
  59.3 3.5 %collective-permute-start = (f32[4,128,128]{2,1,0:T(8,128)S(1)}, f32[4,128,128]{2,1,0:T(8,128)S(1)}, u32[]{:S(2)}, u32[]{:S(2)}) collective-permute-start(f32[4,128,128]{2,1,0:T(8,128)S(1)} %get-tuple-element.41), channel_id=1, source_target_pairs={{0,8},{8,16},{16,24},{24,32},{32,40},{40,48},{48,56},{56,64},{64,7... | collective-permute-start | bytes 786440 | tf_op jit(solution)/shard_map/ppermute | solution.py:22
  62.8 9.0 %collective-permute-done = f32[4,128,128]{2,1,0:T(8,128)S(1)} collective-permute-done((f32[4,128,128]{2,1,0:T(8,128)S(1)}, f32[4,128,128]{2,1,0:T(8,128)S(1)}, u32[]{:S(2)}, u32[]{:S(2)}) %collective-permute-start) | collective-permute-done | bytes 262176 | tf_op jit(solution)/shard_map/ppermute | solution.py:22
  71.8 2.3 %collective-permute-start.1 = (f32[4,128,128]{2,1,0:T(8,128)S(1)}, f32[4,128,128]{2,1,0:T(8,128)S(1)}, u32[]{:S(2)}, u32[]{:S(2)}) collective-permute-start(f32[4,128,128]{2,1,0:T(8,128)S(1)} %add.143), channel_id=1, source_target_pairs={{0,16},{8,24},{16,32},{24,40},{32,48},{40,56},{48,64},{56,72},{64,... | collective-permute-start | bytes 786440 | tf_op jit(solution)/shard_map/ppermute | solution.py:22
  74.2 0.0 copy-done.2
  74.2 0.2 bitcast_convert_fusion.3
  74.4 14.1 %collective-permute-done.1 = f32[4,128,128]{2,1,0:T(8,128)S(1)} collective-permute-done((f32[4,128,128]{2,1,0:T(8,128)S(1)}, f32[4,128,128]{2,1,0:T(8,128)S(1)}, u32[]{:S(2)}, u32[]{:S(2)}) %collective-permute-start.1) | collective-permute-done | bytes 262176 | tf_op jit(solution)/shard_map/ppermute | solution.py:22
  88.5 7.0 %collective-permute-start.2 = (f32[4,128,128]{2,1,0:T(8,128)S(1)}, f32[4,128,128]{2,1,0:T(8,128)S(1)}, u32[]{:S(2)}, u32[]{:S(2)}) collective-permute-start(f32[4,128,128]{2,1,0:T(8,128)S(1)} %add.144), channel_id=1, source_target_pairs={{0,32},{8,40},{16,48},{24,56},{32,64},{40,72},{48,80},{56,88},{64,... | collective-permute-start | bytes 786440 | tf_op jit(solution)/shard_map/ppermute | solution.py:22
  95.5 4.6 %add_convert_fusion = bf16[4,128,4,1024]{3,2,1,0:T(4,128)(2,1)S(1)} fusion(f32[128,1024]{1,0:T(8,128)S(1)} %get-tuple-element.23, f32[4,4]{1,0:T(4,128)S(1)} %get-tuple-element.39, f32[128,1024]{1,0:T(8,128)S(1)} %get-tuple-element.24, f32[4,4]{1,0:T(4,128)S(1)} %get-tuple-element.40, f32[128,1024]{1,0:T(8,128)S(1)} %get-tuple-element.22, ...), kind=kLoop, calls=%fused_computation | loop fusion | flops 16777216 | bytes 6291712 | tf_op jit(solution)/shard_map/convert_element_type | solution.py:36
  100.2 0.0 copy-start
  100.2 0.0 copy-start.4
  100.2 4.4 %copy.27 = bf16[64,8,4,1024]{3,1,2,0:T(8,128)(2,1)} copy(bf16[64,8,4,1024]{3,2,1,0:T(4,128)(2,1)S(1)} %bitcast.171) | data formatting | bytes 8388608
  104.6 3.3 %collective-permute-done.2 = f32[4,128,128]{2,1,0:T(8,128)S(1)} collective-permute-done((f32[4,128,128]{2,1,0:T(8,128)S(1)}, f32[4,128,128]{2,1,0:T(8,128)S(1)}, u32[]{:S(2)}, u32[]{:S(2)}) %collective-permute-start.2) | collective-permute-done | bytes 262176 | tf_op jit(solution)/shard_map/ppermute | solution.py:22
  107.8 0.7 add.145
  108.6 3.4 %collective-permute-start.3 = (f32[4,128,128]{2,1,0:T(8,128)}, f32[4,128,128]{2,1,0:T(8,128)}, u32[]{:S(2)}, u32[]{:S(2)}) collective-permute-start(f32[4,128,128]{2,1,0:T(8,128)} %add.145), channel_id=1, source_target_pairs={{0,64},{8,72},{16,80},{24,88},{32,96},{40,104},{48,112},{56,120},{... | collective-permute-start | bytes 786440 | tf_op jit(solution)/shard_map/ppermute | solution.py:22
  112.0 0.0 copy-done
  112.0 0.0 copy-done.4
  112.0 2.4 %fusion.25 = bf16[512,512]{0,1:T(8,128)(2,1)S(1)} fusion(bf16[512,4096]{1,0:T(8,128)(2,1)S(1)} %copy-done.4, bf16[512,8,4,128]{3,2,1,0:T(4,128)(2,1)S(1)} %bitcast.173), kind=kOutput, calls=%fused_computation.24 | convolution fusion | flops 2147745792 | bytes 8912896 | tf_op jit(solution)/shard_map/dot_general | solution.py:50
  114.4 0.1 reshape.306
  114.5 0.4 copy.17
  114.9 3.2 %collective-permute-done.3 = f32[4,128,128]{2,1,0:T(8,128)} collective-permute-done((f32[4,128,128]{2,1,0:T(8,128)}, f32[4,128,128]{2,1,0:T(8,128)}, u32[]{:S(2)}, u32[]{:S(2)}) %collective-permute-start.3) | collective-permute-done | bytes 262176 | tf_op jit(solution)/shard_map/ppermute | solution.py:22
  118.1 1.1 add.146
  119.2 4.7 %collective-permute-start.4 = (f32[4,128,128]{2,1,0:T(8,128)S(1)}, f32[4,128,128]{2,1,0:T(8,128)S(1)}, u32[]{:S(2)}, u32[]{:S(2)}) collective-permute-start(f32[4,128,128]{2,1,0:T(8,128)S(1)} %add.146), channel_id=1, source_target_pairs={{0,128},{8,136},{16,144},{24,152},{32,160},{40,168},{48,176},{56,1... | collective-permute-start | bytes 786440 | tf_op jit(solution)/shard_map/ppermute | solution.py:22
  123.9 1.6 fusion.21
  125.6 0.0 copy-start.1
  125.6 2.6 %collective-permute-done.4 = f32[4,128,128]{2,1,0:T(8,128)S(1)} collective-permute-done((f32[4,128,128]{2,1,0:T(8,128)S(1)}, f32[4,128,128]{2,1,0:T(8,128)S(1)}, u32[]{:S(2)}, u32[]{:S(2)}) %collective-permute-start.4) | collective-permute-done | bytes 262176 | tf_op jit(solution)/shard_map/ppermute | solution.py:22
  128.1 0.1 fusion.47
  128.2 0.0 copy-start.3
  128.2 0.1 fusion.51
  128.3 0.5 fusion.41
  128.8 0.0 copy-done.1
  128.8 0.5 multiply_reduce_fusion
  129.4 0.0 copy-done.3
  129.4 0.2 multiply_convert_fusion
  129.6 0.3 copy.20
  129.9 6.5 %convolution_convert_fusion = bf16[512,4096]{1,0:T(8,128)(2,1)} fusion(bf16[512,4096]{1,0:T(8,128)(2,1)} %bitcast.174, bf16[64,8,4,128]{3,2,1,0:T(4,128)(2,1)S(1)} %bitcast.178), kind=kOutput, calls=%fused_computation.4 | convolution fusion | flops 2149580800 | bytes 8912896 | tf_op jit(solution)/shard_map/dot_general | solution.py:84
  136.4 0.0 reduce-scatter.2.cloned.1.call-update
  136.4 41.1 %reduce-scatter.2.cloned.1.call-done = bf16[512,512]{1,0:T(8,128)(2,1)} async-done(((bf16[512,4096]{1,0:T(8,128)(2,1)}), bf16[512,512]{1,0:T(8,128)(2,1)}) %reduce-scatter.2.cloned.1.call-update) | async-done | bytes 524304 | tf_op jit(solution)/shard_map/reduce_scatter | solution.py:85
  (4 shorter events, 0.1 us)
Async XLA Ops:
  6.5 40.1 %all-gather.2.cloned.1.call-start = ((), (), s32[]{:S(2)}) async-start(), calls=%async_computation.1 | async-start | bytes 4718592 | tf_op jit(solution)/shard_map/all_gather | solution.py:44
  7.3 170.2 %reduce-scatter.2.cloned.1.call-start = ((), (), s32[]{:S(2)}) async-start(), calls=%async_computation.2 | async-start | bytes 4718592 | tf_op jit(solution)/shard_map/reduce_scatter | solution.py:85
  58.5 15.7 %copy-start.2 = (bf16[4,128,1024]{2,1,0:T(8,128)(2,1)S(1)}, bf16[4,128,1024]{2,1,0:T(8,128)(2,1)}, u32[]{:S(2)}) copy-start(bf16[4,128,1024]{2,1,0:T(8,128)(2,1)} %param.7) | copy-start | bytes 3145732
  59.3 12.5 %collective-permute-start = (f32[4,128,128]{2,1,0:T(8,128)S(1)}, f32[4,128,128]{2,1,0:T(8,128)S(1)}, u32[]{:S(2)}, u32[]{:S(2)}) collective-permute-start(f32[4,128,128]{2,1,0:T(8,128)S(1)} %get-tuple-element.41), channel_id=1, source_target_pairs={{0,8},{8,16},{16,24},{24,32},{32,40},{40,48},{48,56},{56,64},{64,7... | collective-permute-start | bytes 786440 | tf_op jit(solution)/shard_map/ppermute | solution.py:22
  71.8 16.7 %collective-permute-start.1 = (f32[4,128,128]{2,1,0:T(8,128)S(1)}, f32[4,128,128]{2,1,0:T(8,128)S(1)}, u32[]{:S(2)}, u32[]{:S(2)}) collective-permute-start(f32[4,128,128]{2,1,0:T(8,128)S(1)} %add.143), channel_id=1, source_target_pairs={{0,16},{8,24},{16,32},{24,40},{32,48},{40,56},{48,64},{56,72},{64,... | collective-permute-start | bytes 786440 | tf_op jit(solution)/shard_map/ppermute | solution.py:22
  88.5 19.3 %collective-permute-start.2 = (f32[4,128,128]{2,1,0:T(8,128)S(1)}, f32[4,128,128]{2,1,0:T(8,128)S(1)}, u32[]{:S(2)}, u32[]{:S(2)}) collective-permute-start(f32[4,128,128]{2,1,0:T(8,128)S(1)} %add.144), channel_id=1, source_target_pairs={{0,32},{8,40},{16,48},{24,56},{32,64},{40,72},{48,80},{56,88},{64,... | collective-permute-start | bytes 786440 | tf_op jit(solution)/shard_map/ppermute | solution.py:22
  100.2 11.8 %copy-start = (bf16[4,1024,4,128]{3,2,1,0:T(4,128)(2,1)S(1)}, bf16[4,1024,4,128]{3,2,1,0:T(4,128)(2,1)}, u32[]{:S(2)}) copy-start(bf16[4,1024,4,128]{3,2,1,0:T(4,128)(2,1)} %get-tuple-element.46) | copy-start | bytes 12582916
  100.2 11.8 %copy-start.4 = (bf16[512,4096]{1,0:T(8,128)(2,1)S(1)}, bf16[512,4096]{1,0:T(8,128)(2,1)}, u32[]{:S(2)}) copy-start(bf16[512,4096]{1,0:T(8,128)(2,1)} %all-gather.2.cloned.1.call-done) | copy-start | bytes 12582916
  108.6 9.6 %collective-permute-start.3 = (f32[4,128,128]{2,1,0:T(8,128)}, f32[4,128,128]{2,1,0:T(8,128)}, u32[]{:S(2)}, u32[]{:S(2)}) collective-permute-start(f32[4,128,128]{2,1,0:T(8,128)} %add.145), channel_id=1, source_target_pairs={{0,64},{8,72},{16,80},{24,88},{32,96},{40,104},{48,112},{56,120},{... | collective-permute-start | bytes 786440 | tf_op jit(solution)/shard_map/ppermute | solution.py:22
  119.2 9.0 %collective-permute-start.4 = (f32[4,128,128]{2,1,0:T(8,128)S(1)}, f32[4,128,128]{2,1,0:T(8,128)S(1)}, u32[]{:S(2)}, u32[]{:S(2)}) collective-permute-start(f32[4,128,128]{2,1,0:T(8,128)S(1)} %add.146), channel_id=1, source_target_pairs={{0,128},{8,136},{16,144},{24,152},{32,160},{40,168},{48,176},{56,1... | collective-permute-start | bytes 786440 | tf_op jit(solution)/shard_map/ppermute | solution.py:22
  125.6 3.2 %copy-start.1 = (f32[4,4,128,128]{3,2,1,0:T(8,128)S(1)}, f32[4,4,128,128]{3,2,1,0:T(8,128)}, u32[]{:S(2)}) copy-start(f32[4,4,128,128]{3,2,1,0:T(8,128)} %fusion.21) | copy-start | bytes 3145732
  128.2 1.2 copy-start.3
Sparse Core Ops, SparseCore 0:
  9.2 37.4 all-gather.1
  136.5 40.9 reduce-scatter.1
where the time goes:
time: 185 us; the launch traced here: 184 us
  waiting for transfers between devices  94 us (51%)
  other arithmetic  25.4 us (14%)
  matrix products  23.6 us (13%)
  starting transfers between devices  21 us (11%)
  between operations  13.6 us (7%)
  local copies, waits for them, and re-layouts  6.68 us (4%)
    reduce_scatter x1, waiting for transfers between devices, on_device(): lax.psum_scatter(partial_value.astype(jnp.bfloat16), 'tp', scatter_dimens...  41.1 us
    ppermute x5, waiting for transfers between devices, exclusive_prefix(): acc = acc + lax.ppermute(acc, axis, pairs)  32.1 us
    ppermute x5, starting transfers between devices, exclusive_prefix(): acc = acc + lax.ppermute(acc, axis, pairs)  20.9 us
    all_gather x1, waiting for transfers between devices, on_device(): whole = lax.all_gather(tokens, 'tp', axis=1, tiled=True)  20.2 us
    another operation x2, other arithmetic  15.9 us
    dot_general x3, matrix products, project(): out = jnp.dot(whole, w_qkv[p], preferred_element_type=jnp.float32)  14.1 us
    dot_general x1, matrix products, on_device(): partial_value = jnp.dot(attn, w_out, preferred_element_type=jnp.float32)  6.49 us
    convert_element_type x1, other arithmetic, fold_weights(): return folded.astype(jnp.bfloat16).reshape(PHM * rows, PHM * cols)  4.63 us
  transfers between devices with their start and end apart: 7, of which 7 were waited for; matrix products, arithmetic and copies ran while one was open for 18% of the time, Pallas kernels for 0%

commit v1 on v0

--- a/solution.py
+++ b/solution.py
@@ -14,14 +14,28 @@
 epsilon = 1e-06
 
 
-def exclusive_prefix(value, axis, devices):
-    acc = value
-    shift = 1
-    while shift < devices:
-        pairs = [(i, i + shift) for i in range(devices - shift)]
-        acc = acc + lax.ppermute(acc, axis, pairs)
-        shift *= 2
-    return acc - value
+def ring_gather(value, axis, devices, size, stride):
+    here = lax.axis_index(axis)
+    slots = [value]
+    for shift in range(1, size):
+        pairs = []
+        for i in range(devices):
+            k = (i // stride) % size
+            pairs.append((i, i + ((k + shift) % size - k) * stride))
+        slots.append(lax.ppermute(value, axis, pairs))
+    source = ((here // stride) % size - jnp.arange(size)) % size
+    return jnp.stack(slots).astype(jnp.float32), source
+
+
+def exclusive_prefix(value, axis, devices, row):
+    here = lax.axis_index(axis)
+    pos, col = here % row, here // row
+    within, source = ring_gather(value.astype(jnp.bfloat16), axis, devices, row, 1)
+    before = jnp.einsum("k,k...->...", (source < pos).astype(jnp.float32), within)
+    row_total = jnp.sum(within, axis=0)
+    cols = devices // row
+    across, source = ring_gather(row_total.astype(jnp.bfloat16), axis, devices, cols, row)
+    return before + jnp.einsum("k,k...->...", (source < col).astype(jnp.float32), across)
 
 
 def fold_weights(blocks, mixing):
@@ -36,19 +50,22 @@
     return folded.astype(jnp.bfloat16).reshape(PHM * rows, PHM * cols)
 
 
-def on_device(ctx_devices, tokens, qkv_blocks, out_blocks, mix_factors, head_gain):
+def on_device(ctx_devices, ctx_row, tokens, qkv_blocks, out_blocks, mix_factors, head_gain):
     col_width = qkv_blocks.shape[-1]
-    w_qkv = [fold_weights(qkv_blocks[p], mix_factors[p]) for p in range(3)]
+    w_qkv = jnp.concatenate(
+        [fold_weights(qkv_blocks[p], mix_factors[p]) for p in range(3)], axis=1
+    )
     w_out = fold_weights(out_blocks, mix_factors[3])
 
     whole = lax.all_gather(tokens, "tp", axis=1, tiled=True)
     tok_rows = whole.shape[0]
     local_heads = PHM * col_width // HEAD
     nblk = tok_rows // SPAN
+    qkv = jnp.dot(whole, w_qkv, preferred_element_type=jnp.float32).astype(jnp.bfloat16)
 
     def project(p):
-        out = jnp.dot(whole, w_qkv[p], preferred_element_type=jnp.float32)
-        return out.astype(jnp.bfloat16).reshape(nblk, SPAN, local_heads, HEAD)
+        part = qkv[:, p * PHM * col_width:(p + 1) * PHM * col_width]
+        return part.reshape(nblk, SPAN, local_heads, HEAD)
 
     key_heads = project(1)
     value_heads = project(2)
@@ -56,7 +73,7 @@
         "nshd,nshe->nhde", key_heads, value_heads, preferred_element_type=jnp.float32
     )
     totals = jnp.sum(states, axis=0)
-    earlier_sum = exclusive_prefix(totals, "ctx", ctx_devices)
+    earlier_sum = exclusive_prefix(totals, "ctx", ctx_devices, ctx_row)
 
     query_heads = project(0)
     scores = jnp.einsum(
@@ -91,10 +108,15 @@
     return reduced
 
 
+def ctx_row_of(mesh):
+    n = mesh.shape["ctx"]
+    return 8 if n % 8 == 0 else n
+
+
 def solution(mesh):
     placed = (P("ctx", "tp"), P(None, None, None, "tp"), P(None, "tp", None), P(), P(None, "tp"))
     return jax.shard_map(
-        functools.partial(on_device, mesh.shape["ctx"]),
+        functools.partial(on_device, mesh.shape["ctx"], ctx_row_of(mesh)),
         mesh=mesh,
         in_specs=placed,
         out_specs=P("ctx", "tp"),

time: 185 us -> 161 us (0.87)
  waiting for transfers between devices: 94 us -> 59.3 us
  local copies, waits for them, and re-layouts: 6.68 us -> 18.9 us
  other arithmetic: 25.4 us -> 22.5 us
    ppermute x5 -> x10, waiting for transfers between devices: 32.1 us -> 15 us  [ring_gather(): slots.append(lax.ppermute(value, axis, pairs))]
    all_gather x1, waiting for transfers between devices: 20.2 us -> 5.13 us  [on_device(): whole = lax.all_gather(tokens, 'tp', axis=1, tiled=True)]
    unnamed x11 -> x17, local copies, waits for them, and re-layouts: 4.38 us -> 15.1 us
    reduce_scatter x1, waiting for transfers between devices: 41.1 us -> 38.5 us  [on_device(): lax.psum_scatter(partial_value.astype(jnp.bfloat16), 'tp', scatter_dimens...]
    another operation x2 -> x3, other arithmetic: 15.9 us -> 13.8 us
    add x4 -> x0, other arithmetic: 1.86 us -> none  [exclusive_prefix(): acc = acc + lax.ppermute(acc, axis, pairs)]
    ppermute x5 -> x10, starting transfers between devices: 20.9 us -> 21.8 us  [ring_gather(): slots.append(lax.ppermute(value, axis, pairs))]
  transfers between devices with their start and end apart: 7 -> 12, of which waited for: 7 -> 9; matrix products, arithmetic and copies ran while one was open for 18% -> 25% of each run, Pallas kernels for 0% -> 0%
where the time goes in v1:
time: 161 us
  waiting for transfers between devices  59.3 us (37%)
  matrix products  24.6 us (15%)
  other arithmetic  22.5 us (14%)
  starting transfers between devices  21.9 us (14%)
  local copies, waits for them, and re-layouts  18.9 us (12%)
  between operations  13.7 us (9%)
    reduce_scatter x1, waiting for transfers between devices, on_device(): lax.psum_scatter(partial_value.astype(jnp.bfloat16), 'tp', scatter_dimens...  38.5 us
    ppermute x10, starting transfers between devices, ring_gather(): slots.append(lax.ppermute(value, axis, pairs))  21.8 us
    unnamed x17, local copies, waits for them, and re-layouts  15.1 us
    ppermute x10, waiting for transfers between devices, ring_gather(): slots.append(lax.ppermute(value, axis, pairs))  15 us
    dot_general x1, matrix products, on_device(): jnp.dot(whole, w_qkv, preferred_element_type=jnp.float32)  13.8 us
    another operation x2, other arithmetic  13.7 us
    dot_general x1, matrix products, on_device(): partial_value = jnp.dot(attn, w_out, preferred_element_type=jnp.float32)  6.53 us
    all_gather x1, waiting for transfers between devices, on_device(): whole = lax.all_gather(tokens, 'tp', axis=1, tiled=True)  5.13 us
  transfers between devices with their start and end apart: 12, of which 9 were waited for; matrix products, arithmetic and copies ran while one was open for 25% of the time, Pallas kernels for 0%

profile of v1, /device:TPU:8, one launch (start us, length us, event | category | flops | bytes accessed | tf_op | source)
XLA Modules:
  0.0 160.8 jit_solution(9527223819864626604)
XLA Ops:
  6.5 0.0 all-gather.2.cloned.1.call-start
  6.5 0.7 all-gather.2.cloned.1.call-update
  7.3 0.0 reduce-scatter.2.cloned.1.call-start
  7.3 0.9 slice_bitcast_fusion.18
  8.2 2.2 %bitcast_convert_fusion.15 = (f32[1024,128]{1,0:T(8,128)S(1)}, f32[1024,128]{1,0:T(8,128)S(1)}, f32[1024,128]{1,0:T(8,128)S(1)}, f32[1024,128]{1,0:T(8,128)S(1)}...) fusion(bf16[3,4,1024,128]{3,2,1,0:T(8,128)(2,1)} %param.6), kind=kLoop, calls=%fused_computation.62 | loop fusion | flops 1572864 | bytes 9437184 | tf_op jit(solution)/shard_map/convert_element_type | solution.py:47
  10.4 9.1 %add_convert_fusion.1 = (bf16[4,1024,4,128]{3,2,1,0:T(4,128)(2,1)S(1)}, bf16[4,1024,4,128]{3,2,1,0:T(4,128)(2,1)S(1)}) fusion(f32[1024,128]{1,0:T(8,128)S(1)} %get-tuple-element.17, f32[4,4]{1,0:T(4,128)S(1)} %get-tuple-element.30, f32[1024,128]{1,0:T(8,128)S(1)} %get-tuple-element.18, f32[4,4]{1,0:T(4,128)S(1)} %get-tuple-element.31, ...), kind=kLoop, calls=%fused_computation.7 | loop fusion | flops 33554432 | bytes 12583424 | tf_op jit(solution)/shard_map/convert.17
  19.6 2.7 %copy.52 = bf16[512,8,4,128]{3,1,2,0:T(8,128)(2,1)} copy(bf16[512,8,4,128]{3,2,1,0:T(4,128)(2,1)S(1)} %bitcast.181) | data formatting | bytes 8388608
  22.2 2.6 %copy.53 = bf16[512,8,4,128]{3,1,2,0:T(8,128)(2,1)} copy(bf16[512,8,4,128]{3,2,1,0:T(4,128)(2,1)S(1)} %bitcast.180) | data formatting | bytes 8388608
  24.9 4.6 %add_convert_fusion.3 = bf16[4,1024,4,128]{3,2,1,0:T(4,128)(2,1)S(1)} fusion(f32[1024,128]{1,0:T(8,128)S(1)} %get-tuple-element.14, f32[4,4]{1,0:T(4,128)S(1)} %get-tuple-element.38, f32[1024,128]{1,0:T(8,128)S(1)} %get-tuple-element.15, f32[4,4]{1,0:T(4,128)S(1)} %get-tuple-element.39, f32[1024,128]{1,0:T(8,128)S(1)} %get-tuple-element.16, ...), kind=kLoop, calls=%fused_computation.9 | loop fusion | flops 16777216 | bytes 6291712 | tf_op jit(solution)/shard_map/convert.19
  29.5 0.0 copy-start.1
  29.5 2.7 %copy.54 = bf16[512,8,4,128]{3,1,2,0:T(8,128)(2,1)} copy(bf16[512,8,4,128]{3,2,1,0:T(4,128)(2,1)S(1)} %bitcast.182) | data formatting | bytes 8388608
  32.2 0.0 copy-done.1
  32.2 0.2 bitcast_convert_fusion.3
  32.4 4.8 %add_convert_fusion = bf16[4,128,4,1024]{3,2,1,0:T(4,128)(2,1)S(1)} fusion(f32[128,1024]{1,0:T(8,128)S(1)} %get-tuple-element.24, f32[4,4]{1,0:T(4,128)S(1)} %get-tuple-element.41, f32[128,1024]{1,0:T(8,128)S(1)} %get-tuple-element.25, f32[4,4]{1,0:T(4,128)S(1)} %get-tuple-element.42, f32[128,1024]{1,0:T(8,128)S(1)} %get-tuple-element.23, ...), kind=kLoop, calls=%fused_computation.6 | loop fusion | flops 16777216 | bytes 6291712 | tf_op jit(solution)/shard_map/convert_element_type | solution.py:50
  37.3 4.2 %copy.33 = bf16[64,8,4,1024]{3,1,2,0:T(8,128)(2,1)} copy(bf16[64,8,4,1024]{3,2,1,0:T(4,128)(2,1)S(1)} %bitcast.183) | data formatting | bytes 8388608
  41.5 5.1 %all-gather.2.cloned.1.call-done = bf16[512,4096]{1,0:T(8,128)(2,1)} async-done(((bf16[512,512]{1,0:T(8,128)(2,1)}), bf16[512,4096]{1,0:T(8,128)(2,1)}) %all-gather.2.cloned.1.call-update) | async-done | bytes 4194320 | tf_op jit(solution)/shard_map/all_gather | solution.py:60
  46.7 13.8 %fusion.9 = bf16[512,1536]{0,1:T(8,128)(2,1)} fusion(bf16[512,4096]{1,0:T(8,128)(2,1)} %all-gather.2.cloned.1.call-done, bf16[4096,512]{1,0:T(8,128)(2,1)} %bitcast.187, bf16[4096,512]{1,0:T(8,128)(2,1)} %bitcast.188, bf16[4096,512]{1,0:T(8,128)(2,1)} %bitcast.189), kind=kOutput, calls=%fused_computation.15 | convolution fusion | flops 6480986112 | bytes 18350080 | tf_op jit(solution)/shard_map/dot_general | solution.py:64
  60.5 1.5 fusion.65
  61.9 0.1 reshape.328
  62.1 0.4 copy.15
  62.4 0.1 reshape.330
  62.6 0.3 fusion.66
  62.9 1.6 %collective-permute-start = (bf16[4,128,128]{2,1,0:T(8,128)(2,1)S(1)}, bf16[4,128,128]{2,1,0:T(8,128)(2,1)S(1)}, u32[]{:S(2)}, u32[]{:S(2)}) collective-permute-start(bf16[4,128,128]{2,1,0:T(8,128)(2,1)S(1)} %get-tuple-element.43), channel_id=1, source_target_pairs={{0,8},{8,16},{16,24},{24,32},{32,40},{40,48},{48,56},{56,0},{64,72... | collective-permute-start | bytes 393224 | tf_op jit(solution)/shard_map/ppermute | solution.py:25
  64.5 2.5 %collective-permute-start.1 = (bf16[4,128,128]{2,1,0:T(8,128)(2,1)S(1)}, bf16[4,128,128]{2,1,0:T(8,128)(2,1)S(1)}, u32[]{:S(2)}, u32[]{:S(2)}) collective-permute-start(bf16[4,128,128]{2,1,0:T(8,128)(2,1)S(1)} %get-tuple-element.43), channel_id=1, source_target_pairs={{0,16},{8,24},{16,32},{24,40},{32,48},{40,56},{48,0},{56,8},{64,80... | collective-permute-start | bytes 393224 | tf_op jit(solution)/shard_map/ppermute | solution.py:25
  67.1 2.9 %collective-permute-start.2 = (bf16[4,128,128]{2,1,0:T(8,128)(2,1)S(1)}, bf16[4,128,128]{2,1,0:T(8,128)(2,1)}, u32[]{:S(2)}, u32[]{:S(2)}) collective-permute-start(bf16[4,128,128]{2,1,0:T(8,128)(2,1)S(1)} %get-tuple-element.43), channel_id=1, source_target_pairs={{0,24},{8,32},{16,40},{24,48},{32,56},{40,0},{48,8},{56,16},{64,88... | collective-permute-start | bytes 393224 | tf_op jit(solution)/shard_map/ppermute | solution.py:25
  70.0 2.0 %collective-permute-start.3 = (bf16[4,128,128]{2,1,0:T(8,128)(2,1)S(1)}, bf16[4,128,128]{2,1,0:T(8,128)(2,1)}, u32[]{:S(2)}, u32[]{:S(2)}) collective-permute-start(bf16[4,128,128]{2,1,0:T(8,128)(2,1)S(1)} %get-tuple-element.43), channel_id=1, source_target_pairs={{0,32},{8,40},{16,48},{24,56},{32,0},{40,8},{48,16},{56,24},{64,96... | collective-permute-start | bytes 393224 | tf_op jit(solution)/shard_map/ppermute | solution.py:25
  72.0 3.1 %collective-permute-start.4 = (bf16[4,128,128]{2,1,0:T(8,128)(2,1)S(1)}, bf16[4,128,128]{2,1,0:T(8,128)(2,1)}, u32[]{:S(2)}, u32[]{:S(2)}) collective-permute-start(bf16[4,128,128]{2,1,0:T(8,128)(2,1)S(1)} %get-tuple-element.43), channel_id=1, source_target_pairs={{0,40},{8,48},{16,56},{24,0},{32,8},{40,16},{48,24},{56,32},{64,10... | collective-permute-start | bytes 393224 | tf_op jit(solution)/shard_map/ppermute | solution.py:25
  75.1 0.1 reshape.329
  75.3 0.4 copy.17
  75.6 1.6 %fusion.15 = f32[4,4,128,128]{3,2,1,0:T(8,128)} fusion(bf16[4,128,4,128]{3,1,2,0:T(8,128)(2,1)S(1)} %copy.15, bf16[4,128,4,128]{3,1,2,0:T(8,128)(2,1)S(1)} %copy.17, pred[128,128]{1,0:T(8,128)(4,1)S(1)} %iota_compare_fusion, bf16[4,128,4,128]{1,0,3,2:T(4,128)(2,1)S(1)} %reshape.330), kind=kOutput, calls=%fused_computation.21 | convolution fusion | flops 134742016 | bytes 2637824 | tf_op jit(solution)/shard_map/nhst,nthe->nshe/dot_general | solution.py:84
  77.3 0.0 collective-permute-done
  77.3 3.4 %collective-permute-start.5 = (bf16[4,128,128]{2,1,0:T(8,128)(2,1)S(1)}, bf16[4,128,128]{2,1,0:T(8,128)(2,1)S(1)}, u32[]{:S(2)}, u32[]{:S(2)}) collective-permute-start(bf16[4,128,128]{2,1,0:T(8,128)(2,1)S(1)} %get-tuple-element.43), channel_id=1, source_target_pairs={{0,48},{8,56},{16,0},{24,8},{32,16},{40,24},{48,32},{56,40},{64,11... | collective-permute-start | bytes 393224 | tf_op jit(solution)/shard_map/ppermute | solution.py:25
  80.7 0.0 collective-permute-done.1
  80.7 1.4 collective-permute-start.6
  82.1 2.0 %collective-permute-done.2 = bf16[4,128,128]{2,1,0:T(8,128)(2,1)} collective-permute-done((bf16[4,128,128]{2,1,0:T(8,128)(2,1)S(1)}, bf16[4,128,128]{2,1,0:T(8,128)(2,1)}, u32[]{:S(2)}, u32[]{:S(2)}) %collective-permute-start.2) | collective-permute-done | bytes 131104 | tf_op jit(solution)/shard_map/ppermute | solution.py:25
  84.0 4.6 %collective-permute-done.3 = bf16[4,128,128]{2,1,0:T(8,128)(2,1)} collective-permute-done((bf16[4,128,128]{2,1,0:T(8,128)(2,1)S(1)}, bf16[4,128,128]{2,1,0:T(8,128)(2,1)}, u32[]{:S(2)}, u32[]{:S(2)}) %collective-permute-start.3) | collective-permute-done | bytes 131104 | tf_op jit(solution)/shard_map/ppermute | solution.py:25
  88.6 2.8 %collective-permute-done.4 = bf16[4,128,128]{2,1,0:T(8,128)(2,1)} collective-permute-done((bf16[4,128,128]{2,1,0:T(8,128)(2,1)S(1)}, bf16[4,128,128]{2,1,0:T(8,128)(2,1)}, u32[]{:S(2)}, u32[]{:S(2)}) %collective-permute-start.4) | collective-permute-done | bytes 131104 | tf_op jit(solution)/shard_map/ppermute | solution.py:25
  91.4 3.7 %collective-permute-done.5 = bf16[4,128,128]{2,1,0:T(8,128)(2,1)S(1)} collective-permute-done((bf16[4,128,128]{2,1,0:T(8,128)(2,1)S(1)}, bf16[4,128,128]{2,1,0:T(8,128)(2,1)S(1)}, u32[]{:S(2)}, u32[]{:S(2)}) %collective-permute-start.5) | collective-permute-done | bytes 131104 | tf_op jit(solution)/shard_map/ppermute | solution.py:25
  95.1 1.1 collective-permute-done.6
  96.2 1.1 add_add_fusion
  97.3 1.6 collective-permute-start.7
  98.8 1.1 collective-permute-start.8
  100.0 2.1 %collective-permute-start.9 = (bf16[4,128,128]{2,1,0:T(8,128)(2,1)S(1)}, bf16[4,128,128]{2,1,0:T(8,128)(2,1)S(1)}, u32[]{:S(2)}, u32[]{:S(2)}) collective-permute-start(bf16[4,128,128]{2,1,0:T(8,128)(2,1)S(1)} %add_add_fusion), channel_id=1, source_target_pairs={{0,192},{8,200},{16,208},{24,216},{32,224},{40,232},{48,240},{56,2... | collective-permute-start | bytes 393224 | tf_op jit(solution)/shard_map/ppermute | solution.py:25
  102.2 0.9 bitcast_dynamic-update-slice_fusion.4
  103.1 0.9 bitcast_dynamic-update-slice_fusion.3
  104.0 0.9 bitcast_dynamic-update-slice_fusion.2
  105.0 0.0 copy-start
  105.0 0.7 fusion.16
  105.8 0.0 collective-permute-done.7
  105.8 0.2 collective-permute-done.8
  106.0 0.6 collective-permute-done.9
  106.6 0.1 pad_maximum_fusion.1
  106.7 0.5 fusion.22
  107.2 0.1 fusion.36
  107.2 0.0 copy-start.2
  107.3 0.1 fusion.33
  107.3 0.5 fusion.30
  107.8 0.0 copy-done
  107.8 0.5 multiply_reduce_fusion
  108.4 0.2 multiply_convert_fusion
  108.6 0.3 copy.20
  108.9 6.5 %convolution_convert_fusion = bf16[512,4096]{1,0:T(8,128)(2,1)} fusion(bf16[512,4096]{1,0:T(8,128)(2,1)} %bitcast.186, bf16[64,8,4,128]{3,2,1,0:T(4,128)(2,1)S(1)} %bitcast.191), kind=kOutput, calls=%fused_computation.10 | convolution fusion | flops 2149580800 | bytes 8912896 | tf_op jit(solution)/shard_map/dot_general | solution.py:101
  115.4 0.0 reduce-scatter.2.cloned.1.call-update
  115.5 38.5 %reduce-scatter.2.cloned.1.call-done = bf16[512,512]{1,0:T(8,128)(2,1)} async-done(((bf16[512,4096]{1,0:T(8,128)(2,1)}), bf16[512,512]{1,0:T(8,128)(2,1)}) %reduce-scatter.2.cloned.1.call-update) | async-done | bytes 524304 | tf_op jit(solution)/shard_map/reduce_scatter | solution.py:102
  (8 shorter events, 0.1 us)
Async XLA Ops:
  6.5 40.1 %all-gather.2.cloned.1.call-start = ((), (), s32[]{:S(2)}) async-start(), calls=%async_computation.1 | async-start | bytes 4718592 | tf_op jit(solution)/shard_map/all_gather | solution.py:60
  7.3 146.7 %reduce-scatter.2.cloned.1.call-start = ((), (), s32[]{:S(2)}) async-start(), calls=%async_computation.2 | async-start | bytes 4718592 | tf_op jit(solution)/shard_map/reduce_scatter | solution.py:102
  29.5 2.7 %copy-start.1 = (bf16[4,128,1024]{2,1,0:T(8,128)(2,1)S(1)}, bf16[4,128,1024]{2,1,0:T(8,128)(2,1)}, u32[]{:S(2)}) copy-start(bf16[4,128,1024]{2,1,0:T(8,128)(2,1)} %param.7) | copy-start | bytes 3145732
  62.9 14.4 %collective-permute-start = (bf16[4,128,128]{2,1,0:T(8,128)(2,1)S(1)}, bf16[4,128,128]{2,1,0:T(8,128)(2,1)S(1)}, u32[]{:S(2)}, u32[]{:S(2)}) collective-permute-start(bf16[4,128,128]{2,1,0:T(8,128)(2,1)S(1)} %get-tuple-element.43), channel_id=1, source_target_pairs={{0,8},{8,16},{16,24},{24,32},{32,40},{40,48},{48,56},{56,0},{64,72... | collective-permute-start | bytes 393224 | tf_op jit(solution)/shard_map/ppermute | solution.py:25
  64.5 16.2 %collective-permute-start.1 = (bf16[4,128,128]{2,1,0:T(8,128)(2,1)S(1)}, bf16[4,128,128]{2,1,0:T(8,128)(2,1)S(1)}, u32[]{:S(2)}, u32[]{:S(2)}) collective-permute-start(bf16[4,128,128]{2,1,0:T(8,128)(2,1)S(1)} %get-tuple-element.43), channel_id=1, source_target_pairs={{0,16},{8,24},{16,32},{24,40},{32,48},{40,56},{48,0},{56,8},{64,80... | collective-permute-start | bytes 393224 | tf_op jit(solution)/shard_map/ppermute | solution.py:25
  67.1 17.0 %collective-permute-start.2 = (bf16[4,128,128]{2,1,0:T(8,128)(2,1)S(1)}, bf16[4,128,128]{2,1,0:T(8,128)(2,1)}, u32[]{:S(2)}, u32[]{:S(2)}) collective-permute-start(bf16[4,128,128]{2,1,0:T(8,128)(2,1)S(1)} %get-tuple-element.43), channel_id=1, source_target_pairs={{0,24},{8,32},{16,40},{24,48},{32,56},{40,0},{48,8},{56,16},{64,88... | collective-permute-start | bytes 393224 | tf_op jit(solution)/shard_map/ppermute | solution.py:25
  70.0 18.6 %collective-permute-start.3 = (bf16[4,128,128]{2,1,0:T(8,128)(2,1)S(1)}, bf16[4,128,128]{2,1,0:T(8,128)(2,1)}, u32[]{:S(2)}, u32[]{:S(2)}) collective-permute-start(bf16[4,128,128]{2,1,0:T(8,128)(2,1)S(1)} %get-tuple-element.43), channel_id=1, source_target_pairs={{0,32},{8,40},{16,48},{24,56},{32,0},{40,8},{48,16},{56,24},{64,96... | collective-permute-start | bytes 393224 | tf_op jit(solution)/shard_map/ppermute | solution.py:25
  72.0 19.4 %collective-permute-start.4 = (bf16[4,128,128]{2,1,0:T(8,128)(2,1)S(1)}, bf16[4,128,128]{2,1,0:T(8,128)(2,1)}, u32[]{:S(2)}, u32[]{:S(2)}) collective-permute-start(bf16[4,128,128]{2,1,0:T(8,128)(2,1)S(1)} %get-tuple-element.43), channel_id=1, source_target_pairs={{0,40},{8,48},{16,56},{24,0},{32,8},{40,16},{48,24},{56,32},{64,10... | collective-permute-start | bytes 393224 | tf_op jit(solution)/shard_map/ppermute | solution.py:25
  77.3 17.8 %collective-permute-start.5 = (bf16[4,128,128]{2,1,0:T(8,128)(2,1)S(1)}, bf16[4,128,128]{2,1,0:T(8,128)(2,1)S(1)}, u32[]{:S(2)}, u32[]{:S(2)}) collective-permute-start(bf16[4,128,128]{2,1,0:T(8,128)(2,1)S(1)} %get-tuple-element.43), channel_id=1, source_target_pairs={{0,48},{8,56},{16,0},{24,8},{32,16},{40,24},{48,32},{56,40},{64,11... | collective-permute-start | bytes 393224 | tf_op jit(solution)/shard_map/ppermute | solution.py:25
  80.7 15.5 %collective-permute-start.6 = (bf16[4,128,128]{2,1,0:T(8,128)(2,1)S(1)}, bf16[4,128,128]{2,1,0:T(8,128)(2,1)S(1)}, u32[]{:S(2)}, u32[]{:S(2)}) collective-permute-start(bf16[4,128,128]{2,1,0:T(8,128)(2,1)S(1)} %get-tuple-element.43), channel_id=1, source_target_pairs={{0,56},{8,0},{16,8},{24,16},{32,24},{40,32},{48,40},{56,48},{64,12... | collective-permute-start | bytes 393224 | tf_op jit(solution)/shard_map/ppermute | solution.py:25
  97.3 8.5 %collective-permute-start.7 = (bf16[4,128,128]{2,1,0:T(8,128)(2,1)S(1)}, bf16[4,128,128]{2,1,0:T(8,128)(2,1)S(1)}, u32[]{:S(2)}, u32[]{:S(2)}) collective-permute-start(bf16[4,128,128]{2,1,0:T(8,128)(2,1)S(1)} %add_add_fusion), channel_id=1, source_target_pairs={{0,64},{8,72},{16,80},{24,88},{32,96},{40,104},{48,112},{56,120},{... | collective-permute-start | bytes 393224 | tf_op jit(solution)/shard_map/ppermute | solution.py:25
  98.8 7.1 %collective-permute-start.8 = (bf16[4,128,128]{2,1,0:T(8,128)(2,1)S(1)}, bf16[4,128,128]{2,1,0:T(8,128)(2,1)S(1)}, u32[]{:S(2)}, u32[]{:S(2)}) collective-permute-start(bf16[4,128,128]{2,1,0:T(8,128)(2,1)S(1)} %add_add_fusion), channel_id=1, source_target_pairs={{0,128},{8,136},{16,144},{24,152},{32,160},{40,168},{48,176},{56,1... | collective-permute-start | bytes 393224 | tf_op jit(solution)/shard_map/ppermute | solution.py:25
  100.0 6.6 %collective-permute-start.9 = (bf16[4,128,128]{2,1,0:T(8,128)(2,1)S(1)}, bf16[4,128,128]{2,1,0:T(8,128)(2,1)S(1)}, u32[]{:S(2)}, u32[]{:S(2)}) collective-permute-start(bf16[4,128,128]{2,1,0:T(8,128)(2,1)S(1)} %add_add_fusion), channel_id=1, source_target_pairs={{0,192},{8,200},{16,208},{24,216},{32,224},{40,232},{48,240},{56,2... | collective-permute-start | bytes 393224 | tf_op jit(solution)/shard_map/ppermute | solution.py:25
  105.0 2.8 %copy-start = (f32[4,4,128,128]{3,2,1,0:T(8,128)S(1)}, f32[4,4,128,128]{3,2,1,0:T(8,128)}, u32[]{:S(2)}) copy-start(f32[4,4,128,128]{3,2,1,0:T(8,128)} %fusion.15) | copy-start | bytes 3145732
  107.2 1.2 copy-start.2
Sparse Core Ops, SparseCore 0:
  9.2 37.4 all-gather.1
  115.6 38.3 reduce-scatter.1

commit v2 on v1

--- a/solution.py
+++ b/solution.py
@@ -52,30 +52,28 @@
 
 def on_device(ctx_devices, ctx_row, tokens, qkv_blocks, out_blocks, mix_factors, head_gain):
     col_width = qkv_blocks.shape[-1]
-    w_qkv = jnp.concatenate(
-        [fold_weights(qkv_blocks[p], mix_factors[p]) for p in range(3)], axis=1
+    w_kv = jnp.concatenate(
+        [fold_weights(qkv_blocks[p], mix_factors[p]) for p in (1, 2)], axis=1
     )
+    w_q = fold_weights(qkv_blocks[0], mix_factors[0])
     w_out = fold_weights(out_blocks, mix_factors[3])
 
     whole = lax.all_gather(tokens, "tp", axis=1, tiled=True)
     tok_rows = whole.shape[0]
     local_heads = PHM * col_width // HEAD
     nblk = tok_rows // SPAN
-    qkv = jnp.dot(whole, w_qkv, preferred_element_type=jnp.float32).astype(jnp.bfloat16)
-
-    def project(p):
-        part = qkv[:, p * PHM * col_width:(p + 1) * PHM * col_width]
-        return part.reshape(nblk, SPAN, local_heads, HEAD)
-
-    key_heads = project(1)
-    value_heads = project(2)
+    width = PHM * col_width
+    kv = jnp.dot(whole, w_kv, preferred_element_type=jnp.float32).astype(jnp.bfloat16)
+    key_heads = kv[:, :width].reshape(nblk, SPAN, local_heads, HEAD)
+    value_heads = kv[:, width:].reshape(nblk, SPAN, local_heads, HEAD)
     states = jnp.einsum(
         "nshd,nshe->nhde", key_heads, value_heads, preferred_element_type=jnp.float32
     )
     totals = jnp.sum(states, axis=0)
     earlier_sum = exclusive_prefix(totals, "ctx", ctx_devices, ctx_row)
 
-    query_heads = project(0)
+    query = jnp.dot(whole, w_q, preferred_element_type=jnp.float32).astype(jnp.bfloat16)
+    query_heads = query.reshape(nblk, SPAN, local_heads, HEAD)
     scores = jnp.einsum(
         "nshd,nthd->nhst", query_heads, key_heads, preferred_element_type=jnp.float32
     )
@@ -98,13 +96,17 @@
     mean_sq = jnp.mean(combined * combined, axis=-1, keepdims=True)
     normed = combined * lax.rsqrt(mean_sq + epsilon) * head_gain
     attn = normed.astype(jnp.bfloat16).reshape(tok_rows, PHM * col_width)
-    partial_value = jnp.dot(attn, w_out, preferred_element_type=jnp.float32)
-    reduced = lax.psum_scatter(
-        partial_value.astype(jnp.bfloat16),
-        "tp",
-        scatter_dimension=1,
-        tiled=True,
-    )
+    halves = []
+    half = tok_rows // 2
+    for part in range(2):
+        rows = attn[part * half:(part + 1) * half]
+        partial_value = jnp.dot(rows, w_out, preferred_element_type=jnp.float32)
+        halves.append(
+            lax.psum_scatter(
+                partial_value.astype(jnp.bfloat16), "tp", scatter_dimension=1, tiled=True
+            )
+        )
+    reduced = jnp.concatenate(halves, axis=0)
     return reduced
 
 

time: 161 us -> 189 us (1.17)
  waiting for transfers between devices: 59.3 us -> 83.9 us
  matrix products: 24.6 us -> 28.9 us
  local copies, waits for them, and re-layouts: 18.9 us -> 14.9 us
  other arithmetic: 22.5 us -> 25.3 us
    reduce_scatter x1 -> x2, waiting for transfers between devices: 38.5 us -> 66.5 us  [on_device(): lax.psum_scatter(partial_value.astype(jnp.bfloat16), 'tp', scatter_dimens...]
    ppermute x10, waiting for transfers between devices: 15 us -> 9.78 us  [ring_gather(): slots.append(lax.ppermute(value, axis, pairs))]
    dot_general x2 -> x4, matrix products: 20.3 us -> 24.6 us  [the longest x2 9.62 us: on_device(): partial_value = jnp.dot(rows, w_out, preferred_element_type=jnp.float32)]
    unnamed x17 -> x16, local copies, waits for them, and re-layouts: 15.1 us -> 12.4 us
  transfers between devices with their start and end apart: 12 -> 13, of which waited for: 9 -> 9; matrix products, arithmetic and copies ran while one was open for 25% -> 26% of each run, Pallas kernels for 0% -> 0%
where the time goes in v2:
time: 189 us; the launch traced here: 188 us
  waiting for transfers between devices  83.9 us (44%)
  matrix products  28.9 us (15%)
  other arithmetic  25.3 us (13%)
  starting transfers between devices  21.9 us (12%)
  local copies, waits for them, and re-layouts  14.9 us (8%)
  between operations  13.4 us (7%)
    reduce_scatter x2, waiting for transfers between devices, on_device(): lax.psum_scatter(partial_value.astype(jnp.bfloat16), 'tp', scatter_dimens...  66.5 us
    ppermute x10, starting transfers between devices, ring_gather(): slots.append(lax.ppermute(value, axis, pairs))  21.8 us
    another operation x2, other arithmetic  14.7 us
    unnamed x16, local copies, waits for them, and re-layouts  12.4 us
    ppermute x10, waiting for transfers between devices, ring_gather(): slots.append(lax.ppermute(value, axis, pairs))  9.78 us
    dot_general x2, matrix products, on_device(): partial_value = jnp.dot(rows, w_out, preferred_element_type=jnp.float32)  9.62 us
    dot_general x1, matrix products, on_device(): jnp.dot(whole, w_kv, preferred_element_type=jnp.float32)  9.19 us
    all_gather x1, waiting for transfers between devices, on_device(): whole = lax.all_gather(tokens, 'tp', axis=1, tiled=True)  6.89 us
  transfers between devices with their start and end apart: 13, of which 9 were waited for; matrix products, arithmetic and copies ran while one was open for 26% of the time, Pallas kernels for 0%

profile of v2, /device:TPU:8, one launch (start us, length us, event | category | flops | bytes accessed | tf_op | source)
XLA Modules:
  0.0 188.3 jit_solution(2630909805078558264)
XLA Ops:
  6.5 0.7 all-gather.2.cloned.1.call-update
  7.3 0.0 reduce-scatter.3.cloned.1.call-start
  7.3 0.9 slice_bitcast_fusion.10
  8.2 2.4 %bitcast_convert_fusion.7 = (f32[1024,128]{1,0:T(8,128)S(1)}, f32[1024,128]{1,0:T(8,128)S(1)}, f32[1024,128]{1,0:T(8,128)S(1)}, f32[1024,128]{1,0:T(8,128)S(1)},...) fusion(bf16[3,4,1024,128]{3,2,1,0:T(8,128)(2,1)} %param.6), kind=kLoop, calls=%fused_computation.60 | loop fusion | flops 1572864 | bytes 9437184 | tf_op jit(solution)/shard_map/convert_element_type | solution.py:47
  10.6 9.1 %add_convert_fusion.2 = (bf16[4,1024,4,128]{3,2,1,0:T(4,128)(2,1)S(1)}, bf16[4,1024,4,128]{3,2,1,0:T(4,128)(2,1)S(1)}) fusion(f32[1024,128]{1,0:T(8,128)S(1)} %get-tuple-element.9, f32[4,4]{1,0:T(4,128)S(1)} %get-tuple-element.34, f32[1024,128]{1,0:T(8,128)S(1)} %get-tuple-element.10, f32[4,4]{1,0:T(4,128)S(1)} %get-tuple-element.35, ...), kind=kLoop, calls=%fused_computation.6 | loop fusion | flops 33554432 | bytes 12583424 | tf_op jit(solution)/shard_map/convert.18
  19.7 2.6 %copy.65 = bf16[512,8,4,128]{3,1,2,0:T(8,128)(2,1)} copy(bf16[512,8,4,128]{3,2,1,0:T(4,128)(2,1)S(1)} %bitcast.194) | data formatting | bytes 8388608
  22.3 2.7 %copy.66 = bf16[512,8,4,128]{3,1,2,0:T(8,128)(2,1)} copy(bf16[512,8,4,128]{3,2,1,0:T(4,128)(2,1)S(1)} %bitcast.193) | data formatting | bytes 8388608
  25.0 0.2 bitcast_convert_fusion.3
  25.2 4.6 %add_convert_fusion = bf16[4,128,4,1024]{3,2,1,0:T(4,128)(2,1)S(1)} fusion(f32[128,1024]{1,0:T(8,128)S(1)} %get-tuple-element.23, f32[4,4]{1,0:T(4,128)S(1)} %get-tuple-element.42, f32[128,1024]{1,0:T(8,128)S(1)} %get-tuple-element.24, f32[4,4]{1,0:T(4,128)S(1)} %get-tuple-element.43, f32[128,1024]{1,0:T(8,128)S(1)} %get-tuple-element.22, ...), kind=kLoop, calls=%fused_computation.4 | loop fusion | flops 16777216 | bytes 6291712 | tf_op jit(solution)/shard_map/convert_element_type | solution.py:50
  29.9 4.2 %copy.34 = bf16[64,8,4,1024]{3,1,2,0:T(8,128)(2,1)} copy(bf16[64,8,4,1024]{3,2,1,0:T(4,128)(2,1)S(1)} %bitcast.195) | data formatting | bytes 8388608
  34.1 5.6 %add_convert_fusion.1 = bf16[4,1024,4,128]{3,2,1,0:T(4,128)(2,1)} fusion(f32[1024,128]{1,0:T(8,128)S(1)} %get-tuple-element.17, f32[4,4]{1,0:T(4,128)S(1)} %get-tuple-element.31, f32[1024,128]{1,0:T(8,128)S(1)} %get-tuple-element.18, f32[4,4]{1,0:T(4,128)S(1)} %get-tuple-element.32, f32[1024,128]{1,0:T(8,128)S(1)} %get-tuple-element.8, ...), kind=kLoop, calls=%fused_computation.5 | loop fusion | flops 16777216 | bytes 6291712 | tf_op jit(solution)/shard_map/convert.17
  39.8 6.9 %all-gather.2.cloned.1.call-done = bf16[512,4096]{1,0:T(8,128)(2,1)} async-done(((bf16[512,512]{1,0:T(8,128)(2,1)}), bf16[512,4096]{1,0:T(8,128)(2,1)}) %all-gather.2.cloned.1.call-update) | async-done | bytes 4194320 | tf_op jit(solution)/shard_map/all_gather | solution.py:61
  46.7 9.2 %fusion.10 = bf16[512,1024]{0,1:T(8,128)(2,1)S(1)} fusion(bf16[512,4096]{1,0:T(8,128)(2,1)} %all-gather.2.cloned.1.call-done, bf16[4096,512]{1,0:T(8,128)(2,1)} %bitcast.201, bf16[4096,512]{1,0:T(8,128)(2,1)} %bitcast.202), kind=kOutput, calls=%fused_computation.16 | convolution fusion | flops 4312268800 | bytes 13631488 | tf_op jit(solution)/shard_map/dot_general | solution.py:66
  55.9 0.1 fusion.74
  55.9 0.1 reshape.332
  56.1 0.4 copy.15
  56.4 0.1 reshape.334
  56.6 0.3 fusion.76
  56.9 1.6 collective-permute-start
  58.5 2.5 %collective-permute-start.1 = (bf16[4,128,128]{2,1,0:T(8,128)(2,1)S(1)}, bf16[4,128,128]{2,1,0:T(8,128)(2,1)S(1)}, u32[]{:S(2)}, u32[]{:S(2)}) collective-permute-start(bf16[4,128,128]{2,1,0:T(8,128)(2,1)S(1)} %get-tuple-element.44), channel_id=1, source_target_pairs={{0,16},{8,24},{16,32},{24,40},{32,48},{40,56},{48,0},{56,8},{64,80... | collective-permute-start | bytes 393224 | tf_op jit(solution)/shard_map/ppermute | solution.py:25
  61.1 2.9 %collective-permute-start.2 = (bf16[4,128,128]{2,1,0:T(8,128)(2,1)S(1)}, bf16[4,128,128]{2,1,0:T(8,128)(2,1)}, u32[]{:S(2)}, u32[]{:S(2)}) collective-permute-start(bf16[4,128,128]{2,1,0:T(8,128)(2,1)S(1)} %get-tuple-element.44), channel_id=1, source_target_pairs={{0,24},{8,32},{16,40},{24,48},{32,56},{40,0},{48,8},{56,16},{64,88... | collective-permute-start | bytes 393224 | tf_op jit(solution)/shard_map/ppermute | solution.py:25
  64.0 2.0 %collective-permute-start.3 = (bf16[4,128,128]{2,1,0:T(8,128)(2,1)S(1)}, bf16[4,128,128]{2,1,0:T(8,128)(2,1)}, u32[]{:S(2)}, u32[]{:S(2)}) collective-permute-start(bf16[4,128,128]{2,1,0:T(8,128)(2,1)S(1)} %get-tuple-element.44), channel_id=1, source_target_pairs={{0,32},{8,40},{16,48},{24,56},{32,0},{40,8},{48,16},{56,24},{64,96... | collective-permute-start | bytes 393224 | tf_op jit(solution)/shard_map/ppermute | solution.py:25
  66.0 3.1 %collective-permute-start.4 = (bf16[4,128,128]{2,1,0:T(8,128)(2,1)S(1)}, bf16[4,128,128]{2,1,0:T(8,128)(2,1)}, u32[]{:S(2)}, u32[]{:S(2)}) collective-permute-start(bf16[4,128,128]{2,1,0:T(8,128)(2,1)S(1)} %get-tuple-element.44), channel_id=1, source_target_pairs={{0,40},{8,48},{16,56},{24,0},{32,8},{40,16},{48,24},{56,32},{64,10... | collective-permute-start | bytes 393224 | tf_op jit(solution)/shard_map/ppermute | solution.py:25
  69.1 5.8 %fusion.20 = bf16[512,512]{0,1:T(8,128)(2,1)S(1)} fusion(bf16[512,4096]{1,0:T(8,128)(2,1)} %all-gather.2.cloned.1.call-done, bf16[512,8,4,128]{3,2,1,0:T(4,128)(2,1)} %bitcast.198), kind=kOutput, calls=%fused_computation.24 | convolution fusion | flops 2147745792 | bytes 8912896 | tf_op jit(solution)/shard_map/dot_general | solution.py:75
  75.0 0.1 reshape.333
  75.1 0.4 copy.17
  75.5 1.6 fusion.19
  77.1 3.4 %collective-permute-start.5 = (bf16[4,128,128]{2,1,0:T(8,128)(2,1)S(1)}, bf16[4,128,128]{2,1,0:T(8,128)(2,1)S(1)}, u32[]{:S(2)}, u32[]{:S(2)}) collective-permute-start(bf16[4,128,128]{2,1,0:T(8,128)(2,1)S(1)} %get-tuple-element.44), channel_id=1, source_target_pairs={{0,48},{8,56},{16,0},{24,8},{32,16},{40,24},{48,32},{56,40},{64,11... | collective-permute-start | bytes 393224 | tf_op jit(solution)/shard_map/ppermute | solution.py:25
  80.5 0.0 collective-permute-done.1
  80.5 1.4 collective-permute-start.6
  81.9 0.0 collective-permute-done.2
  81.9 0.6 collective-permute-done.3
  82.6 2.7 %collective-permute-done.4 = bf16[4,128,128]{2,1,0:T(8,128)(2,1)} collective-permute-done((bf16[4,128,128]{2,1,0:T(8,128)(2,1)S(1)}, bf16[4,128,128]{2,1,0:T(8,128)(2,1)}, u32[]{:S(2)}, u32[]{:S(2)}) %collective-permute-start.4) | collective-permute-done | bytes 131104 | tf_op jit(solution)/shard_map/ppermute | solution.py:25
  85.3 3.7 %collective-permute-done.5 = bf16[4,128,128]{2,1,0:T(8,128)(2,1)S(1)} collective-permute-done((bf16[4,128,128]{2,1,0:T(8,128)(2,1)S(1)}, bf16[4,128,128]{2,1,0:T(8,128)(2,1)S(1)}, u32[]{:S(2)}, u32[]{:S(2)}) %collective-permute-start.5) | collective-permute-done | bytes 131104 | tf_op jit(solution)/shard_map/ppermute | solution.py:25
  89.0 1.8 collective-permute-done.6
  90.8 1.1 add_add_fusion
  91.9 1.6 collective-permute-start.7
  93.4 1.1 collective-permute-start.8
  94.6 2.1 %collective-permute-start.9 = (bf16[4,128,128]{2,1,0:T(8,128)(2,1)S(1)}, bf16[4,128,128]{2,1,0:T(8,128)(2,1)S(1)}, u32[]{:S(2)}, u32[]{:S(2)}) collective-permute-start(bf16[4,128,128]{2,1,0:T(8,128)(2,1)S(1)} %add_add_fusion), channel_id=1, source_target_pairs={{0,192},{8,200},{16,208},{24,216},{32,224},{40,232},{48,240},{56,2... | collective-permute-start | bytes 393224 | tf_op jit(solution)/shard_map/ppermute | solution.py:25
  96.8 0.9 bitcast_dynamic-update-slice_fusion.4
  97.7 0.9 bitcast_dynamic-update-slice_fusion.3
  98.6 0.9 bitcast_dynamic-update-slice_fusion.2
  99.6 0.7 fusion.23
  100.3 0.0 collective-permute-done.7
  100.4 0.3 collective-permute-done.8
  100.7 0.6 collective-permute-done.9
  101.3 0.1 pad_maximum_fusion.1
  101.3 0.5 fusion.27
  101.8 0.1 fusion.45
  101.9 0.0 copy-start.2
  101.9 0.1 fusion.42
  102.0 0.5 fusion.35
  102.5 0.5 multiply_reduce_fusion
  103.1 0.2 multiply_convert_fusion
  103.3 0.2 copy.20
  103.5 4.8 %convolution_convert_fusion.1 = bf16[256,4096]{1,0:T(8,128)(2,1)} fusion(bf16[512,4096]{1,0:T(8,128)(2,1)} %bitcast.199, bf16[32,8,4,128]{3,2,1,0:T(4,128)(2,1)S(1)} %bitcast.207), kind=kOutput, calls=%fused_computation.9 | convolution fusion | flops 1074790400 | bytes 6553600 | tf_op jit(solution)/shard_map/dot_general | solution.py:103
  108.3 0.0 reduce-scatter.3.cloned.1.call-update
  108.4 0.0 reduce-scatter.5.cloned.1.call-start
  108.4 0.2 copy.21
  108.6 4.8 %convolution_convert_fusion = bf16[256,4096]{1,0:T(8,128)(2,1)} fusion(bf16[512,4096]{1,0:T(8,128)(2,1)} %bitcast.200, bf16[32,8,4,128]{3,2,1,0:T(4,128)(2,1)S(1)} %bitcast.206), kind=kOutput, calls=%fused_computation.8 | convolution fusion | flops 1074790400 | bytes 6553600 | tf_op jit(solution)/shard_map/dot_general | solution.py:103
  113.4 0.0 reduce-scatter.5.cloned.1.call-update
  113.5 28.7 %reduce-scatter.3.cloned.1.call-done = bf16[256,512]{1,0:T(8,128)(2,1)} async-done(((bf16[256,4096]{1,0:T(8,128)(2,1)}), bf16[256,512]{1,0:T(8,128)(2,1)}) %reduce-scatter.3.cloned.1.call-update) | async-done | bytes 262160 | tf_op jit(solution)/shard_map/reduce_scatter | solution.py:105
  142.1 37.8 %reduce-scatter.5.cloned.1.call-done = bf16[256,512]{1,0:T(8,128)(2,1)} async-done(((bf16[256,4096]{1,0:T(8,128)(2,1)}), bf16[256,512]{1,0:T(8,128)(2,1)}) %reduce-scatter.5.cloned.1.call-update) | async-done | bytes 262160 | tf_op jit(solution)/shard_map/reduce_scatter | solution.py:105
  179.9 1.9 pad_maximum_fusion.2
  (15 shorter events, 0.2 us)
Async XLA Ops:
  6.5 40.1 %all-gather.2.cloned.1.call-start = ((), (), s32[]{:S(2)}) async-start(), calls=%async_computation.2 | async-start | bytes 4718592 | tf_op jit(solution)/shard_map/all_gather | solution.py:61
  7.3 134.9 %reduce-scatter.3.cloned.1.call-start = ((), (), s32[]{:S(2)}) async-start(), calls=%async_computation.3 | async-start | bytes 2359296 | tf_op jit(solution)/shard_map/reduce_scatter | solution.py:105
  22.3 2.7 %copy-start.1 = (bf16[4,128,1024]{2,1,0:T(8,128)(2,1)S(1)}, bf16[4,128,1024]{2,1,0:T(8,128)(2,1)}, u32[]{:S(2)}) copy-start(bf16[4,128,1024]{2,1,0:T(8,128)(2,1)} %param.7) | copy-start | bytes 3145732
  56.9 20.3 %collective-permute-start = (bf16[4,128,128]{2,1,0:T(8,128)(2,1)S(1)}, bf16[4,128,128]{2,1,0:T(8,128)(2,1)S(1)}, u32[]{:S(2)}, u32[]{:S(2)}) collective-permute-start(bf16[4,128,128]{2,1,0:T(8,128)(2,1)S(1)} %get-tuple-element.44), channel_id=1, source_target_pairs={{0,8},{8,16},{16,24},{24,32},{32,40},{40,48},{48,56},{56,0},{64,72... | collective-permute-start | bytes 393224 | tf_op jit(solution)/shard_map/ppermute | solution.py:25
  58.5 22.0 %collective-permute-start.1 = (bf16[4,128,128]{2,1,0:T(8,128)(2,1)S(1)}, bf16[4,128,128]{2,1,0:T(8,128)(2,1)S(1)}, u32[]{:S(2)}, u32[]{:S(2)}) collective-permute-start(bf16[4,128,128]{2,1,0:T(8,128)(2,1)S(1)} %get-tuple-element.44), channel_id=1, source_target_pairs={{0,16},{8,24},{16,32},{24,40},{32,48},{40,56},{48,0},{56,8},{64,80... | collective-permute-start | bytes 393224 | tf_op jit(solution)/shard_map/ppermute | solution.py:25
  61.1 20.9 %collective-permute-start.2 = (bf16[4,128,128]{2,1,0:T(8,128)(2,1)S(1)}, bf16[4,128,128]{2,1,0:T(8,128)(2,1)}, u32[]{:S(2)}, u32[]{:S(2)}) collective-permute-start(bf16[4,128,128]{2,1,0:T(8,128)(2,1)S(1)} %get-tuple-element.44), channel_id=1, source_target_pairs={{0,24},{8,32},{16,40},{24,48},{32,56},{40,0},{48,8},{56,16},{64,88... | collective-permute-start | bytes 393224 | tf_op jit(solution)/shard_map/ppermute | solution.py:25
  64.0 18.6 %collective-permute-start.3 = (bf16[4,128,128]{2,1,0:T(8,128)(2,1)S(1)}, bf16[4,128,128]{2,1,0:T(8,128)(2,1)}, u32[]{:S(2)}, u32[]{:S(2)}) collective-permute-start(bf16[4,128,128]{2,1,0:T(8,128)(2,1)S(1)} %get-tuple-element.44), channel_id=1, source_target_pairs={{0,32},{8,40},{16,48},{24,56},{32,0},{40,8},{48,16},{56,24},{64,96... | collective-permute-start | bytes 393224 | tf_op jit(solution)/shard_map/ppermute | solution.py:25
  66.0 19.3 %collective-permute-start.4 = (bf16[4,128,128]{2,1,0:T(8,128)(2,1)S(1)}, bf16[4,128,128]{2,1,0:T(8,128)(2,1)}, u32[]{:S(2)}, u32[]{:S(2)}) collective-permute-start(bf16[4,128,128]{2,1,0:T(8,128)(2,1)S(1)} %get-tuple-element.44), channel_id=1, source_target_pairs={{0,40},{8,48},{16,56},{24,0},{32,8},{40,16},{48,24},{56,32},{64,10... | collective-permute-start | bytes 393224 | tf_op jit(solution)/shard_map/ppermute | solution.py:25
  77.1 11.9 %collective-permute-start.5 = (bf16[4,128,128]{2,1,0:T(8,128)(2,1)S(1)}, bf16[4,128,128]{2,1,0:T(8,128)(2,1)S(1)}, u32[]{:S(2)}, u32[]{:S(2)}) collective-permute-start(bf16[4,128,128]{2,1,0:T(8,128)(2,1)S(1)} %get-tuple-element.44), channel_id=1, source_target_pairs={{0,48},{8,56},{16,0},{24,8},{32,16},{40,24},{48,32},{56,40},{64,11... | collective-permute-start | bytes 393224 | tf_op jit(solution)/shard_map/ppermute | solution.py:25
  80.5 10.3 %collective-permute-start.6 = (bf16[4,128,128]{2,1,0:T(8,128)(2,1)S(1)}, bf16[4,128,128]{2,1,0:T(8,128)(2,1)S(1)}, u32[]{:S(2)}, u32[]{:S(2)}) collective-permute-start(bf16[4,128,128]{2,1,0:T(8,128)(2,1)S(1)} %get-tuple-element.44), channel_id=1, source_target_pairs={{0,56},{8,0},{16,8},{24,16},{32,24},{40,32},{48,40},{56,48},{64,12... | collective-permute-start | bytes 393224 | tf_op jit(solution)/shard_map/ppermute | solution.py:25
  91.9 8.5 %collective-permute-start.7 = (bf16[4,128,128]{2,1,0:T(8,128)(2,1)S(1)}, bf16[4,128,128]{2,1,0:T(8,128)(2,1)S(1)}, u32[]{:S(2)}, u32[]{:S(2)}) collective-permute-start(bf16[4,128,128]{2,1,0:T(8,128)(2,1)S(1)} %add_add_fusion), channel_id=1, source_target_pairs={{0,64},{8,72},{16,80},{24,88},{32,96},{40,104},{48,112},{56,120},{... | collective-permute-start | bytes 393224 | tf_op jit(solution)/shard_map/ppermute | solution.py:25
  93.4 7.2 %collective-permute-start.8 = (bf16[4,128,128]{2,1,0:T(8,128)(2,1)S(1)}, bf16[4,128,128]{2,1,0:T(8,128)(2,1)S(1)}, u32[]{:S(2)}, u32[]{:S(2)}) collective-permute-start(bf16[4,128,128]{2,1,0:T(8,128)(2,1)S(1)} %add_add_fusion), channel_id=1, source_target_pairs={{0,128},{8,136},{16,144},{24,152},{32,160},{40,168},{48,176},{56,1... | collective-permute-start | bytes 393224 | tf_op jit(solution)/shard_map/ppermute | solution.py:25
  94.6 6.7 %collective-permute-start.9 = (bf16[4,128,128]{2,1,0:T(8,128)(2,1)S(1)}, bf16[4,128,128]{2,1,0:T(8,128)(2,1)S(1)}, u32[]{:S(2)}, u32[]{:S(2)}) collective-permute-start(bf16[4,128,128]{2,1,0:T(8,128)(2,1)S(1)} %add_add_fusion), channel_id=1, source_target_pairs={{0,192},{8,200},{16,208},{24,216},{32,224},{40,232},{48,240},{56,2... | collective-permute-start | bytes 393224 | tf_op jit(solution)/shard_map/ppermute | solution.py:25
  99.6 2.9 %copy-start = (f32[4,4,128,128]{3,2,1,0:T(8,128)S(1)}, f32[4,4,128,128]{3,2,1,0:T(8,128)}, u32[]{:S(2)}) copy-start(f32[4,4,128,128]{3,2,1,0:T(8,128)} %fusion.19) | copy-start | bytes 3145732
  101.9 1.2 copy-start.2
  108.4 71.6 %reduce-scatter.5.cloned.1.call-start = ((), (), s32[]{:S(2)}) async-start(), calls=%async_computation.4 | async-start | bytes 2359296 | tf_op jit(solution)/shard_map/reduce_scatter | solution.py:105
Sparse Core Ops, SparseCore 0:
  9.2 37.4 all-gather.1
  108.5 33.5 reduce-scatter.2
  144.7 35.2 reduce-scatter.4

commit v3 on v1

v3 whole, which is shorter than its diff:
```python
import functools

import jax
import jax.numpy as jnp
from jax import lax
from jax.sharding import PartitionSpec as P

PHM = 4
SPAN = 128
HEAD = 128
BLOCK = 1024


epsilon = 1e-06


def ring_gather(value, axis, devices, size, stride, before):
    here = lax.axis_index(axis)
    k_here = (here // stride) % size
    total = value.astype(jnp.float32)
    earlier = jnp.zeros_like(total)
    for shift in range(1, size):
        pairs = []
        for i in range(devices):
            k = (i // stride) % size
            pairs.append((i, i + ((k + shift) % size - k) * stride))
        got = lax.ppermute(value, axis, pairs).astype(jnp.float32)
        source = (k_here - shift) % size
        total = total + got
        earlier = earlier + jnp.where(source < before, got, 0.0)
    return total, earlier


def exclusive_prefix(value, axis, devices, row):
    here = lax.axis_index(axis)
    pos, col = here % row, here // row
    row_total, before = ring_gather(value.astype(jnp.bfloat16), axis, devices, row, 1, pos)
    _, rows_before = ring_gather(row_total, axis, devices, devices // row, row, col)
    return before + rows_before


def fold_weights(blocks, mixing):
    projections, terms, rows, cols = blocks.shape
    folded = None
    for term_index in range(terms):
        mix = jnp.transpose(mixing[:, term_index], (1, 0, 2))[:, None, :, :, None]
        block = jnp.transpose(blocks[:, term_index].astype(jnp.float32), (1, 0, 2))
        part = mix * block[None, :, :, None, :]
        folded = part if folded is None else folded + part
    return folded.astype(jnp.bfloat16).reshape(PHM * rows, projections * PHM * cols)


def on_device(ctx_devices, ctx_row, tokens, qkv_blocks, out_blocks, mix_factors, head_gain):
    col_width = qkv_blocks.shape[-1]
    w_kv, w_q, w_out = lax.optimization_barrier(
        (
            fold_weights(qkv_blocks[1:], mix_factors[1:3]),
            fold_weights(qkv_blocks[:1], mix_factors[:1]),
            fold_weights(out_blocks[None], mix_factors[3:]),
        )
    )

    whole = lax.all_gather(tokens, "tp", axis=1, tiled=True)
    tok_rows = whole.shape[0]
    local_heads = PHM * col_width // HEAD
    nblk = tok_rows // SPAN
    width = PHM * col_width
    kv = jnp.dot(whole, w_kv, preferred_element_type=jnp.float32).astype(jnp.bfloat16)
    key_heads = kv[:, :width].reshape(nblk, SPAN, local_heads, HEAD)
    value_heads = kv[:, width:].reshape(nblk, SPAN, local_heads, HEAD)
    states = jnp.einsum(
        "nshd,nshe->nhde", key_heads, value_heads, preferred_element_type=jnp.float32
    )
    totals = jnp.sum(states, axis=0)
    earlier_sum = exclusive_prefix(totals, "ctx", ctx_devices, ctx_row)

    query = jnp.dot(whole, w_q, preferred_element_type=jnp.float32).astype(jnp.bfloat16)
    query_heads = query.reshape(nblk, SPAN, local_heads, HEAD)
    scores = jnp.einsum(
        "nshd,nthd->nhst", query_heads, key_heads, preferred_element_type=jnp.float32
    )
    causal = jnp.arange(SPAN)[:, None] >= jnp.arange(SPAN)[None, :]
    scores = jnp.where(causal[None, None], scores, 0.0).astype(jnp.bfloat16)
    within = jnp.einsum("nhst,nthe->nshe", scores, value_heads, preferred_element_type=jnp.float32)

    prefixes = [earlier_sum]
    for n in range(1, nblk):
        prefixes.append(prefixes[-1] + states[n - 1])
    prefix = jnp.stack(prefixes, axis=0)
    prefix_hi = prefix.astype(jnp.bfloat16)
    prefix_lo = (prefix - prefix_hi.astype(jnp.float32)).astype(jnp.bfloat16)
    carried_out = jnp.einsum(
        "nshd,nhde->nshe",
        jnp.concatenate([query_heads, query_heads], axis=-1),
        jnp.concatenate([prefix_hi, prefix_lo], axis=-2),
        preferred_element_type=jnp.float32,
    )
    combined = within + carried_out
    mean_sq = jnp.mean(combined * combined, axis=-1, keepdims=True)
    normed = combined * lax.rsqrt(mean_sq + epsilon) * head_gain
    attn = normed.astype(jnp.bfloat16).reshape(tok_rows, PHM * col_width)
    attn = lax.optimization_barrier(attn)
    partial_value = jnp.dot(attn, w_out, preferred_element_type=jnp.float32)
    reduced = lax.psum_scatter(
        partial_value.astype(jnp.bfloat16),
        "tp",
        scatter_dimension=1,
        tiled=True,
    )
    return reduced


def ctx_row_of(mesh):
    n = mesh.shape["ctx"]
    return 8 if n % 8 == 0 else n


def solution(mesh):
    placed = (P("ctx", "tp"), P(None, None, None, "tp"), P(None, "tp", None), P(), P(None, "tp"))
    return jax.shard_map(
        functools.partial(on_device, mesh.shape["ctx"], ctx_row_of(mesh)),
        mesh=mesh,
        in_specs=placed,
        out_specs=P("ctx", "tp"),
        check_vma=False,
    )
```

time: 161 us -> 176 us (1.093)
  local copies, waits for them, and re-layouts: 18.9 us -> 26.3 us
  other arithmetic: 22.5 us -> 27.2 us
  waiting for transfers between devices: 59.3 us -> 61.2 us
    add x0 -> x1, local copies, waits for them, and re-layouts: none -> 14.5 us  [fold_weights(): folded = part if folded is None else folded + part]
    unnamed x17 -> x9, local copies, waits for them, and re-layouts: 15.1 us -> 7 us
    ppermute x10, waiting for transfers between devices: 15 us -> 21.6 us  [ring_gather(): got = lax.ppermute(value, axis, pairs).astype(jnp.float32)]
    another operation x3, other arithmetic: 13.8 us -> 19.8 us
    convert_element_type x3 -> x4, other arithmetic: 7.28 us -> 1.9 us  [the longest x2 1.7 us: fold_weights(): block = jnp.transpose(blocks[:, term_index].astype(jnp.float32), (1, 0, 2))]
    all_gather x1, waiting for transfers between devices: 5.13 us -> 0.01 us  [on_device(): whole = lax.all_gather(tokens, 'tp', axis=1, tiled=True)]
    transpose x0 -> x9, local copies, waits for them, and re-layouts: none -> 3.26 us  [the longest x4 3.24 us: fold_weights(): block = jnp.transpose(blocks[:, term_index].astype(jnp.float32), (1, 0, 2))]
    add x0 -> x1, other arithmetic: none -> 2 us  [ring_gather(): total = total + got]
  transfers between devices with their start and end apart: 12 -> 12, of which waited for: 9 -> 9; matrix products, arithmetic and copies ran while one was open for 25% -> 32% of each run, Pallas kernels for 0% -> 0%
where the time goes in v3:
time: 176 us; the launch traced here: 175 us
  waiting for transfers between devices  61.2 us (35%)
  other arithmetic  27.2 us (15%)
  local copies, waits for them, and re-layouts  26.3 us (15%)
  matrix products  25.1 us (14%)
  starting transfers between devices  21.8 us (12%)
  between operations  13.7 us (8%)
    reduce_scatter x1, waiting for transfers between devices, on_device(): lax.psum_scatter(partial_value.astype(jnp.bfloat16), 'tp', scatter_dimens...  38.9 us
    ppermute x10, starting transfers between devices, ring_gather(): got = lax.ppermute(value, axis, pairs).astype(jnp.float32)  21.8 us
    ppermute x10, waiting for transfers between devices, ring_gather(): got = lax.ppermute(value, axis, pairs).astype(jnp.float32)  21.6 us
    another operation x3, other arithmetic  19.8 us
    add x1, local copies, waits for them, and re-layouts, fold_weights(): folded = part if folded is None else folded + part  14.5 us
    dot_general x1, matrix products, on_device(): jnp.dot(whole, w_kv, preferred_element_type=jnp.float32)  9.11 us
    unnamed x9, local copies, waits for them, and re-layouts  7 us
    dot_general x1, matrix products, on_device(): partial_value = jnp.dot(attn, w_out, preferred_element_type=jnp.float32)  6.49 us
  transfers between devices with their start and end apart: 12, of which 9 were waited for; matrix products, arithmetic and copies ran while one was open for 32% of the time, Pallas kernels for 0%

profile of v3, /device:TPU:8, one launch (start us, length us, event | category | flops | bytes accessed | tf_op | source)
XLA Modules:
  0.0 175.2 jit_solution(8106566087197291224)
XLA Ops:
  6.5 0.0 copy-start.1
  6.5 0.0 all-gather.2.cloned.1.call-start
  6.5 0.7 all-gather.2.cloned.1.call-update
  7.3 0.0 reduce-scatter.2.cloned.1.call-start
  7.3 1.8 %convert_bitcast_fusion.3 = (f32[1024,2,128]{2,0,1:T(8,128)S(1)}, f32[1024,2,128]{2,0,1:T(8,128)S(1)}, f32[1024,2,128]{2,0,1:T(8,128)S(1)}, f32[1024,2,128]{2,0,1:T(8,128)S(1)}) fusion(bf16[3,4,1024,128]{3,2,1,0:T(8,128)(2,1)} %param.6), kind=kLoop, calls=%fused_computation.24 | loop fusion | flops 1048576 | bytes 6291456 | tf_op jit(solution)/shard_map/transpose | solution.py:47
  9.1 0.8 copy.27
  9.9 0.0 copy-done.1
  10.0 0.8 copy.25
  10.8 0.8 copy.23
  11.6 0.8 copy.21
  12.5 10.3 %add_convert_fusion = bf16[4,1024,2,4,128]{4,3,2,1,0:T(4,128)(2,1)} fusion(f32[1024,2,128]{2,1,0:T(2,128)S(1)} %copy.27, f32[4,2,4]{2,1,0:T(2,128)S(1)} %copy.26, f32[1024,2,128]{2,1,0:T(2,128)S(1)} %copy.25, f32[4,2,4]{2,1,0:T(2,128)S(1)} %copy.24, f32[1024,2,128]{2,1,0:T(2,128)S(1)} %copy.23, f32[4,2,4]{2,1,0:T(2,128)S(1)} %copy.22, ...), kind=kLoop, calls=%fused_computation | loop fusion | flops 33554432 | bytes 12583424 | tf_op jit(solution)/shard_map/convert.18
  22.8 14.5 %add.192 = bf16[4096,1024]{1,0:T(8,128)(2,1)} reshape(bf16[4,1024,2,4,128]{4,3,2,1,0:T(4,128)(2,1)} %add_convert_fusion) | data formatting | bytes 16777216 | tf_op jit(solution)/shard_map/add | solution.py:49
  37.3 0.0 copy-start
  37.3 1.5 bitcast_convert_fusion.3
  38.8 4.6 %add_convert_fusion.2 = bf16[4,1024,4,128]{3,2,1,0:T(4,128)(2,1)S(1)} fusion(f32[1024,128]{1,0:T(8,128)S(1)} %get-tuple-element.15, f32[4,4]{1,0:T(4,128)S(1)} %get-tuple-element.31, f32[1024,128]{1,0:T(8,128)S(1)} %get-tuple-element.16, f32[4,4]{1,0:T(4,128)S(1)} %get-tuple-element.32, f32[1024,128]{1,0:T(8,128)S(1)} %get-tuple-element.14, ...), kind=kLoop, calls=%fused_computation.2 | loop fusion | flops 16777216 | bytes 6291712 | tf_op jit(solution)/shard_map/convert.17
  43.4 2.6 %copy.48 = bf16[512,8,4,128]{3,1,2,0:T(8,128)(2,1)} copy(bf16[512,8,4,128]{3,2,1,0:T(4,128)(2,1)S(1)} %bitcast.152) | data formatting | bytes 8388608
  46.0 0.0 copy-done
  46.0 0.2 fusion.32
  46.3 4.8 %add_convert_fusion.1 = bf16[4,128,4,1024]{3,2,1,0:T(4,128)(2,1)S(1)} fusion(f32[128,1024]{1,0:T(8,128)S(1)} %get-tuple-element.26, f32[4,4]{1,0:T(4,128)S(1)} %get-tuple-element.35, f32[128,1024]{1,0:T(8,128)S(1)} %get-tuple-element.27, f32[4,4]{1,0:T(4,128)S(1)} %get-tuple-element.36, f32[128,1024]{1,0:T(8,128)S(1)} %get-tuple-element.28, ...), kind=kLoop, calls=%fused_computation.1 | loop fusion | flops 16777216 | bytes 6291712 | tf_op jit(solution)/shard_map/convert.16
  51.1 4.3 %copy.37 = bf16[64,8,4,1024]{3,1,2,0:T(8,128)(2,1)} copy(bf16[64,8,4,1024]{3,2,1,0:T(4,128)(2,1)S(1)} %bitcast.153) | data formatting | bytes 8388608
  55.4 0.0 all-gather.2.cloned.1.call-done
  55.4 9.1 %fusion = bf16[512,1024]{0,1:T(8,128)(2,1)S(1)} fusion(bf16[4096,1024]{1,0:T(8,128)(2,1)} %add.192, bf16[512,4096]{1,0:T(8,128)(2,1)} %all-gather.2.cloned.1.call-done), kind=kOutput, calls=%fused_computation.7 | convolution fusion | flops 4295491584 | bytes 13631488 | tf_op jit(solution)/shard_map/dot_general | solution.py:68
  64.5 0.1 fusion.38
  64.6 0.1 reshape.236
  64.7 0.4 copy.30
  65.1 0.1 reshape.238
  65.2 0.3 fusion.39
  65.5 5.8 %collective-permute-start.6 = (bf16[4,128,128]{2,1,0:T(8,128)(2,1)S(1)}, bf16[4,128,128]{2,1,0:T(8,128)(2,1)S(1)}, u32[]{:S(2)}, u32[]{:S(2)}) collective-permute-start(bf16[4,128,128]{2,1,0:T(8,128)(2,1)S(1)} %get-tuple-element.41), channel_id=1, source_target_pairs={{0,56},{8,0},{16,8},{24,16},{32,24},{40,32},{48,40},{56,48},{64,12... | collective-permute-start | bytes 393224 | tf_op jit(solution)/shard_map/ppermute | solution.py:27
  71.3 1.5 collective-permute-start.5
  72.8 0.6 collective-permute-start.4
  73.4 5.0 %collective-permute-start.3 = (bf16[4,128,128]{2,1,0:T(8,128)(2,1)S(1)}, bf16[4,128,128]{2,1,0:T(8,128)(2,1)}, u32[]{:S(2)}, u32[]{:S(2)}) collective-permute-start(bf16[4,128,128]{2,1,0:T(8,128)(2,1)S(1)} %get-tuple-element.41), channel_id=1, source_target_pairs={{0,32},{8,40},{16,48},{24,56},{32,0},{40,8},{48,16},{56,24},{64,96... | collective-permute-start | bytes 393224 | tf_op jit(solution)/shard_map/ppermute | solution.py:27
  78.4 0.0 collective-permute-start.2
  78.4 0.0 collective-permute-done.6
  78.4 2.4 %collective-permute-start.1 = (bf16[4,128,128]{2,1,0:T(8,128)(2,1)S(1)}, bf16[4,128,128]{2,1,0:T(8,128)(2,1)}, u32[]{:S(2)}, u32[]{:S(2)}) collective-permute-start(bf16[4,128,128]{2,1,0:T(8,128)(2,1)S(1)} %get-tuple-element.41), channel_id=1, source_target_pairs={{0,16},{8,24},{16,32},{24,40},{32,48},{40,56},{48,0},{56,8},{64,80... | collective-permute-start | bytes 393224 | tf_op jit(solution)/shard_map/ppermute | solution.py:27
  80.9 1.1 collective-permute-done.5
  82.0 1.5 collective-permute-start
  83.5 5.8 %fusion.4 = bf16[512,512]{0,1:T(8,128)(2,1)S(1)} fusion(bf16[4096,512]{1,0:T(8,128)(2,1)} %bitcast.155, bf16[512,4096]{1,0:T(8,128)(2,1)} %all-gather.2.cloned.1.call-done), kind=kOutput, calls=%fused_computation.13 | convolution fusion | flops 2147745792 | bytes 8912896 | tf_op jit(solution)/shard_map/dot_general | solution.py:77
  89.3 0.1 reshape.237
  89.4 0.4 copy.32
  89.8 4.0 %collective-permute-done.4 = bf16[4,128,128]{2,1,0:T(8,128)(2,1)} collective-permute-done((bf16[4,128,128]{2,1,0:T(8,128)(2,1)S(1)}, bf16[4,128,128]{2,1,0:T(8,128)(2,1)}, u32[]{:S(2)}, u32[]{:S(2)}) %collective-permute-start.4) | collective-permute-done | bytes 131104 | tf_op jit(solution)/shard_map/ppermute | solution.py:27
  93.8 0.0 collective-permute-done.3
  93.8 3.3 %collective-permute-done.2 = bf16[4,128,128]{2,1,0:T(8,128)(2,1)} collective-permute-done((bf16[4,128,128]{2,1,0:T(8,128)(2,1)S(1)}, bf16[4,128,128]{2,1,0:T(8,128)(2,1)}, u32[]{:S(2)}, u32[]{:S(2)}) %collective-permute-start.2) | collective-permute-done | bytes 131104 | tf_op jit(solution)/shard_map/ppermute | solution.py:27
  97.1 3.0 %collective-permute-done.1 = bf16[4,128,128]{2,1,0:T(8,128)(2,1)} collective-permute-done((bf16[4,128,128]{2,1,0:T(8,128)(2,1)S(1)}, bf16[4,128,128]{2,1,0:T(8,128)(2,1)}, u32[]{:S(2)}, u32[]{:S(2)}) %collective-permute-start.1) | collective-permute-done | bytes 131104 | tf_op jit(solution)/shard_map/ppermute | solution.py:27
  100.0 1.4 collective-permute-done
  101.5 2.0 %convert_add_fusion = f32[4,128,128]{2,1,0:T(8,128)} fusion(bf16[4,128,128]{2,1,0:T(8,128)(2,1)S(1)} %collective-permute-done.6, bf16[4,128,128]{2,1,0:T(8,128)(2,1)S(1)} %collective-permute-done.5, bf16[4,128,128]{2,1,0:T(8,128)(2,1)} %collective-permute-done.4, bf16[4,128,128]{2,1,0:T(8,128)(2,1)} %collective-permute-done.3, ...), kind=kLoop, calls=%fused_computation.35 | loop fusion | flops 983040 | bytes 1310720 | tf_op jit(solution)/shard_map/add | solution.py:29
  103.5 0.5 collective-permute-start.9
  104.0 2.6 %collective-permute-start.8 = (f32[4,128,128]{2,1,0:T(8,128)}, f32[4,128,128]{2,1,0:T(8,128)S(1)}, u32[]{:S(2)}, u32[]{:S(2)}) collective-permute-start(f32[4,128,128]{2,1,0:T(8,128)} %convert_add_fusion), channel_id=1, source_target_pairs={{0,128},{8,136},{16,144},{24,152},{32,160},{40,168},{48,176},{56,1... | collective-permute-start | bytes 786440 | tf_op jit(solution)/shard_map/ppermute | solution.py:27
  106.5 1.9 %collective-permute-start.7 = (f32[4,128,128]{2,1,0:T(8,128)}, f32[4,128,128]{2,1,0:T(8,128)}, u32[]{:S(2)}, u32[]{:S(2)}) collective-permute-start(f32[4,128,128]{2,1,0:T(8,128)} %convert_add_fusion), channel_id=1, source_target_pairs={{0,64},{8,72},{16,80},{24,88},{32,96},{40,104},{48,112},{56,120},{... | collective-permute-start | bytes 786440 | tf_op jit(solution)/shard_map/ppermute | solution.py:27
  108.4 1.6 fusion.3
  110.1 1.5 collective-permute-done.9
  111.6 6.5 %collective-permute-done.8 = f32[4,128,128]{2,1,0:T(8,128)S(1)} collective-permute-done((f32[4,128,128]{2,1,0:T(8,128)}, f32[4,128,128]{2,1,0:T(8,128)S(1)}, u32[]{:S(2)}, u32[]{:S(2)}) %collective-permute-start.8) | collective-permute-done | bytes 262176 | tf_op jit(solution)/shard_map/ppermute | solution.py:27
  118.1 0.8 collective-permute-done.7
  118.9 1.4 fusion.33
  120.3 0.1 fusion.36
  120.4 0.1 subtract_convert_fusion
  120.5 0.1 fusion.11
  120.6 1.7 multiply_reduce_fusion
  122.4 0.0 copy-done.2
  122.4 0.2 multiply_convert_fusion
  122.6 0.3 copy.34
  122.9 0.1 copy.49
  123.0 6.5 %convolution_convert_fusion = bf16[512,4096]{1,0:T(8,128)(2,1)} fusion(bf16[512,512]{1,0:T(8,128)(2,1)S(1)} %bitcast.160, bf16[512,4096]{1,0:T(8,128)(2,1)} %bitcast.154), kind=kOutput, calls=%fused_computation.3 | convolution fusion | flops 2149580800 | bytes 8912896 | tf_op jit(solution)/shard_map/dot_general | solution.py:103
  129.5 0.0 reduce-scatter.2.cloned.1.call-update
  129.5 38.9 %reduce-scatter.2.cloned.1.call-done = bf16[512,512]{1,0:T(8,128)(2,1)} async-done(((bf16[512,4096]{1,0:T(8,128)(2,1)}), bf16[512,512]{1,0:T(8,128)(2,1)}) %reduce-scatter.2.cloned.1.call-update) | async-done | bytes 524304 | tf_op jit(solution)/shard_map/reduce_scatter | solution.py:104
  (9 shorter events, 0.0 us)
Async XLA Ops:
  6.5 3.4 %copy-start.1 = (f32[4,4,4,4]{3,2,1,0:T(4,128)S(1)}, f32[4,4,4,4]{3,2,1,0:T(4,128)}, u32[]{:S(2)}) copy-start(f32[4,4,4,4]{3,2,1,0:T(4,128)} %param.8) | copy-start | bytes 3076
  6.5 48.8 %all-gather.2.cloned.1.call-start = ((), (), s32[]{:S(2)}) async-start(), calls=%async_computation.1 | async-start | bytes 4718592 | tf_op jit(solution)/shard_map/all_gather | solution.py:63
  7.3 161.1 %reduce-scatter.2.cloned.1.call-start = ((), (), s32[]{:S(2)}) async-start(), calls=%async_computation.2 | async-start | bytes 4718592 | tf_op jit(solution)/shard_map/reduce_scatter | solution.py:104
  37.3 8.8 %copy-start = (bf16[4,128,1024]{2,1,0:T(8,128)(2,1)S(1)}, bf16[4,128,1024]{2,1,0:T(8,128)(2,1)}, u32[]{:S(2)}) copy-start(bf16[4,128,1024]{2,1,0:T(8,128)(2,1)} %param.7) | copy-start | bytes 3145732
  65.5 12.9 %collective-permute-start.6 = (bf16[4,128,128]{2,1,0:T(8,128)(2,1)S(1)}, bf16[4,128,128]{2,1,0:T(8,128)(2,1)S(1)}, u32[]{:S(2)}, u32[]{:S(2)}) collective-permute-start(bf16[4,128,128]{2,1,0:T(8,128)(2,1)S(1)} %get-tuple-element.41), channel_id=1, source_target_pairs={{0,56},{8,0},{16,8},{24,16},{32,24},{40,32},{48,40},{56,48},{64,12... | collective-permute-start | bytes 393224 | tf_op jit(solution)/shard_map/ppermute | solution.py:27
  71.3 10.7 %collective-permute-start.5 = (bf16[4,128,128]{2,1,0:T(8,128)(2,1)S(1)}, bf16[4,128,128]{2,1,0:T(8,128)(2,1)S(1)}, u32[]{:S(2)}, u32[]{:S(2)}) collective-permute-start(bf16[4,128,128]{2,1,0:T(8,128)(2,1)S(1)} %get-tuple-element.41), channel_id=1, source_target_pairs={{0,48},{8,56},{16,0},{24,8},{32,16},{40,24},{48,32},{56,40},{64,11... | collective-permute-start | bytes 393224 | tf_op jit(solution)/shard_map/ppermute | solution.py:27
  72.8 21.0 %collective-permute-start.4 = (bf16[4,128,128]{2,1,0:T(8,128)(2,1)S(1)}, bf16[4,128,128]{2,1,0:T(8,128)(2,1)}, u32[]{:S(2)}, u32[]{:S(2)}) collective-permute-start(bf16[4,128,128]{2,1,0:T(8,128)(2,1)S(1)} %get-tuple-element.41), channel_id=1, source_target_pairs={{0,40},{8,48},{16,56},{24,0},{32,8},{40,16},{48,24},{56,32},{64,10... | collective-permute-start | bytes 393224 | tf_op jit(solution)/shard_map/ppermute | solution.py:27
  73.4 20.4 %collective-permute-start.3 = (bf16[4,128,128]{2,1,0:T(8,128)(2,1)S(1)}, bf16[4,128,128]{2,1,0:T(8,128)(2,1)}, u32[]{:S(2)}, u32[]{:S(2)}) collective-permute-start(bf16[4,128,128]{2,1,0:T(8,128)(2,1)S(1)} %get-tuple-element.41), channel_id=1, source_target_pairs={{0,32},{8,40},{16,48},{24,56},{32,0},{40,8},{48,16},{56,24},{64,96... | collective-permute-start | bytes 393224 | tf_op jit(solution)/shard_map/ppermute | solution.py:27
  78.4 18.6 %collective-permute-start.2 = (bf16[4,128,128]{2,1,0:T(8,128)(2,1)S(1)}, bf16[4,128,128]{2,1,0:T(8,128)(2,1)}, u32[]{:S(2)}, u32[]{:S(2)}) collective-permute-start(bf16[4,128,128]{2,1,0:T(8,128)(2,1)S(1)} %get-tuple-element.41), channel_id=1, source_target_pairs={{0,24},{8,32},{16,40},{24,48},{32,56},{40,0},{48,8},{56,16},{64,88... | collective-permute-start | bytes 393224 | tf_op jit(solution)/shard_map/ppermute | solution.py:27
  78.4 21.6 %collective-permute-start.1 = (bf16[4,128,128]{2,1,0:T(8,128)(2,1)S(1)}, bf16[4,128,128]{2,1,0:T(8,128)(2,1)}, u32[]{:S(2)}, u32[]{:S(2)}) collective-permute-start(bf16[4,128,128]{2,1,0:T(8,128)(2,1)S(1)} %get-tuple-element.41), channel_id=1, source_target_pairs={{0,16},{8,24},{16,32},{24,40},{32,48},{40,56},{48,0},{56,8},{64,80... | collective-permute-start | bytes 393224 | tf_op jit(solution)/shard_map/ppermute | solution.py:27
  82.0 19.5 %collective-permute-start = (bf16[4,128,128]{2,1,0:T(8,128)(2,1)S(1)}, bf16[4,128,128]{2,1,0:T(8,128)(2,1)}, u32[]{:S(2)}, u32[]{:S(2)}) collective-permute-start(bf16[4,128,128]{2,1,0:T(8,128)(2,1)S(1)} %get-tuple-element.41), channel_id=1, source_target_pairs={{0,8},{8,16},{16,24},{24,32},{32,40},{40,48},{48,56},{56,0},{64,72... | collective-permute-start | bytes 393224 | tf_op jit(solution)/shard_map/ppermute | solution.py:27
  103.5 18.9 %copy-start.2 = (f32[4,128]{1,0:T(4,128)S(1)}, f32[4,128]{1,0:T(4,128)}, u32[]{:S(2)}) copy-start(f32[4,128]{1,0:T(4,128)} %param.9) | copy-start | bytes 6148
  103.5 8.1 %collective-permute-start.9 = (f32[4,128,128]{2,1,0:T(8,128)}, f32[4,128,128]{2,1,0:T(8,128)S(1)}, u32[]{:S(2)}, u32[]{:S(2)}) collective-permute-start(f32[4,128,128]{2,1,0:T(8,128)} %convert_add_fusion), channel_id=1, source_target_pairs={{0,192},{8,200},{16,208},{24,216},{32,224},{40,232},{48,240},{56,2... | collective-permute-start | bytes 786440 | tf_op jit(solution)/shard_map/ppermute | solution.py:27
  104.0 14.2 %collective-permute-start.8 = (f32[4,128,128]{2,1,0:T(8,128)}, f32[4,128,128]{2,1,0:T(8,128)S(1)}, u32[]{:S(2)}, u32[]{:S(2)}) collective-permute-start(f32[4,128,128]{2,1,0:T(8,128)} %convert_add_fusion), channel_id=1, source_target_pairs={{0,128},{8,136},{16,144},{24,152},{32,160},{40,168},{48,176},{56,1... | collective-permute-start | bytes 786440 | tf_op jit(solution)/shard_map/ppermute | solution.py:27
  106.5 12.4 %collective-permute-start.7 = (f32[4,128,128]{2,1,0:T(8,128)}, f32[4,128,128]{2,1,0:T(8,128)}, u32[]{:S(2)}, u32[]{:S(2)}) collective-permute-start(f32[4,128,128]{2,1,0:T(8,128)} %convert_add_fusion), channel_id=1, source_target_pairs={{0,64},{8,72},{16,80},{24,88},{32,96},{40,104},{48,112},{56,120},{... | collective-permute-start | bytes 786440 | tf_op jit(solution)/shard_map/ppermute | solution.py:27
Sparse Core Ops, SparseCore 0:
  9.2 37.4 all-gather.1
  129.6 38.7 reduce-scatter.1

commit v4 on v3

--- a/solution.py
+++ b/solution.py
@@ -40,32 +40,43 @@
 
 
 def fold_weights(blocks, mixing):
-    projections, terms, rows, cols = blocks.shape
+    terms, rows, cols = blocks.shape
     folded = None
     for term_index in range(terms):
-        mix = jnp.transpose(mixing[:, term_index], (1, 0, 2))[:, None, :, :, None]
-        block = jnp.transpose(blocks[:, term_index].astype(jnp.float32), (1, 0, 2))
-        part = mix * block[None, :, :, None, :]
+        part = (
+            mixing[term_index][:, None, :, None]
+            * blocks[term_index].astype(jnp.float32)[None, :, None, :]
+        )
         folded = part if folded is None else folded + part
-    return folded.astype(jnp.bfloat16).reshape(PHM * rows, projections * PHM * cols)
+    return folded.reshape(PHM * rows, PHM * cols)
+
+
+def split_bf16(value):
+    high = value.astype(jnp.bfloat16)
+    return high, (value - high.astype(jnp.float32)).astype(jnp.bfloat16)
+
+
+def project(whole, parts):
+    high, low = parts
+    out = jnp.dot(whole, high, preferred_element_type=jnp.float32)
+    out = out + jnp.dot(whole, low, preferred_element_type=jnp.float32)
+    return out.astype(jnp.bfloat16)
 
 
 def on_device(ctx_devices, ctx_row, tokens, qkv_blocks, out_blocks, mix_factors, head_gain):
     col_width = qkv_blocks.shape[-1]
-    w_kv, w_q, w_out = lax.optimization_barrier(
-        (
-            fold_weights(qkv_blocks[1:], mix_factors[1:3]),
-            fold_weights(qkv_blocks[:1], mix_factors[:1]),
-            fold_weights(out_blocks[None], mix_factors[3:]),
-        )
+    w_kv = split_bf16(
+        jnp.concatenate([fold_weights(qkv_blocks[p], mix_factors[p]) for p in (1, 2)], axis=1)
     )
+    w_q = split_bf16(fold_weights(qkv_blocks[0], mix_factors[0]))
+    w_out = fold_weights(out_blocks, mix_factors[3]).astype(jnp.bfloat16)
 
     whole = lax.all_gather(tokens, "tp", axis=1, tiled=True)
     tok_rows = whole.shape[0]
     local_heads = PHM * col_width // HEAD
     nblk = tok_rows // SPAN
     width = PHM * col_width
-    kv = jnp.dot(whole, w_kv, preferred_element_type=jnp.float32).astype(jnp.bfloat16)
+    kv = project(whole, w_kv)
     key_heads = kv[:, :width].reshape(nblk, SPAN, local_heads, HEAD)
     value_heads = kv[:, width:].reshape(nblk, SPAN, local_heads, HEAD)
     states = jnp.einsum(
@@ -74,7 +85,7 @@
     totals = jnp.sum(states, axis=0)
     earlier_sum = exclusive_prefix(totals, "ctx", ctx_devices, ctx_row)
 
-    query = jnp.dot(whole, w_q, preferred_element_type=jnp.float32).astype(jnp.bfloat16)
+    query = project(whole, w_q)
     query_heads = query.reshape(nblk, SPAN, local_heads, HEAD)
     scores = jnp.einsum(
         "nshd,nthd->nhst", query_heads, key_heads, preferred_element_type=jnp.float32
@@ -99,7 +110,6 @@
     mean_sq = jnp.mean(combined * combined, axis=-1, keepdims=True)
     normed = combined * lax.rsqrt(mean_sq + epsilon) * head_gain
     attn = normed.astype(jnp.bfloat16).reshape(tok_rows, PHM * col_width)
-    attn = lax.optimization_barrier(attn)
     partial_value = jnp.dot(attn, w_out, preferred_element_type=jnp.float32)
     reduced = lax.psum_scatter(
         partial_value.astype(jnp.bfloat16),

time: 176 us -> 184 us (1.045)
  matrix products: 25.1 us -> 47.5 us
  local copies, waits for them, and re-layouts: 26.3 us -> 17.4 us
  waiting for transfers between devices: 61.2 us -> 57.9 us
  other arithmetic: 27.2 us -> 25.2 us
    dot_general x2 -> x4, matrix products: 14.9 us -> 36.6 us  [the longest x2 18.6 us: project(): out = jnp.dot(whole, high, preferred_element_type=jnp.float32)]
    another operation x3 -> x0, other arithmetic: 19.8 us -> none
    add x1 -> x0, local copies, waits for them, and re-layouts: 14.5 us -> none  [fold_weights(): folded = part if folded is None else folded + part]
    add x0 -> x2, other arithmetic: none -> 13.7 us  [fold_weights(): folded = part if folded is None else folded + part]
    convert_element_type x2 -> x3, other arithmetic: 1.7 us -> 7.69 us  [the longest x1 5.62 us: on_device(): w_out = fold_weights(out_blocks, mix_factors[3]).astype(jnp.bfloat16)]
    ppermute x10, waiting for transfers between devices: 21.6 us -> 16 us  [ring_gather(): got = lax.ppermute(value, axis, pairs).astype(jnp.float32)]
    concatenate x0 -> x1, local copies, waits for them, and re-layouts: none -> 4.27 us  [on_device(): jnp.concatenate([fold_weights(qkv_blocks[p], mix_factors[p]) for p in (1,...]
    unnamed x9 -> x14, local copies, waits for them, and re-layouts: 7 us -> 10.7 us
  transfers between devices with their start and end apart: 12 -> 12, of which waited for: 9 -> 8; matrix products, arithmetic and copies ran while one was open for 32% -> 27% of each run, Pallas kernels for 0% -> 0%
where the time goes in v4:
time: 184 us; the launch traced here: 183 us
  waiting for transfers between devices  57.9 us (31%)
  matrix products  47.5 us (26%)
  other arithmetic  25.2 us (14%)
  starting transfers between devices  21.8 us (12%)
  local copies, waits for them, and re-layouts  17.4 us (9%)
  between operations  13.6 us (7%)
    reduce_scatter x1, waiting for transfers between devices, on_device(): lax.psum_scatter(partial_value.astype(jnp.bfloat16), 'tp', scatter_dimens...  39.1 us
    ppermute x10, starting transfers between devices, ring_gather(): got = lax.ppermute(value, axis, pairs).astype(jnp.float32)  21.7 us
    dot_general x2, matrix products, project(): out = jnp.dot(whole, high, preferred_element_type=jnp.float32)  18.6 us
    dot_general x2, matrix products, project(): out = out + jnp.dot(whole, low, preferred_element_type=jnp.float32)  18 us
    ppermute x10, waiting for transfers between devices, ring_gather(): got = lax.ppermute(value, axis, pairs).astype(jnp.float32)  16 us
    add x2, other arithmetic, fold_weights(): folded = part if folded is None else folded + part  13.7 us
    unnamed x14, local copies, waits for them, and re-layouts  10.7 us
    dot_general x1, matrix products, on_device(): partial_value = jnp.dot(attn, w_out, preferred_element_type=jnp.float32)  6.49 us
  transfers between devices with their start and end apart: 12, of which 8 were waited for; matrix products, arithmetic and copies ran while one was open for 27% of the time, Pallas kernels for 0%

profile of v4, /device:TPU:8, one launch (start us, length us, event | category | flops | bytes accessed | tf_op | source)
XLA Modules:
  0.0 183.3 jit_solution(2547419844864629867)
XLA Ops:
  6.5 0.0 all-gather.2.cloned.1.call-start
  6.5 0.7 all-gather.2.cloned.1.call-update
  7.3 0.0 reduce-scatter.2.cloned.1.call-start
  7.3 0.9 slice_bitcast_fusion.10
  8.2 0.0 copy-start
  8.2 1.6 bitcast_convert_fusion.5
  9.8 5.6 %add_convert_fusion = bf16[4,128,4,1024]{3,2,1,0:T(4,128)(2,1)} fusion(f32[128,1024]{1,0:T(8,128)S(1)} %get-tuple-element.25, f32[4,4]{1,0:T(4,128)S(1)} %get-tuple-element.41, f32[128,1024]{1,0:T(8,128)S(1)} %get-tuple-element.26, f32[4,4]{1,0:T(4,128)S(1)} %get-tuple-element.42, f32[128,1024]{1,0:T(8,128)S(1)} %get-tuple-element.24, ...), kind=kLoop, calls=%fused_computation.7 | loop fusion | flops 16777216 | bytes 6291712 | tf_op jit(solution)/shard_map/convert_element_type | solution.py:72
  15.4 6.5 %copy.24 = bf16[64,8,4,1024]{3,1,2,0:T(8,128)(2,1)} copy(bf16[64,8,4,1024]{3,2,1,0:T(4,128)(2,1)} %bitcast.168) | data formatting | bytes 8388608
  21.9 0.0 copy-done
  21.9 0.5 bitcast_convert_fusion.9
  22.4 8.0 %multiply_add_fusion.1 = (f32[4,1024,4,128]{3,2,1,0:T(4,128)S(1)}, f32[4,1024,4,128]{3,2,1,0:T(4,128)S(1)}) fusion(f32[1024,128]{1,0:T(8,128)S(1)} %get-tuple-element.9, f32[4,4]{1,0:T(4,128)S(1)} %get-tuple-element.33, f32[1024,128]{1,0:T(8,128)S(1)} %get-tuple-element.10, f32[4,4]{1,0:T(4,128)S(1)} %get-tuple-element.34, ...), kind=kLoop, calls=%fused_computation.9 | loop fusion | flops 29360128 | bytes 20972032 | tf_op jit(solution)/shard_map/add | solution.py:50
  30.4 4.2 %bitcast_dynamic-update-slice_fusion.1 = f32[4096,1024]{1,0:T(8,128)} fusion(f32[512,8,4,128]{3,2,1,0:T(4,128)S(1)} %bitcast.167), kind=kLoop, calls=%fused_computation.6 | loop fusion | bytes 16777216
  34.6 4.3 %bitcast_dynamic-update-slice_fusion = f32[4096,1024]{1,0:T(8,128)} fusion(f32[4096,1024]{1,0:T(8,128)} %bitcast_dynamic-update-slice_fusion.1, f32[512,8,4,128]{3,2,1,0:T(4,128)S(1)} %bitcast.166), kind=kLoop, calls=%fused_computation.5 | loop fusion | bytes 16777216 | tf_op jit(solution)/shard_map/concatenate | solution.py:69
  38.9 5.7 %multiply_add_fusion = f32[4,1024,4,128]{3,2,1,0:T(4,128)} fusion(f32[1024,128]{1,0:T(8,128)S(1)} %get-tuple-element.17, f32[4,4]{1,0:T(4,128)S(1)} %get-tuple-element.30, f32[1024,128]{1,0:T(8,128)S(1)} %get-tuple-element.18, f32[4,4]{1,0:T(4,128)S(1)} %get-tuple-element.31, f32[1024,128]{1,0:T(8,128)S(1)} %get-tuple-element.8, ...), kind=kLoop, calls=%fused_computation.8 | loop fusion | flops 14680064 | bytes 10486016 | tf_op jit(solution)/shard_map/add | solution.py:50
  44.6 2.0 %all-gather.2.cloned.1.call-done = bf16[512,4096]{1,0:T(8,128)(2,1)} async-done(((bf16[512,512]{1,0:T(8,128)(2,1)}), bf16[512,4096]{1,0:T(8,128)(2,1)}) %all-gather.2.cloned.1.call-update) | async-done | bytes 4194320 | tf_op jit(solution)/shard_map/all_gather | solution.py:74
  46.7 11.5 %fusion.6 = f32[1024,512]{1,0:T(8,128)S(1)} fusion(bf16[512,4096]{1,0:T(8,128)(2,1)} %all-gather.2.cloned.1.call-done, f32[4096,1024]{1,0:T(8,128)} %bitcast_dynamic-update-slice_fusion), kind=kOutput, calls=%fused_computation.15 | convolution fusion | flops 4299161600 | bytes 23068672 | tf_op jit(solution)/shard_map/dot_general | solution.py:61
  58.2 0.0 copy-done.2
  58.2 15.6 %fusion.8 = bf16[512,1024]{0,1:T(8,128)(2,1)S(1)} fusion(f32[1024,512]{1,0:T(8,128)S(1)} %fusion.6, bf16[512,4096]{1,0:T(8,128)(2,1)S(1)} %copy-done.2, f32[4096,1024]{1,0:T(8,128)} %bitcast_dynamic-update-slice_fusion), kind=kOutput, calls=%fused_computation.18 | convolution fusion | flops 4312793088 | bytes 24117248 | tf_op jit(solution)/shard_map/dot_general | solution.py:62
  73.8 0.1 fusion.52
  73.9 0.1 reshape.302
  74.0 0.4 copy.14
  74.4 0.1 reshape.304
  74.6 0.0 slice-start
  74.6 0.0 copy-start.3
  74.6 0.9 fusion.53
  75.5 1.6 collective-permute-start
  77.1 2.5 %collective-permute-start.1 = (bf16[4,128,128]{2,1,0:T(8,128)(2,1)}, bf16[4,128,128]{2,1,0:T(8,128)(2,1)S(1)}, u32[]{:S(2)}, u32[]{:S(2)}) collective-permute-start(bf16[4,128,128]{2,1,0:T(8,128)(2,1)} %get-tuple-element.43), channel_id=1, source_target_pairs={{0,16},{8,24},{16,32},{24,40},{32,48},{40,56},{48,0},{56,8},{64,80... | collective-permute-start | bytes 393224 | tf_op jit(solution)/shard_map/ppermute | solution.py:27
  79.6 3.1 %collective-permute-start.2 = (bf16[4,128,128]{2,1,0:T(8,128)(2,1)}, bf16[4,128,128]{2,1,0:T(8,128)(2,1)S(1)}, u32[]{:S(2)}, u32[]{:S(2)}) collective-permute-start(bf16[4,128,128]{2,1,0:T(8,128)(2,1)} %get-tuple-element.43), channel_id=1, source_target_pairs={{0,24},{8,32},{16,40},{24,48},{32,56},{40,0},{48,8},{56,16},{64,88... | collective-permute-start | bytes 393224 | tf_op jit(solution)/shard_map/ppermute | solution.py:27
  82.7 1.9 %collective-permute-start.3 = (bf16[4,128,128]{2,1,0:T(8,128)(2,1)}, bf16[4,128,128]{2,1,0:T(8,128)(2,1)}, u32[]{:S(2)}, u32[]{:S(2)}) collective-permute-start(bf16[4,128,128]{2,1,0:T(8,128)(2,1)} %get-tuple-element.43), channel_id=1, source_target_pairs={{0,32},{8,40},{16,48},{24,56},{32,0},{40,8},{48,16},{56,24},{64,96... | collective-permute-start | bytes 393224 | tf_op jit(solution)/shard_map/ppermute | solution.py:27
  84.6 3.6 %collective-permute-start.4 = (bf16[4,128,128]{2,1,0:T(8,128)(2,1)}, bf16[4,128,128]{2,1,0:T(8,128)(2,1)}, u32[]{:S(2)}, u32[]{:S(2)}) collective-permute-start(bf16[4,128,128]{2,1,0:T(8,128)(2,1)} %get-tuple-element.43), channel_id=1, source_target_pairs={{0,40},{8,48},{16,56},{24,0},{32,8},{40,16},{48,24},{56,32},{64,10... | collective-permute-start | bytes 393224 | tf_op jit(solution)/shard_map/ppermute | solution.py:27
  88.2 7.1 %fusion.2 = f32[512,512]{1,0:T(8,128)S(1)} fusion(bf16[512,4096]{1,0:T(8,128)(2,1)} %all-gather.2.cloned.1.call-done, f32[512,8,4,128]{3,2,1,0:T(4,128)} %bitcast.169), kind=kOutput, calls=%fused_computation.12 | convolution fusion | flops 2147483648 | bytes 13631488 | tf_op jit(solution)/shard_map/dot_general | solution.py:61
  95.3 0.0 collective-permute-done
  95.3 3.0 %collective-permute-start.5 = (bf16[4,128,128]{2,1,0:T(8,128)(2,1)}, bf16[4,128,128]{2,1,0:T(8,128)(2,1)}, u32[]{:S(2)}, u32[]{:S(2)}) collective-permute-start(bf16[4,128,128]{2,1,0:T(8,128)(2,1)} %get-tuple-element.43), channel_id=1, source_target_pairs={{0,48},{8,56},{16,0},{24,8},{32,16},{40,24},{48,32},{56,40},{64,11... | collective-permute-start | bytes 393224 | tf_op jit(solution)/shard_map/ppermute | solution.py:27
  98.3 0.0 collective-permute-done.1
  98.3 1.4 collective-permute-start.6
  99.7 0.0 slice-done
  99.7 0.0 copy-done.3
  99.7 2.4 %fusion.17 = bf16[512,512]{0,1:T(8,128)(2,1)S(1)} fusion(f32[512,512]{1,0:T(8,128)S(1)} %fusion.2, bf16[512,4096]{1,0:T(8,128)(2,1)S(1)} %copy-done.3, f32[512,8,4,128]{3,2,1,0:T(4,128)S(1)} %bitcast.172), kind=kOutput, calls=%fused_computation.25 | convolution fusion | flops 2156396544 | bytes 14155776 | tf_op jit(solution)/shard_map/dot_general | solution.py:62
  102.1 0.1 reshape.303
  102.2 0.4 copy.16
  102.6 0.0 collective-permute-done.2
  102.6 0.0 collective-permute-done.3
  102.6 1.6 collective-permute-done.4
  104.2 3.7 %collective-permute-done.5 = bf16[4,128,128]{2,1,0:T(8,128)(2,1)} collective-permute-done((bf16[4,128,128]{2,1,0:T(8,128)(2,1)}, bf16[4,128,128]{2,1,0:T(8,128)(2,1)}, u32[]{:S(2)}, u32[]{:S(2)}) %collective-permute-start.5) | collective-permute-done | bytes 131104 | tf_op jit(solution)/shard_map/ppermute | solution.py:27
  108.0 1.6 collective-permute-done.6
  109.6 2.0 %convert_add_fusion = f32[4,128,128]{2,1,0:T(8,128)} fusion(bf16[4,128,128]{2,1,0:T(8,128)(2,1)} %collective-permute-done.6, bf16[4,128,128]{2,1,0:T(8,128)(2,1)} %collective-permute-done.5, bf16[4,128,128]{2,1,0:T(8,128)(2,1)} %collective-permute-done.4, bf16[4,128,128]{2,1,0:T(8,128)(2,1)} %collective-permute-done.3, ...), kind=kLoop, calls=%fused_computation.45 | loop fusion | flops 983040 | bytes 1310720 | tf_op jit(solution)/shard_map/add | solution.py:29
  111.6 1.5 collective-permute-start.7
  113.0 1.1 collective-permute-start.8
  114.2 2.1 %collective-permute-start.9 = (f32[4,128,128]{2,1,0:T(8,128)}, f32[4,128,128]{2,1,0:T(8,128)}, u32[]{:S(2)}, u32[]{:S(2)}) collective-permute-start(f32[4,128,128]{2,1,0:T(8,128)} %convert_add_fusion), channel_id=1, source_target_pairs={{0,192},{8,200},{16,208},{24,216},{32,224},{40,232},{48,240},{56,2... | collective-permute-start | bytes 786440 | tf_op jit(solution)/shard_map/ppermute | solution.py:27
  116.3 1.6 fusion.20
  117.9 3.0 %collective-permute-done.7 = f32[4,128,128]{2,1,0:T(8,128)S(1)} collective-permute-done((f32[4,128,128]{2,1,0:T(8,128)}, f32[4,128,128]{2,1,0:T(8,128)S(1)}, u32[]{:S(2)}, u32[]{:S(2)}) %collective-permute-start.7) | collective-permute-done | bytes 262176 | tf_op jit(solution)/shard_map/ppermute | solution.py:27
  120.9 3.0 %collective-permute-done.8 = f32[4,128,128]{2,1,0:T(8,128)S(1)} collective-permute-done((f32[4,128,128]{2,1,0:T(8,128)}, f32[4,128,128]{2,1,0:T(8,128)S(1)}, u32[]{:S(2)}, u32[]{:S(2)}) %collective-permute-start.8) | collective-permute-done | bytes 262176 | tf_op jit(solution)/shard_map/ppermute | solution.py:27
  123.9 3.1 %collective-permute-done.9 = f32[4,128,128]{2,1,0:T(8,128)} collective-permute-done((f32[4,128,128]{2,1,0:T(8,128)}, f32[4,128,128]{2,1,0:T(8,128)}, u32[]{:S(2)}, u32[]{:S(2)}) %collective-permute-start.9) | collective-permute-done | bytes 262176 | tf_op jit(solution)/shard_map/ppermute | solution.py:27
  127.0 1.3 fusion.47
  128.3 0.1 fusion.50
  128.4 0.1 fusion.27
  128.5 0.1 subtract_convert_fusion.6
  128.6 1.7 multiply_reduce_fusion
  130.4 0.0 copy-done.1
  130.4 0.2 multiply_convert_fusion
  130.6 0.3 copy.18
  130.9 6.5 %convolution_convert_fusion = bf16[512,4096]{1,0:T(8,128)(2,1)} fusion(bf16[512,4096]{1,0:T(8,128)(2,1)} %bitcast.173, bf16[64,8,4,128]{3,2,1,0:T(4,128)(2,1)S(1)} %bitcast.176), kind=kOutput, calls=%fused_computation.11 | convolution fusion | flops 2149580800 | bytes 8912896 | tf_op jit(solution)/shard_map/dot_general | solution.py:113
  137.4 0.0 reduce-scatter.2.cloned.1.call-update
  137.4 39.1 %reduce-scatter.2.cloned.1.call-done = bf16[512,512]{1,0:T(8,128)(2,1)} async-done(((bf16[512,4096]{1,0:T(8,128)(2,1)}), bf16[512,512]{1,0:T(8,128)(2,1)}) %reduce-scatter.2.cloned.1.call-update) | async-done | bytes 524304 | tf_op jit(solution)/shard_map/reduce_scatter | solution.py:114
  (7 shorter events, 0.0 us)
Async XLA Ops:
  6.5 40.1 %all-gather.2.cloned.1.call-start = ((), (), s32[]{:S(2)}) async-start(), calls=%async_computation.1 | async-start | bytes 4718592 | tf_op jit(solution)/shard_map/all_gather | solution.py:74
  7.3 169.2 %reduce-scatter.2.cloned.1.call-start = ((), (), s32[]{:S(2)}) async-start(), calls=%async_computation.2 | async-start | bytes 4718592 | tf_op jit(solution)/shard_map/reduce_scatter | solution.py:114
  8.2 13.7 %copy-start = (bf16[3,4,1024,128]{3,2,1,0:T(8,128)(2,1)S(1)}, bf16[3,4,1024,128]{3,2,1,0:T(8,128)(2,1)}, u32[]{:S(2)}) copy-start(bf16[3,4,1024,128]{3,2,1,0:T(8,128)(2,1)} %param.6) | copy-start | bytes 9437188
  46.7 11.5 %copy-start.2 = (bf16[512,4096]{1,0:T(8,128)(2,1)S(1)}, bf16[512,4096]{1,0:T(8,128)(2,1)}, u32[]{:S(2)}) copy-start(bf16[512,4096]{1,0:T(8,128)(2,1)} %all-gather.2.cloned.1.call-done) | copy-start | bytes 12582916
  74.6 25.1 %slice-start = ((s8[8388608]{0:T(1024)(128)(4,1)}), s8[4194304]{0:T(1024)(128)(4,1)S(1)}, s32[]{:S(2)}) async-start(s8[8388608]{0:T(1024)(128)(4,1)} %bitcast.170), calls=%async_computation.3 | async-start | bytes 8388608
  74.6 25.1 %copy-start.3 = (bf16[512,4096]{1,0:T(8,128)(2,1)S(1)}, bf16[512,4096]{1,0:T(8,128)(2,1)}, u32[]{:S(2)}) copy-start(bf16[512,4096]{1,0:T(8,128)(2,1)} %all-gather.2.cloned.1.call-done) | copy-start | bytes 12582916
  75.5 19.8 %collective-permute-start = (bf16[4,128,128]{2,1,0:T(8,128)(2,1)}, bf16[4,128,128]{2,1,0:T(8,128)(2,1)S(1)}, u32[]{:S(2)}, u32[]{:S(2)}) collective-permute-start(bf16[4,128,128]{2,1,0:T(8,128)(2,1)} %get-tuple-element.43), channel_id=1, source_target_pairs={{0,8},{8,16},{16,24},{24,32},{32,40},{40,48},{48,56},{56,0},{64,72... | collective-permute-start | bytes 393224 | tf_op jit(solution)/shard_map/ppermute | solution.py:27
  77.1 21.2 %collective-permute-start.1 = (bf16[4,128,128]{2,1,0:T(8,128)(2,1)}, bf16[4,128,128]{2,1,0:T(8,128)(2,1)S(1)}, u32[]{:S(2)}, u32[]{:S(2)}) collective-permute-start(bf16[4,128,128]{2,1,0:T(8,128)(2,1)} %get-tuple-element.43), channel_id=1, source_target_pairs={{0,16},{8,24},{16,32},{24,40},{32,48},{40,56},{48,0},{56,8},{64,80... | collective-permute-start | bytes 393224 | tf_op jit(solution)/shard_map/ppermute | solution.py:27
  79.6 23.0 %collective-permute-start.2 = (bf16[4,128,128]{2,1,0:T(8,128)(2,1)}, bf16[4,128,128]{2,1,0:T(8,128)(2,1)S(1)}, u32[]{:S(2)}, u32[]{:S(2)}) collective-permute-start(bf16[4,128,128]{2,1,0:T(8,128)(2,1)} %get-tuple-element.43), channel_id=1, source_target_pairs={{0,24},{8,32},{16,40},{24,48},{32,56},{40,0},{48,8},{56,16},{64,88... | collective-permute-start | bytes 393224 | tf_op jit(solution)/shard_map/ppermute | solution.py:27
  82.7 19.9 %collective-permute-start.3 = (bf16[4,128,128]{2,1,0:T(8,128)(2,1)}, bf16[4,128,128]{2,1,0:T(8,128)(2,1)}, u32[]{:S(2)}, u32[]{:S(2)}) collective-permute-start(bf16[4,128,128]{2,1,0:T(8,128)(2,1)} %get-tuple-element.43), channel_id=1, source_target_pairs={{0,32},{8,40},{16,48},{24,56},{32,0},{40,8},{48,16},{56,24},{64,96... | collective-permute-start | bytes 393224 | tf_op jit(solution)/shard_map/ppermute | solution.py:27
  84.6 19.7 %collective-permute-start.4 = (bf16[4,128,128]{2,1,0:T(8,128)(2,1)}, bf16[4,128,128]{2,1,0:T(8,128)(2,1)}, u32[]{:S(2)}, u32[]{:S(2)}) collective-permute-start(bf16[4,128,128]{2,1,0:T(8,128)(2,1)} %get-tuple-element.43), channel_id=1, source_target_pairs={{0,40},{8,48},{16,56},{24,0},{32,8},{40,16},{48,24},{56,32},{64,10... | collective-permute-start | bytes 393224 | tf_op jit(solution)/shard_map/ppermute | solution.py:27
  88.2 11.5 %slice-start.1 = ((s8[8388608]{0:T(1024)(128)(4,1)}), s8[4194304]{0:T(1024)(128)(4,1)S(1)}, s32[]{:S(2)}) async-start(s8[8388608]{0:T(1024)(128)(4,1)} %bitcast.170), calls=%async_computation.4 | async-start | bytes 8388608
  95.3 12.6 %collective-permute-start.5 = (bf16[4,128,128]{2,1,0:T(8,128)(2,1)}, bf16[4,128,128]{2,1,0:T(8,128)(2,1)}, u32[]{:S(2)}, u32[]{:S(2)}) collective-permute-start(bf16[4,128,128]{2,1,0:T(8,128)(2,1)} %get-tuple-element.43), channel_id=1, source_target_pairs={{0,48},{8,56},{16,0},{24,8},{32,16},{40,24},{48,32},{56,40},{64,11... | collective-permute-start | bytes 393224 | tf_op jit(solution)/shard_map/ppermute | solution.py:27
  98.3 11.3 %collective-permute-start.6 = (bf16[4,128,128]{2,1,0:T(8,128)(2,1)}, bf16[4,128,128]{2,1,0:T(8,128)(2,1)}, u32[]{:S(2)}, u32[]{:S(2)}) collective-permute-start(bf16[4,128,128]{2,1,0:T(8,128)(2,1)} %get-tuple-element.43), channel_id=1, source_target_pairs={{0,56},{8,0},{16,8},{24,16},{32,24},{40,32},{48,40},{56,48},{64,12... | collective-permute-start | bytes 393224 | tf_op jit(solution)/shard_map/ppermute | solution.py:27
  111.6 9.4 %collective-permute-start.7 = (f32[4,128,128]{2,1,0:T(8,128)}, f32[4,128,128]{2,1,0:T(8,128)S(1)}, u32[]{:S(2)}, u32[]{:S(2)}) collective-permute-start(f32[4,128,128]{2,1,0:T(8,128)} %convert_add_fusion), channel_id=1, source_target_pairs={{0,64},{8,72},{16,80},{24,88},{32,96},{40,104},{48,112},{56,120},{... | collective-permute-start | bytes 786440 | tf_op jit(solution)/shard_map/ppermute | solution.py:27
  113.0 10.9 %collective-permute-start.8 = (f32[4,128,128]{2,1,0:T(8,128)}, f32[4,128,128]{2,1,0:T(8,128)S(1)}, u32[]{:S(2)}, u32[]{:S(2)}) collective-permute-start(f32[4,128,128]{2,1,0:T(8,128)} %convert_add_fusion), channel_id=1, source_target_pairs={{0,128},{8,136},{16,144},{24,152},{32,160},{40,168},{48,176},{56,1... | collective-permute-start | bytes 786440 | tf_op jit(solution)/shard_map/ppermute | solution.py:27
  114.2 12.9 %collective-permute-start.9 = (f32[4,128,128]{2,1,0:T(8,128)}, f32[4,128,128]{2,1,0:T(8,128)}, u32[]{:S(2)}, u32[]{:S(2)}) collective-permute-start(f32[4,128,128]{2,1,0:T(8,128)} %convert_add_fusion), channel_id=1, source_target_pairs={{0,192},{8,200},{16,208},{24,216},{32,224},{40,232},{48,240},{56,2... | collective-permute-start | bytes 786440 | tf_op jit(solution)/shard_map/ppermute | solution.py:27
  117.9 12.4 %copy-start.1 = (f32[4,128]{1,0:T(4,128)S(1)}, f32[4,128]{1,0:T(4,128)}, u32[]{:S(2)}) copy-start(f32[4,128]{1,0:T(4,128)} %param.9) | copy-start | bytes 6148
Sparse Core Ops, SparseCore 0:
  9.2 37.4 all-gather.1
  137.5 38.8 reduce-scatter.1

commit v5 on v4

--- a/solution.py
+++ b/solution.py
@@ -51,24 +51,24 @@
     return folded.reshape(PHM * rows, PHM * cols)
 
 
-def split_bf16(value):
-    high = value.astype(jnp.bfloat16)
-    return high, (value - high.astype(jnp.float32)).astype(jnp.bfloat16)
-
-
-def project(whole, parts):
-    high, low = parts
-    out = jnp.dot(whole, high, preferred_element_type=jnp.float32)
-    out = out + jnp.dot(whole, low, preferred_element_type=jnp.float32)
-    return out.astype(jnp.bfloat16)
+def project(blocked, blocks, mixing, tok_rows):
+    projections, terms, rows, cols = blocks.shape
+    weights = jnp.transpose(blocks, (2, 0, 1, 3)).reshape(rows, projections * terms * cols)
+    product = jnp.dot(blocked, weights, preferred_element_type=jnp.float32)
+    product = product.reshape(tok_rows, PHM, projections, terms, cols)
+    outs = []
+    for p in range(projections):
+        summed = None
+        for term_index in range(terms):
+            for c in range(PHM):
+                part = product[:, c, p, term_index, None, :] * mixing[p, term_index, c][None, :, None]
+                summed = part if summed is None else summed + part
+        outs.append(summed.astype(jnp.bfloat16).reshape(tok_rows, PHM * cols))
+    return outs
 
 
 def on_device(ctx_devices, ctx_row, tokens, qkv_blocks, out_blocks, mix_factors, head_gain):
     col_width = qkv_blocks.shape[-1]
-    w_kv = split_bf16(
-        jnp.concatenate([fold_weights(qkv_blocks[p], mix_factors[p]) for p in (1, 2)], axis=1)
-    )
-    w_q = split_bf16(fold_weights(qkv_blocks[0], mix_factors[0]))
     w_out = fold_weights(out_blocks, mix_factors[3]).astype(jnp.bfloat16)
 
     whole = lax.all_gather(tokens, "tp", axis=1, tiled=True)
@@ -76,16 +76,17 @@
     local_heads = PHM * col_width // HEAD
     nblk = tok_rows // SPAN
     width = PHM * col_width
-    kv = project(whole, w_kv)
-    key_heads = kv[:, :width].reshape(nblk, SPAN, local_heads, HEAD)
-    value_heads = kv[:, width:].reshape(nblk, SPAN, local_heads, HEAD)
+    blocked = whole.reshape(tok_rows * PHM, BLOCK)
+    key, value = project(blocked, qkv_blocks[1:], mix_factors[1:3], tok_rows)
+    key_heads = key.reshape(nblk, SPAN, local_heads, HEAD)
+    value_heads = value.reshape(nblk, SPAN, local_heads, HEAD)
     states = jnp.einsum(
         "nshd,nshe->nhde", key_heads, value_heads, preferred_element_type=jnp.float32
     )
     totals = jnp.sum(states, axis=0)
     earlier_sum = exclusive_prefix(totals, "ctx", ctx_devices, ctx_row)
 
-    query = project(whole, w_q)
+    (query,) = project(blocked, qkv_blocks[:1], mix_factors[:1], tok_rows)
     query_heads = query.reshape(nblk, SPAN, local_heads, HEAD)
     scores = jnp.einsum(
         "nshd,nthd->nhst", query_heads, key_heads, preferred_element_type=jnp.float32

time: 184 us -> 180 us (0.978)
  matrix products: 47.5 us -> 17.9 us
  waiting for transfers between devices: 57.9 us -> 81 us
  local copies, waits for them, and re-layouts: 17.4 us -> 30.2 us
  other arithmetic: 25.2 us -> 14.3 us
    dot_general x4 -> x2, matrix products: 36.6 us -> 8.96 us  [project(): product = jnp.dot(blocked, weights, preferred_element_type=jnp.float32)]
    all_gather x1, waiting for transfers between devices: 2.05 us -> 22.1 us  [on_device(): whole = lax.all_gather(tokens, 'tp', axis=1, tiled=True)]
    mul x0 -> x19, local copies, waits for them, and re-layouts: none -> 15.6 us  [project(): product[:, c, p, term_index, None, :]]
    add x2 -> x0, other arithmetic: 13.7 us -> none  [fold_weights(): folded = part if folded is None else folded + part]
    convert_element_type x0 -> x3, other arithmetic: none -> 5.8 us  [project(): outs.append(summed.astype(jnp.bfloat16).reshape(tok_rows, PHM * cols))]
    ppermute x10, waiting for transfers between devices: 16 us -> 20.3 us  [ring_gather(): got = lax.ppermute(value, axis, pairs).astype(jnp.float32)]
    concatenate x1 -> x0, local copies, waits for them, and re-layouts: 4.27 us -> none  [on_device(): jnp.concatenate([fold_weights(qkv_blocks[p], mix_factors[p]) for p in (1,...]
    slice x1 -> x7, local copies, waits for them, and re-layouts: 0.07 us -> 3.61 us  [the longest x3 3.6 us: project(): product[:, c, p, term_index, None, :]]
  transfers between devices with their start and end apart: 12 -> 12, of which waited for: 8 -> 9; matrix products, arithmetic and copies ran while one was open for 27% -> 12% of each run, Pallas kernels for 0% -> 0%
where the time goes in v5:
time: 180 us
  waiting for transfers between devices  81 us (45%)
  local copies, waits for them, and re-layouts  30.2 us (17%)
  starting transfers between devices  22.1 us (12%)
  matrix products  17.9 us (10%)
  other arithmetic  14.3 us (8%)
  between operations  14.3 us (8%)
    reduce_scatter x1, waiting for transfers between devices, on_device(): lax.psum_scatter(partial_value.astype(jnp.bfloat16), 'tp', scatter_dimens...  38.6 us
    all_gather x1, waiting for transfers between devices, on_device(): whole = lax.all_gather(tokens, 'tp', axis=1, tiled=True)  22.1 us
    ppermute x10, starting transfers between devices, ring_gather(): got = lax.ppermute(value, axis, pairs).astype(jnp.float32)  22 us
    ppermute x10, waiting for transfers between devices, ring_gather(): got = lax.ppermute(value, axis, pairs).astype(jnp.float32)  20.3 us
    mul x19, local copies, waits for them, and re-layouts, project(): product[:, c, p, term_index, None, :]  15.6 us
    unnamed x74, local copies, waits for them, and re-layouts  10.6 us
    dot_general x2, matrix products, project(): product = jnp.dot(blocked, weights, preferred_element_type=jnp.float32)  8.96 us
    dot_general x1, matrix products, on_device(): partial_value = jnp.dot(attn, w_out, preferred_element_type=jnp.float32)  6.53 us
  transfers between devices with their start and end apart: 12, of which 9 were waited for; matrix products, arithmetic and copies ran while one was open for 12% of the time, Pallas kernels for 0%

profile of v5, /device:TPU:8, one launch (start us, length us, event | category | flops | bytes accessed | tf_op | source)
XLA Modules:
  0.0 179.8 jit_solution(1971253986834321097)
XLA Ops:
  6.5 2.2 %copy.24 = bf16[512,512]{0,1:T(8,128)(2,1)} copy(bf16[512,512]{1,0:T(8,128)(2,1)} %param.5) | data formatting | bytes 1048576 | tf_op args[0]
  8.7 0.0 all-gather.2.cloned.1.call-update
  8.8 0.0 reduce-scatter.2.cloned.1.call-start
  9.0 2.7 %copy.56 = bf16[2,4,1024,128]{2,3,1,0:T(8,128)(2,1)} copy(bf16[2,4,1024,128]{3,2,1,0:T(8,128)(2,1)S(1)} %slice-done) | data formatting | bytes 4194304
  11.7 1.3 copy.57
  13.0 1.4 bitcast_convert_fusion.3
  14.4 4.6 %add_convert_fusion = bf16[4,128,4,1024]{3,2,1,0:T(4,128)(2,1)S(1)} fusion(f32[128,1024]{1,0:T(8,128)S(1)} %get-tuple-element.59, f32[4,4]{1,0:T(4,128)S(1)} %get-tuple-element.111, f32[128,1024]{1,0:T(8,128)S(1)} %get-tuple-element.60, f32[4,4]{1,0:T(4,128)S(1)} %get-tuple-element.112, f32[128,1024]{1,0:T(8,128)S(1)} %get-tuple-element.58, ...), kind=kLoop, calls=%fused_computation | loop fusion | flops 16777216 | bytes 6291712 | tf_op jit(solution)/shard_map/convert_element_type | solution.py:72
  19.1 4.3 %copy.59 = bf16[64,8,4,1024]{3,1,2,0:T(8,128)(2,1)} copy(bf16[64,8,4,1024]{3,2,1,0:T(4,128)(2,1)S(1)} %bitcast.248) | data formatting | bytes 8388608
  23.4 0.6 slice_bitcast_fusion.22
  24.0 0.6 slice_bitcast_fusion.38
  24.6 22.1 %all-gather.2.cloned.1.call-done = bf16[512,4096]{0,1:T(8,128)(2,1)} async-done(((bf16[512,512]{0,1:T(8,128)(2,1)}), bf16[512,4096]{0,1:T(8,128)(2,1)}) %all-gather.2.cloned.1.call-update) | async-done | bytes 4194320 | tf_op jit(solution)/shard_map/all_gather | solution.py:74
  46.7 6.6 %fusion = f32[512,4,2,4,128]{4,0,3,2,1:T(8,128)S(1)} fusion(bf16[512,4,1024,1,1]{0,2,4,3,1:T(8,128)(2,1)} %bitcast.301, bf16[2,4,1024,128]{2,3,1,0:T(8,128)(2,1)S(1)} %copy-done), kind=kOutput, calls=%fused_computation.3 | convolution fusion | flops 4294967296 | bytes 14680064 | tf_op jit(solution)/shard_map/dot_general | solution.py:57
  53.2 1.4 fusion.33
  54.6 1.8 %fusion.34 = (f32[512,1,1,1,128]{4,0,3,2,1:T(8,128)}, f32[512,1,1,1,128]{4,0,3,2,1:T(8,128)}, f32[512,1,1,1,128]{4,0,3,2,1:T(8,128)}, f32[512,1,1,1,128]{4,0,3,2...) fusion(f32[512,4,2,4,128]{4,0,3,2,1:T(8,128)S(1)} %fusion), kind=kLoop, calls=%fused_computation.120 | loop fusion | bytes 6815744 | tf_op jit(solution)/shard_map/slice | solution.py:64
  56.5 0.1 copy.29
  56.6 0.1 copy.30
  56.7 0.1 copy.31
  56.9 1.1 copy.32
  58.0 1.8 copy.33
  59.7 1.8 %copy.34 = f32[4,128,128]{1,2,0:T(8,128)} copy(f32[4,128,128]{2,1,0:T(8,128)} %bitcast.281) | data formatting | bytes 524288 | tf_op jit(solution)/shard_map/mul | solution.py:64
  61.5 1.8 copy.35
  63.3 1.8 copy.36
  65.1 1.8 %copy.37 = f32[4,128,128]{1,2,0:T(8,128)} copy(f32[4,128,128]{2,1,0:T(8,128)} %bitcast.278) | data formatting | bytes 524288 | tf_op jit(solution)/shard_map/mul | solution.py:64
  66.9 1.8 %copy.38 = f32[4,128,128]{1,2,0:T(8,128)} copy(f32[4,128,128]{2,1,0:T(8,128)} %bitcast.277) | data formatting | bytes 524288 | tf_op jit(solution)/shard_map/mul | solution.py:64
  68.7 0.8 copy.39
  69.6 0.1 copy.40
  69.7 0.1 copy.41
  69.8 0.1 copy.42
  70.0 0.1 copy.43
  70.1 0.8 copy.44
  71.1 3.0 %add_convert_fusion.1 = bf16[4,128,4,128]{1,3,2,0:T(8,128)(2,1)S(1)} fusion(f32[4]{0:T(128)S(1)} %get-tuple-element.62, f32[4,128,128]{1,2,0:T(8,128)} %copy.44, f32[4]{0:T(128)S(1)} %get-tuple-element.63, f32[4,128,128]{1,2,0:T(8,128)S(1)} %copy.43, f32[4]{0:T(128)S(1)} %get-tuple-element.64, f32[4,128,128]{1,2,0:T(8,128)S(1)} %copy.42, ...), kind=kLoop, calls=%fused_computation.21 | loop fusion | flops 8388608 | bytes 4718848 | tf_op jit(solution)/shard_map/convert_element_type | solution.py:66
  74.2 1.4 add_convert_fusion.3
  75.6 0.3 fusion.36
  75.9 1.6 collective-permute-start
  77.6 2.5 %collective-permute-start.1 = (bf16[4,128,128]{2,1,0:T(8,128)(2,1)S(1)}, bf16[4,128,128]{2,1,0:T(8,128)(2,1)S(1)}, u32[]{:S(2)}, u32[]{:S(2)}) collective-permute-start(bf16[4,128,128]{2,1,0:T(8,128)(2,1)S(1)} %get-tuple-element.113), channel_id=1, source_target_pairs={{0,16},{8,24},{16,32},{24,40},{32,48},{40,56},{48,0},{56,8},{64,80... | collective-permute-start | bytes 393224 | tf_op jit(solution)/shard_map/ppermute | solution.py:27
  80.1 2.9 %collective-permute-start.2 = (bf16[4,128,128]{2,1,0:T(8,128)(2,1)S(1)}, bf16[4,128,128]{2,1,0:T(8,128)(2,1)S(1)}, u32[]{:S(2)}, u32[]{:S(2)}) collective-permute-start(bf16[4,128,128]{2,1,0:T(8,128)(2,1)S(1)} %get-tuple-element.113), channel_id=1, source_target_pairs={{0,24},{8,32},{16,40},{24,48},{32,56},{40,0},{48,8},{56,16},{64,88... | collective-permute-start | bytes 393224 | tf_op jit(solution)/shard_map/ppermute | solution.py:27
  83.1 2.0 %collective-permute-start.3 = (bf16[4,128,128]{2,1,0:T(8,128)(2,1)S(1)}, bf16[4,128,128]{2,1,0:T(8,128)(2,1)S(1)}, u32[]{:S(2)}, u32[]{:S(2)}) collective-permute-start(bf16[4,128,128]{2,1,0:T(8,128)(2,1)S(1)} %get-tuple-element.113), channel_id=1, source_target_pairs={{0,32},{8,40},{16,48},{24,56},{32,0},{40,8},{48,16},{56,24},{64,96... | collective-permute-start | bytes 393224 | tf_op jit(solution)/shard_map/ppermute | solution.py:27
  85.1 3.1 %collective-permute-start.4 = (bf16[4,128,128]{2,1,0:T(8,128)(2,1)S(1)}, bf16[4,128,128]{2,1,0:T(8,128)(2,1)S(1)}, u32[]{:S(2)}, u32[]{:S(2)}) collective-permute-start(bf16[4,128,128]{2,1,0:T(8,128)(2,1)S(1)} %get-tuple-element.113), channel_id=1, source_target_pairs={{0,40},{8,48},{16,56},{24,0},{32,8},{40,16},{48,24},{56,32},{64,10... | collective-permute-start | bytes 393224 | tf_op jit(solution)/shard_map/ppermute | solution.py:27
  88.2 2.4 %convolution_bitcast_fusion = f32[512,4,1,4,128]{4,0,3,1,2:T(8,128)S(1)} fusion(bf16[512,4,1024,1]{0,2,3,1:T(8,128)(2,1)S(1)} %bitcast.302, bf16[1,4,1024,128]{2,3,1,0:T(8,128)(2,1)S(1)} %copy-done.1), kind=kOutput, calls=%fused_computation.2 | convolution fusion | flops 2147483648 | bytes 9437184 | tf_op jit(solution)/shard_map/dot_general | solution.py:57
  90.8 0.4 fusion.35
  91.2 3.7 %collective-permute-start.5 = (bf16[4,128,128]{2,1,0:T(8,128)(2,1)S(1)}, bf16[4,128,128]{2,1,0:T(8,128)(2,1)S(1)}, u32[]{:S(2)}, u32[]{:S(2)}) collective-permute-start(bf16[4,128,128]{2,1,0:T(8,128)(2,1)S(1)} %get-tuple-element.113), channel_id=1, source_target_pairs={{0,48},{8,56},{16,0},{24,8},{32,16},{40,24},{48,32},{56,40},{64,11... | collective-permute-start | bytes 393224 | tf_op jit(solution)/shard_map/ppermute | solution.py:27
  94.9 1.4 collective-permute-start.6
  96.4 1.4 add_convert_fusion.2
  97.8 3.8 %collective-permute-done.3 = bf16[4,128,128]{2,1,0:T(8,128)(2,1)S(1)} collective-permute-done((bf16[4,128,128]{2,1,0:T(8,128)(2,1)S(1)}, bf16[4,128,128]{2,1,0:T(8,128)(2,1)S(1)}, u32[]{:S(2)}, u32[]{:S(2)}) %collective-permute-start.3) | collective-permute-done | bytes 131104 | tf_op jit(solution)/shard_map/ppermute | solution.py:27
  101.5 2.8 %collective-permute-done.4 = bf16[4,128,128]{2,1,0:T(8,128)(2,1)S(1)} collective-permute-done((bf16[4,128,128]{2,1,0:T(8,128)(2,1)S(1)}, bf16[4,128,128]{2,1,0:T(8,128)(2,1)S(1)}, u32[]{:S(2)}, u32[]{:S(2)}) %collective-permute-start.4) | collective-permute-done | bytes 131104 | tf_op jit(solution)/shard_map/ppermute | solution.py:27
  104.4 3.8 %collective-permute-done.5 = bf16[4,128,128]{2,1,0:T(8,128)(2,1)S(1)} collective-permute-done((bf16[4,128,128]{2,1,0:T(8,128)(2,1)S(1)}, bf16[4,128,128]{2,1,0:T(8,128)(2,1)S(1)}, u32[]{:S(2)}, u32[]{:S(2)}) %collective-permute-start.5) | collective-permute-done | bytes 131104 | tf_op jit(solution)/shard_map/ppermute | solution.py:27
  108.2 1.1 collective-permute-done.6
  109.3 0.8 convert_add_fusion
  110.1 1.5 collective-permute-start.7
  111.6 1.1 collective-permute-start.8
  112.7 2.1 %collective-permute-start.9 = (f32[4,128,128]{2,1,0:T(8,128)}, f32[4,128,128]{2,1,0:T(8,128)}, u32[]{:S(2)}, u32[]{:S(2)}) collective-permute-start(f32[4,128,128]{2,1,0:T(8,128)} %convert_add_fusion), channel_id=1, source_target_pairs={{0,192},{8,200},{16,208},{24,216},{32,224},{40,232},{48,240},{56,2... | collective-permute-start | bytes 786440 | tf_op jit(solution)/shard_map/ppermute | solution.py:27
  114.9 1.6 fusion.4
  116.5 3.1 %collective-permute-done.7 = f32[4,128,128]{2,1,0:T(8,128)} collective-permute-done((f32[4,128,128]{2,1,0:T(8,128)}, f32[4,128,128]{2,1,0:T(8,128)}, u32[]{:S(2)}, u32[]{:S(2)}) %collective-permute-start.7) | collective-permute-done | bytes 262176 | tf_op jit(solution)/shard_map/ppermute | solution.py:27
  119.6 3.0 %collective-permute-done.8 = f32[4,128,128]{2,1,0:T(8,128)} collective-permute-done((f32[4,128,128]{2,1,0:T(8,128)}, f32[4,128,128]{2,1,0:T(8,128)}, u32[]{:S(2)}, u32[]{:S(2)}) %collective-permute-start.8) | collective-permute-done | bytes 262176 | tf_op jit(solution)/shard_map/ppermute | solution.py:27
  122.6 2.7 %collective-permute-done.9 = f32[4,128,128]{2,1,0:T(8,128)} collective-permute-done((f32[4,128,128]{2,1,0:T(8,128)}, f32[4,128,128]{2,1,0:T(8,128)}, u32[]{:S(2)}, u32[]{:S(2)}) %collective-permute-start.9) | collective-permute-done | bytes 262176 | tf_op jit(solution)/shard_map/ppermute | solution.py:27
  125.3 1.2 fusion.28
  126.5 0.1 fusion.31
  126.5 0.1 fusion.12
  126.6 0.1 subtract_convert_fusion
  126.7 0.5 multiply_reduce_fusion
  127.3 0.2 multiply_convert_fusion
  127.5 0.3 copy.47
  127.8 6.5 %convolution_convert_fusion = bf16[512,4096]{1,0:T(8,128)(2,1)} fusion(bf16[512,4096]{1,0:T(8,128)(2,1)} %bitcast.249, bf16[64,8,4,128]{3,2,1,0:T(4,128)(2,1)S(1)} %bitcast.300), kind=kOutput, calls=%fused_computation.1 | convolution fusion | flops 2149580800 | bytes 8912896 | tf_op jit(solution)/shard_map/dot_general | solution.py:114
  134.3 38.6 %reduce-scatter.2.cloned.1.call-done = bf16[512,512]{1,0:T(8,128)(2,1)} async-done(((bf16[512,4096]{1,0:T(8,128)(2,1)}), bf16[512,512]{1,0:T(8,128)(2,1)}) %reduce-scatter.2.cloned.1.call-update) | async-done | bytes 524304 | tf_op jit(solution)/shard_map/reduce_scatter | solution.py:115
  (83 shorter events, 0.2 us)
Async XLA Ops:
  6.5 2.5 %slice-start = ((bf16[3,4,1024,128]{3,2,1,0:T(8,128)(2,1)}), bf16[2,4,1024,128]{3,2,1,0:T(8,128)(2,1)S(1)}, s32[]{:S(2)}) async-start(bf16[3,4,1024,128]{3,2,1,0:T(8,128)(2,1)} %param.6), calls=%async_computation.3 | async-start | bytes 4194304 | tf_op jit(solution)/shard_map/slice | solution.py:80
  6.5 40.1 %all-gather.2.cloned.1.call-start = ((), (), s32[]{:S(2)}) async-start(), calls=%async_computation.1 | async-start | bytes 4718592 | tf_op jit(solution)/shard_map/all_gather | solution.py:74
  8.8 164.2 %reduce-scatter.2.cloned.1.call-start = ((), (), s32[]{:S(2)}) async-start(), calls=%async_computation.2 | async-start | bytes 4718592 | tf_op jit(solution)/shard_map/reduce_scatter | solution.py:115
  9.0 2.7 %slice-start.1 = ((bf16[3,4,1024,128]{3,2,1,0:T(8,128)(2,1)}), bf16[1,4,1024,128]{3,2,1,0:T(8,128)(2,1)S(1)}, s32[]{:S(2)}) async-start(bf16[3,4,1024,128]{3,2,1,0:T(8,128)(2,1)} %param.6), calls=%async_computation.4 | async-start | bytes 2097152 | tf_op jit(solution)/shard_map/slice | solution.py:89
  9.0 4.0 %copy-start.16 = (f32[4,4,4,4]{3,2,1,0:T(4,128)S(1)}, f32[4,4,4,4]{3,2,1,0:T(4,128)}, u32[]{:S(2)}) copy-start(f32[4,4,4,4]{3,2,1,0:T(4,128)} %param.8) | copy-start | bytes 3076
  19.1 27.6 %copy-start = (bf16[2,4,1024,128]{2,3,1,0:T(8,128)(2,1)S(1)}, bf16[2,4,1024,128]{2,3,1,0:T(8,128)(2,1)}, u32[]{:S(2)}) copy-start(bf16[2,4,1024,128]{2,3,1,0:T(8,128)(2,1)} %copy.56) | copy-start | bytes 6291460
  71.0 3.2 %copy-start.3 = (f32[512,1,1,1,128]{4,0,3,2,1:T(8,128)S(1)}, f32[512,1,1,1,128]{4,0,3,2,1:T(8,128)}, u32[]{:S(2)}) copy-start(f32[512,1,1,1,128]{4,0,3,2,1:T(8,128)} %get-tuple-element.26) | copy-start | bytes 786436
  71.0 3.2 %copy-start.4 = (f32[512,1,1,1,128]{4,0,3,2,1:T(8,128)S(1)}, f32[512,1,1,1,128]{4,0,3,2,1:T(8,128)}, u32[]{:S(2)}) copy-start(f32[512,1,1,1,128]{4,0,3,2,1:T(8,128)} %get-tuple-element.27) | copy-start | bytes 786436
  71.0 3.2 %copy-start.5 = (f32[512,1,1,1,128]{4,0,3,2,1:T(8,128)S(1)}, f32[512,1,1,1,128]{4,0,3,2,1:T(8,128)}, u32[]{:S(2)}) copy-start(f32[512,1,1,1,128]{4,0,3,2,1:T(8,128)} %get-tuple-element.28) | copy-start | bytes 786436
  71.0 3.2 %copy-start.6 = (f32[512,1,1,1,128]{4,0,3,2,1:T(8,128)S(1)}, f32[512,1,1,1,128]{4,0,3,2,1:T(8,128)}, u32[]{:S(2)}) copy-start(f32[512,1,1,1,128]{4,0,3,2,1:T(8,128)} %get-tuple-element.29) | copy-start | bytes 786436
  71.0 3.2 %copy-start.7 = (f32[512,1,1,1,128]{4,0,3,2,1:T(8,128)S(1)}, f32[512,1,1,1,128]{4,0,3,2,1:T(8,128)}, u32[]{:S(2)}) copy-start(f32[512,1,1,1,128]{4,0,3,2,1:T(8,128)} %get-tuple-element.30) | copy-start | bytes 786436
  71.0 3.2 %copy-start.8 = (f32[512,1,1,1,128]{4,0,3,2,1:T(8,128)S(1)}, f32[512,1,1,1,128]{4,0,3,2,1:T(8,128)}, u32[]{:S(2)}) copy-start(f32[512,1,1,1,128]{4,0,3,2,1:T(8,128)} %get-tuple-element.31) | copy-start | bytes 786436
  71.0 3.2 %copy-start.9 = (f32[512,1,1,1,128]{4,0,3,2,1:T(8,128)S(1)}, f32[512,1,1,1,128]{4,0,3,2,1:T(8,128)}, u32[]{:S(2)}) copy-start(f32[512,1,1,1,128]{4,0,3,2,1:T(8,128)} %get-tuple-element.32) | copy-start | bytes 786436
  71.0 3.2 %copy-start.10 = (f32[512,1,1,1,128]{4,0,3,2,1:T(8,128)S(1)}, f32[512,1,1,1,128]{4,0,3,2,1:T(8,128)}, u32[]{:S(2)}) copy-start(f32[512,1,1,1,128]{4,0,3,2,1:T(8,128)} %get-tuple-element.33) | copy-start | bytes 786436
  71.0 3.2 %copy-start.11 = (f32[512,1,1,1,128]{4,0,3,2,1:T(8,128)S(1)}, f32[512,1,1,1,128]{4,0,3,2,1:T(8,128)}, u32[]{:S(2)}) copy-start(f32[512,1,1,1,128]{4,0,3,2,1:T(8,128)} %get-tuple-element.34) | copy-start | bytes 786436
  71.0 3.2 %copy-start.12 = (f32[512,1,1,1,128]{4,0,3,2,1:T(8,128)S(1)}, f32[512,1,1,1,128]{4,0,3,2,1:T(8,128)}, u32[]{:S(2)}) copy-start(f32[512,1,1,1,128]{4,0,3,2,1:T(8,128)} %get-tuple-element.35) | copy-start | bytes 786436
  71.0 3.2 %copy-start.13 = (f32[512,1,1,1,128]{4,0,3,2,1:T(8,128)S(1)}, f32[512,1,1,1,128]{4,0,3,2,1:T(8,128)}, u32[]{:S(2)}) copy-start(f32[512,1,1,1,128]{4,0,3,2,1:T(8,128)} %get-tuple-element.36) | copy-start | bytes 786436
  71.0 3.2 %copy-start.14 = (f32[512,1,1,1,128]{4,0,3,2,1:T(8,128)S(1)}, f32[512,1,1,1,128]{4,0,3,2,1:T(8,128)}, u32[]{:S(2)}) copy-start(f32[512,1,1,1,128]{4,0,3,2,1:T(8,128)} %get-tuple-element.37) | copy-start | bytes 786436
  71.0 3.2 %copy-start.15 = (f32[512,1,1,1,128]{4,0,3,2,1:T(8,128)S(1)}, f32[512,1,1,1,128]{4,0,3,2,1:T(8,128)}, u32[]{:S(2)}) copy-start(f32[512,1,1,1,128]{4,0,3,2,1:T(8,128)} %get-tuple-element.38) | copy-start | bytes 786436
  74.1 14.1 %copy-start.1 = (bf16[1,4,1024,128]{2,3,1,0:T(8,128)(2,1)S(1)}, bf16[1,4,1024,128]{2,3,1,0:T(8,128)(2,1)}, u32[]{:S(2)}) copy-start(bf16[1,4,1024,128]{2,3,1,0:T(8,128)(2,1)} %copy.57) | copy-start | bytes 3145732
  74.1 14.1 %copy-start.34 = (bf16[512,4096]{0,1:T(8,128)(2,1)S(1)}, bf16[512,4096]{0,1:T(8,128)(2,1)}, u32[]{:S(2)}) copy-start(bf16[512,4096]{0,1:T(8,128)(2,1)} %all-gather.2.cloned.1.call-done) | copy-start | bytes 12582916
  75.9 15.2 %collective-permute-start = (bf16[4,128,128]{2,1,0:T(8,128)(2,1)S(1)}, bf16[4,128,128]{2,1,0:T(8,128)(2,1)S(1)}, u32[]{:S(2)}, u32[]{:S(2)}) collective-permute-start(bf16[4,128,128]{2,1,0:T(8,128)(2,1)S(1)} %get-tuple-element.113), channel_id=1, source_target_pairs={{0,8},{8,16},{16,24},{24,32},{32,40},{40,48},{48,56},{56,0},{64,72... | collective-permute-start | bytes 393224 | tf_op jit(solution)/shard_map/ppermute | solution.py:27
  77.6 17.3 %collective-permute-start.1 = (bf16[4,128,128]{2,1,0:T(8,128)(2,1)S(1)}, bf16[4,128,128]{2,1,0:T(8,128)(2,1)S(1)}, u32[]{:S(2)}, u32[]{:S(2)}) collective-permute-start(bf16[4,128,128]{2,1,0:T(8,128)(2,1)S(1)} %get-tuple-element.113), channel_id=1, source_target_pairs={{0,16},{8,24},{16,32},{24,40},{32,48},{40,56},{48,0},{56,8},{64,80... | collective-permute-start | bytes 393224 | tf_op jit(solution)/shard_map/ppermute | solution.py:27
  80.1 17.6 %collective-permute-start.2 = (bf16[4,128,128]{2,1,0:T(8,128)(2,1)S(1)}, bf16[4,128,128]{2,1,0:T(8,128)(2,1)S(1)}, u32[]{:S(2)}, u32[]{:S(2)}) collective-permute-start(bf16[4,128,128]{2,1,0:T(8,128)(2,1)S(1)} %get-tuple-element.113), channel_id=1, source_target_pairs={{0,24},{8,32},{16,40},{24,48},{32,56},{40,0},{48,8},{56,16},{64,88... | collective-permute-start | bytes 393224 | tf_op jit(solution)/shard_map/ppermute | solution.py:27
  83.1 18.5 %collective-permute-start.3 = (bf16[4,128,128]{2,1,0:T(8,128)(2,1)S(1)}, bf16[4,128,128]{2,1,0:T(8,128)(2,1)S(1)}, u32[]{:S(2)}, u32[]{:S(2)}) collective-permute-start(bf16[4,128,128]{2,1,0:T(8,128)(2,1)S(1)} %get-tuple-element.113), channel_id=1, source_target_pairs={{0,32},{8,40},{16,48},{24,56},{32,0},{40,8},{48,16},{56,24},{64,96... | collective-permute-start | bytes 393224 | tf_op jit(solution)/shard_map/ppermute | solution.py:27
  85.1 19.3 %collective-permute-start.4 = (bf16[4,128,128]{2,1,0:T(8,128)(2,1)S(1)}, bf16[4,128,128]{2,1,0:T(8,128)(2,1)S(1)}, u32[]{:S(2)}, u32[]{:S(2)}) collective-permute-start(bf16[4,128,128]{2,1,0:T(8,128)(2,1)S(1)} %get-tuple-element.113), channel_id=1, source_target_pairs={{0,40},{8,48},{16,56},{24,0},{32,8},{40,16},{48,24},{56,32},{64,10... | collective-permute-start | bytes 393224 | tf_op jit(solution)/shard_map/ppermute | solution.py:27
  90.6 5.6 %copy-start.18 = (f32[4]{0:T(128)S(1)}, f32[4]{0:T(128)}, u32[]{:S(2)}) copy-start(f32[4]{0:T(128)} %get-tuple-element.77) | copy-start | bytes 52
  90.6 5.6 %copy-start.19 = (f32[4]{0:T(128)S(1)}, f32[4]{0:T(128)}, u32[]{:S(2)}) copy-start(f32[4]{0:T(128)} %get-tuple-element.78) | copy-start | bytes 52
  90.6 5.6 %copy-start.20 = (f32[4]{0:T(128)S(1)}, f32[4]{0:T(128)}, u32[]{:S(2)}) copy-start(f32[4]{0:T(128)} %get-tuple-element.79) | copy-start | bytes 52
  90.7 5.6 %copy-start.21 = (f32[4]{0:T(128)S(1)}, f32[4]{0:T(128)}, u32[]{:S(2)}) copy-start(f32[4]{0:T(128)} %get-tuple-element.80) | copy-start | bytes 52
  90.7 5.6 %copy-start.22 = (f32[4]{0:T(128)S(1)}, f32[4]{0:T(128)}, u32[]{:S(2)}) copy-start(f32[4]{0:T(128)} %get-tuple-element.81) | copy-start | bytes 52
  90.7 5.6 %copy-start.23 = (f32[4]{0:T(128)S(1)}, f32[4]{0:T(128)}, u32[]{:S(2)}) copy-start(f32[4]{0:T(128)} %get-tuple-element.82) | copy-start | bytes 52
  90.7 5.6 %copy-start.24 = (f32[4]{0:T(128)S(1)}, f32[4]{0:T(128)}, u32[]{:S(2)}) copy-start(f32[4]{0:T(128)} %get-tuple-element.83) | copy-start | bytes 52
  90.7 5.6 %copy-start.25 = (f32[4]{0:T(128)S(1)}, f32[4]{0:T(128)}, u32[]{:S(2)}) copy-start(f32[4]{0:T(128)} %get-tuple-element.84) | copy-start | bytes 52
  90.7 5.6 %copy-start.26 = (f32[4]{0:T(128)S(1)}, f32[4]{0:T(128)}, u32[]{:S(2)}) copy-start(f32[4]{0:T(128)} %get-tuple-element.85) | copy-start | bytes 52
  90.7 5.6 %copy-start.27 = (f32[4]{0:T(128)S(1)}, f32[4]{0:T(128)}, u32[]{:S(2)}) copy-start(f32[4]{0:T(128)} %get-tuple-element.86) | copy-start | bytes 52
  90.7 5.6 %copy-start.28 = (f32[4]{0:T(128)S(1)}, f32[4]{0:T(128)}, u32[]{:S(2)}) copy-start(f32[4]{0:T(128)} %get-tuple-element.87) | copy-start | bytes 52
  90.7 5.6 %copy-start.29 = (f32[4]{0:T(128)S(1)}, f32[4]{0:T(128)}, u32[]{:S(2)}) copy-start(f32[4]{0:T(128)} %get-tuple-element.88) | copy-start | bytes 52
  90.7 5.6 %copy-start.30 = (f32[4]{0:T(128)S(1)}, f32[4]{0:T(128)}, u32[]{:S(2)}) copy-start(f32[4]{0:T(128)} %get-tuple-element.89) | copy-start | bytes 52
  90.8 5.6 %copy-start.31 = (f32[4]{0:T(128)S(1)}, f32[4]{0:T(128)}, u32[]{:S(2)}) copy-start(f32[4]{0:T(128)} %get-tuple-element.90) | copy-start | bytes 52
  90.8 5.6 %copy-start.32 = (f32[4]{0:T(128)S(1)}, f32[4]{0:T(128)}, u32[]{:S(2)}) copy-start(f32[4]{0:T(128)} %get-tuple-element.91) | copy-start | bytes 52
  90.8 5.6 %copy-start.33 = (f32[4]{0:T(128)S(1)}, f32[4]{0:T(128)}, u32[]{:S(2)}) copy-start(f32[4]{0:T(128)} %get-tuple-element.92) | copy-start | bytes 52
  91.2 17.0 %collective-permute-start.5 = (bf16[4,128,128]{2,1,0:T(8,128)(2,1)S(1)}, bf16[4,128,128]{2,1,0:T(8,128)(2,1)S(1)}, u32[]{:S(2)}, u32[]{:S(2)}) collective-permute-start(bf16[4,128,128]{2,1,0:T(8,128)(2,1)S(1)} %get-tuple-element.113), channel_id=1, source_target_pairs={{0,48},{8,56},{16,0},{24,8},{32,16},{40,24},{48,32},{56,40},{64,11... | collective-permute-start | bytes 393224 | tf_op jit(solution)/shard_map/ppermute | solution.py:27
  94.9 14.4 %collective-permute-start.6 = (bf16[4,128,128]{2,1,0:T(8,128)(2,1)S(1)}, bf16[4,128,128]{2,1,0:T(8,128)(2,1)S(1)}, u32[]{:S(2)}, u32[]{:S(2)}) collective-permute-start(bf16[4,128,128]{2,1,0:T(8,128)(2,1)S(1)} %get-tuple-element.113), channel_id=1, source_target_pairs={{0,56},{8,0},{16,8},{24,16},{32,24},{40,32},{48,40},{56,48},{64,12... | collective-permute-start | bytes 393224 | tf_op jit(solution)/shard_map/ppermute | solution.py:27
  110.1 9.5 %collective-permute-start.7 = (f32[4,128,128]{2,1,0:T(8,128)}, f32[4,128,128]{2,1,0:T(8,128)}, u32[]{:S(2)}, u32[]{:S(2)}) collective-permute-start(f32[4,128,128]{2,1,0:T(8,128)} %convert_add_fusion), channel_id=1, source_target_pairs={{0,64},{8,72},{16,80},{24,88},{32,96},{40,104},{48,112},{56,120},{... | collective-permute-start | bytes 786440 | tf_op jit(solution)/shard_map/ppermute | solution.py:27
  111.6 11.0 %collective-permute-start.8 = (f32[4,128,128]{2,1,0:T(8,128)}, f32[4,128,128]{2,1,0:T(8,128)}, u32[]{:S(2)}, u32[]{:S(2)}) collective-permute-start(f32[4,128,128]{2,1,0:T(8,128)} %convert_add_fusion), channel_id=1, source_target_pairs={{0,128},{8,136},{16,144},{24,152},{32,160},{40,168},{48,176},{56,1... | collective-permute-start | bytes 786440 | tf_op jit(solution)/shard_map/ppermute | solution.py:27
  112.7 12.5 %collective-permute-start.9 = (f32[4,128,128]{2,1,0:T(8,128)}, f32[4,128,128]{2,1,0:T(8,128)}, u32[]{:S(2)}, u32[]{:S(2)}) collective-permute-start(f32[4,128,128]{2,1,0:T(8,128)} %convert_add_fusion), channel_id=1, source_target_pairs={{0,192},{8,200},{16,208},{24,216},{32,224},{40,232},{48,240},{56,2... | collective-permute-start | bytes 786440 | tf_op jit(solution)/shard_map/ppermute | solution.py:27
  116.5 10.3 %copy-start.2 = (f32[4,4,128,128]{3,2,1,0:T(8,128)S(1)}, f32[4,4,128,128]{3,2,1,0:T(8,128)}, u32[]{:S(2)}) copy-start(f32[4,4,128,128]{3,2,1,0:T(8,128)} %fusion.4) | copy-start | bytes 3145732
  126.5 0.8 copy-start.17
Sparse Core Ops, SparseCore 0:
  9.2 37.4 all-gather.1
  134.5 38.4 reduce-scatter.1

commit v6 on v5

--- a/solution.py
+++ b/solution.py
@@ -51,17 +51,21 @@
     return folded.reshape(PHM * rows, PHM * cols)
 
 
-def project(blocked, blocks, mixing, tok_rows):
+def project(whole, blocks, mixing):
     projections, terms, rows, cols = blocks.shape
+    tok_rows = whole.shape[0]
     weights = jnp.transpose(blocks, (2, 0, 1, 3)).reshape(rows, projections * terms * cols)
-    product = jnp.dot(blocked, weights, preferred_element_type=jnp.float32)
-    product = product.reshape(tok_rows, PHM, projections, terms, cols)
+    products = [
+        jnp.dot(whole[:, c * rows:(c + 1) * rows], weights, preferred_element_type=jnp.float32)
+        for c in range(PHM)
+    ]
     outs = []
     for p in range(projections):
         summed = None
         for term_index in range(terms):
+            at = (p * terms + term_index) * cols
             for c in range(PHM):
-                part = product[:, c, p, term_index, None, :] * mixing[p, term_index, c][None, :, None]
+                part = products[c][:, None, at:at + cols] * mixing[p, term_index, c][None, :, None]
                 summed = part if summed is None else summed + part
         outs.append(summed.astype(jnp.bfloat16).reshape(tok_rows, PHM * cols))
     return outs
@@ -76,8 +80,7 @@
     local_heads = PHM * col_width // HEAD
     nblk = tok_rows // SPAN
     width = PHM * col_width
-    blocked = whole.reshape(tok_rows * PHM, BLOCK)
-    key, value = project(blocked, qkv_blocks[1:], mix_factors[1:3], tok_rows)
+    key, value = project(whole, qkv_blocks[1:], mix_factors[1:3])
     key_heads = key.reshape(nblk, SPAN, local_heads, HEAD)
     value_heads = value.reshape(nblk, SPAN, local_heads, HEAD)
     states = jnp.einsum(
@@ -86,7 +89,7 @@
     totals = jnp.sum(states, axis=0)
     earlier_sum = exclusive_prefix(totals, "ctx", ctx_devices, ctx_row)
 
-    (query,) = project(blocked, qkv_blocks[:1], mix_factors[:1], tok_rows)
+    (query,) = project(whole, qkv_blocks[:1], mix_factors[:1])
     query_heads = query.reshape(nblk, SPAN, local_heads, HEAD)
     scores = jnp.einsum(
         "nshd,nthd->nhst", query_heads, key_heads, preferred_element_type=jnp.float32

time: 180 us -> 195 us (1.083)
  local copies, waits for them, and re-layouts: 30.2 us -> 37.8 us
  matrix products: 17.9 us -> 21.9 us
  other arithmetic: 14.3 us -> 16.6 us
    mul x19, local copies, waits for them, and re-layouts: 15.6 us -> 23.3 us  [project(): products[c][:, None, at:at + cols] * mixing[p, term_index, c][None, :, None]]
    dot_general x2 -> x8, matrix products: 8.96 us -> 13 us  [project(): jnp.dot(whole[:, c * rows:(c + 1) * rows], weights, preferred_element_typ...]
    unnamed x74 -> x69, local copies, waits for them, and re-layouts: 10.6 us -> 8.43 us
    slice x7 -> x12, local copies, waits for them, and re-layouts: 3.61 us -> 5.76 us  [the longest x8 5.14 us: project(): products[c][:, None, at:at + cols] * mixing[p, term_index, c][None, :, None]]
    convert_element_type x3, other arithmetic: 5.8 us -> 7.91 us  [project(): outs.append(summed.astype(jnp.bfloat16).reshape(tok_rows, PHM * cols))]
  transfers between devices with their start and end apart: 12 -> 12, of which waited for: 9 -> 9; matrix products, arithmetic and copies ran while one was open for 12% -> 11% of each run, Pallas kernels for 0% -> 0%
where the time goes in v6:
time: 195 us; the launch traced here: 194 us
  waiting for transfers between devices  82 us (42%)
  local copies, waits for them, and re-layouts  37.8 us (19%)
  starting transfers between devices  21.9 us (11%)
  matrix products  21.9 us (11%)
  other arithmetic  16.6 us (9%)
  between operations  14.2 us (7%)
    reduce_scatter x1, waiting for transfers between devices, on_device(): lax.psum_scatter(partial_value.astype(jnp.bfloat16), 'tp', scatter_dimens...  38.5 us
    mul x19, local copies, waits for them, and re-layouts, project(): products[c][:, None, at:at + cols] * mixing[p, term_index, c][None, :, None]  23.3 us
    all_gather x1, waiting for transfers between devices, on_device(): whole = lax.all_gather(tokens, 'tp', axis=1, tiled=True)  22.7 us
    ppermute x10, starting transfers between devices, ring_gather(): got = lax.ppermute(value, axis, pairs).astype(jnp.float32)  21.8 us
    ppermute x10, waiting for transfers between devices, ring_gather(): got = lax.ppermute(value, axis, pairs).astype(jnp.float32)  20 us
    dot_general x8, matrix products, project(): jnp.dot(whole[:, c * rows:(c + 1) * rows], weights, preferred_element_typ...  13 us
    unnamed x69, local copies, waits for them, and re-layouts  8.43 us
    convert_element_type x3, other arithmetic, project(): outs.append(summed.astype(jnp.bfloat16).reshape(tok_rows, PHM * cols))  7.91 us
  transfers between devices with their start and end apart: 12, of which 9 were waited for; matrix products, arithmetic and copies ran while one was open for 11% of the time, Pallas kernels for 0%

profile of v6, /device:TPU:8, one launch (start us, length us, event | category | flops | bytes accessed | tf_op | source)
XLA Modules:
  0.0 194.4 jit_solution(4068808935251880692)
XLA Ops:
  6.5 0.7 all-gather.2.cloned.1.call-update
  7.5 0.6 slice-done
  8.1 2.7 %copy.47 = bf16[2,4,1024,128]{2,3,1,0:T(8,128)(2,1)} copy(bf16[2,4,1024,128]{3,2,1,0:T(8,128)(2,1)S(1)} %slice-done) | data formatting | bytes 4194304
  10.8 1.3 copy.48
  12.1 1.4 bitcast_convert_fusion.3
  13.5 4.8 %add_convert_fusion = bf16[4,128,4,1024]{3,2,1,0:T(4,128)(2,1)S(1)} fusion(f32[128,1024]{1,0:T(8,128)S(1)} %get-tuple-element.59, f32[4,4]{1,0:T(4,128)S(1)} %get-tuple-element.111, f32[128,1024]{1,0:T(8,128)S(1)} %get-tuple-element.60, f32[4,4]{1,0:T(4,128)S(1)} %get-tuple-element.112, f32[128,1024]{1,0:T(8,128)S(1)} %get-tuple-element.58, ...), kind=kLoop, calls=%fused_computation | loop fusion | flops 16777216 | bytes 6291712 | tf_op jit(solution)/shard_map/convert_element_type | solution.py:76
  18.4 4.3 %copy.50 = bf16[64,8,4,1024]{3,1,2,0:T(8,128)(2,1)} copy(bf16[64,8,4,1024]{3,2,1,0:T(4,128)(2,1)S(1)} %bitcast.227) | data formatting | bytes 8388608
  22.7 0.6 slice_bitcast_fusion.22
  23.3 0.6 slice_bitcast_fusion.38
  23.9 22.7 %all-gather.2.cloned.1.call-done = bf16[512,4096]{1,0:T(8,128)(2,1)} async-done(((bf16[512,512]{1,0:T(8,128)(2,1)}), bf16[512,4096]{1,0:T(8,128)(2,1)}) %all-gather.2.cloned.1.call-update) | async-done | bytes 4194320 | tf_op jit(solution)/shard_map/all_gather | solution.py:78
  46.7 2.5 %fusion.23 = f32[512,1024]{1,0:T(8,128)S(1)} fusion(bf16[1024,1024]{0,1:T(8,128)(2,1)S(1)} %bitcast.231, bf16[512,4096]{1,0:T(8,128)(2,1)} %all-gather.2.cloned.1.call-done), kind=kOutput, calls=%fused_computation.34 | convolution fusion | flops 1073741824 | bytes 5242880 | tf_op jit(solution)/shard_map/dot_general | solution.py:59
  49.2 1.0 fusion.46
  50.1 0.8 copy.26
  51.0 2.5 %fusion.19 = f32[512,1024]{1,0:T(8,128)S(1)} fusion(bf16[1024,1024]{0,1:T(8,128)(2,1)S(1)} %bitcast.232, bf16[512,4096]{1,0:T(8,128)(2,1)} %all-gather.2.cloned.1.call-done), kind=kOutput, calls=%fused_computation.30 | convolution fusion | flops 1073741824 | bytes 5242880 | tf_op jit(solution)/shard_map/dot_general | solution.py:59
  53.5 1.3 fusion.47
  54.8 1.8 copy.27
  56.5 2.5 %fusion.15 = f32[512,1024]{1,0:T(8,128)S(1)} fusion(bf16[1024,1024]{0,1:T(8,128)(2,1)S(1)} %bitcast.233, bf16[512,4096]{1,0:T(8,128)(2,1)} %all-gather.2.cloned.1.call-done), kind=kOutput, calls=%fused_computation.26 | convolution fusion | flops 1073741824 | bytes 5242880 | tf_op jit(solution)/shard_map/dot_general | solution.py:59
  59.0 1.4 fusion.48
  60.4 1.8 copy.28
  62.2 2.5 %fusion.11 = f32[512,1024]{1,0:T(8,128)S(1)} fusion(bf16[1024,1024]{0,1:T(8,128)(2,1)S(1)} %bitcast.234, bf16[512,4096]{1,0:T(8,128)(2,1)} %all-gather.2.cloned.1.call-done), kind=kOutput, calls=%fused_computation.22 | convolution fusion | flops 1073741824 | bytes 5242880 | tf_op jit(solution)/shard_map/dot_general | solution.py:59
  64.8 1.3 fusion.49
  66.0 1.9 copy.29
  67.9 0.8 copy.30
  68.7 0.8 copy.31
  69.6 0.8 copy.32
  70.4 0.8 copy.33
  71.2 0.8 copy.34
  72.1 1.9 copy.35
  74.0 1.8 copy.36
  75.7 1.8 copy.37
  77.5 0.8 copy.38
  78.4 1.8 copy.39
  80.2 1.8 copy.40
  81.9 1.8 copy.41
  83.7 3.3 %add_convert_fusion.1 = bf16[4,128,4,128]{1,3,2,0:T(8,128)(2,1)S(1)} fusion(f32[4]{0:T(128)S(1)} %get-tuple-element.62, f32[4,128,128]{1,2,0:T(8,128)} %copy.41, f32[4]{0:T(128)S(1)} %get-tuple-element.63, f32[4,128,128]{1,2,0:T(8,128)} %copy.40, f32[4]{0:T(128)S(1)} %get-tuple-element.64, f32[4,128,128]{1,2,0:T(8,128)} %copy.39, ...), kind=kLoop, calls=%fused_computation.17 | loop fusion | flops 8388608 | bytes 4718848 | tf_op jit(solution)/shard_map/convert_element_type | solution.py:70
  87.1 3.2 %add_convert_fusion.3 = bf16[4,128,4,128]{3,1,2,0:T(8,128)(2,1)S(1)} fusion(f32[4]{0:T(128)S(1)} %get-tuple-element.93, f32[4,128,128]{2,1,0:T(8,128)} %bitcast.247, f32[4]{0:T(128)S(1)} %get-tuple-element.94, f32[4,128,128]{2,1,0:T(8,128)S(1)} %bitcast.243, f32[4]{0:T(128)S(1)} %get-tuple-element.95, f32[4,128,128]{2,1,0:T(8,128)S(1)} %bitcast.239, ...), kind=kLoop, calls=%fused_computation.19 | loop fusion | flops 8388608 | bytes 4718848 | tf_op jit(solution)/shard_map/convert_element_type | solution.py:70
  90.6 1.6 collective-permute-start
  92.2 2.5 %collective-permute-start.1 = (bf16[4,128,128]{2,1,0:T(8,128)(2,1)S(1)}, bf16[4,128,128]{2,1,0:T(8,128)(2,1)S(1)}, u32[]{:S(2)}, u32[]{:S(2)}) collective-permute-start(bf16[4,128,128]{2,1,0:T(8,128)(2,1)S(1)} %get-tuple-element.113), channel_id=1, source_target_pairs={{0,16},{8,24},{16,32},{24,40},{32,48},{40,56},{48,0},{56,8},{64,80... | collective-permute-start | bytes 393224 | tf_op jit(solution)/shard_map/ppermute | solution.py:27
  94.8 2.9 %collective-permute-start.2 = (bf16[4,128,128]{2,1,0:T(8,128)(2,1)S(1)}, bf16[4,128,128]{2,1,0:T(8,128)(2,1)S(1)}, u32[]{:S(2)}, u32[]{:S(2)}) collective-permute-start(bf16[4,128,128]{2,1,0:T(8,128)(2,1)S(1)} %get-tuple-element.113), channel_id=1, source_target_pairs={{0,24},{8,32},{16,40},{24,48},{32,56},{40,0},{48,8},{56,16},{64,88... | collective-permute-start | bytes 393224 | tf_op jit(solution)/shard_map/ppermute | solution.py:27
  97.7 2.0 %collective-permute-start.3 = (bf16[4,128,128]{2,1,0:T(8,128)(2,1)S(1)}, bf16[4,128,128]{2,1,0:T(8,128)(2,1)S(1)}, u32[]{:S(2)}, u32[]{:S(2)}) collective-permute-start(bf16[4,128,128]{2,1,0:T(8,128)(2,1)S(1)} %get-tuple-element.113), channel_id=1, source_target_pairs={{0,32},{8,40},{16,48},{24,56},{32,0},{40,8},{48,16},{56,24},{64,96... | collective-permute-start | bytes 393224 | tf_op jit(solution)/shard_map/ppermute | solution.py:27
  99.7 3.1 %collective-permute-start.4 = (bf16[4,128,128]{2,1,0:T(8,128)(2,1)S(1)}, bf16[4,128,128]{2,1,0:T(8,128)(2,1)S(1)}, u32[]{:S(2)}, u32[]{:S(2)}) collective-permute-start(bf16[4,128,128]{2,1,0:T(8,128)(2,1)S(1)} %get-tuple-element.113), channel_id=1, source_target_pairs={{0,40},{8,48},{16,56},{24,0},{32,8},{40,16},{48,24},{56,32},{64,10... | collective-permute-start | bytes 393224 | tf_op jit(solution)/shard_map/ppermute | solution.py:27
  102.8 0.7 fusion.21
  103.7 0.7 fusion.17
  104.5 0.7 fusion.13
  105.5 0.7 fusion.9
  106.3 3.5 %collective-permute-start.5 = (bf16[4,128,128]{2,1,0:T(8,128)(2,1)S(1)}, bf16[4,128,128]{2,1,0:T(8,128)(2,1)S(1)}, u32[]{:S(2)}, u32[]{:S(2)}) collective-permute-start(bf16[4,128,128]{2,1,0:T(8,128)(2,1)S(1)} %get-tuple-element.113), channel_id=1, source_target_pairs={{0,48},{8,56},{16,0},{24,8},{32,16},{40,24},{48,32},{56,40},{64,11... | collective-permute-start | bytes 393224 | tf_op jit(solution)/shard_map/ppermute | solution.py:27
  109.8 1.4 collective-permute-start.6
  111.3 1.4 add_convert_fusion.2
  112.7 3.5 %collective-permute-done.3 = bf16[4,128,128]{2,1,0:T(8,128)(2,1)S(1)} collective-permute-done((bf16[4,128,128]{2,1,0:T(8,128)(2,1)S(1)}, bf16[4,128,128]{2,1,0:T(8,128)(2,1)S(1)}, u32[]{:S(2)}, u32[]{:S(2)}) %collective-permute-start.3) | collective-permute-done | bytes 131104 | tf_op jit(solution)/shard_map/ppermute | solution.py:27
  116.2 2.8 %collective-permute-done.4 = bf16[4,128,128]{2,1,0:T(8,128)(2,1)S(1)} collective-permute-done((bf16[4,128,128]{2,1,0:T(8,128)(2,1)S(1)}, bf16[4,128,128]{2,1,0:T(8,128)(2,1)S(1)}, u32[]{:S(2)}, u32[]{:S(2)}) %collective-permute-start.4) | collective-permute-done | bytes 131104 | tf_op jit(solution)/shard_map/ppermute | solution.py:27
  119.0 3.8 %collective-permute-done.5 = bf16[4,128,128]{2,1,0:T(8,128)(2,1)S(1)} collective-permute-done((bf16[4,128,128]{2,1,0:T(8,128)(2,1)S(1)}, bf16[4,128,128]{2,1,0:T(8,128)(2,1)S(1)}, u32[]{:S(2)}, u32[]{:S(2)}) %collective-permute-start.5) | collective-permute-done | bytes 131104 | tf_op jit(solution)/shard_map/ppermute | solution.py:27
  122.8 1.1 collective-permute-done.6
  123.9 0.8 convert_add_fusion
  124.8 1.5 collective-permute-start.7
  126.2 1.1 collective-permute-start.8
  127.4 2.1 %collective-permute-start.9 = (f32[4,128,128]{2,1,0:T(8,128)}, f32[4,128,128]{2,1,0:T(8,128)}, u32[]{:S(2)}, u32[]{:S(2)}) collective-permute-start(f32[4,128,128]{2,1,0:T(8,128)} %convert_add_fusion), channel_id=1, source_target_pairs={{0,192},{8,200},{16,208},{24,216},{32,224},{40,232},{48,240},{56,2... | collective-permute-start | bytes 786440 | tf_op jit(solution)/shard_map/ppermute | solution.py:27
  129.5 1.6 fusion.2
  131.1 3.1 %collective-permute-done.7 = f32[4,128,128]{2,1,0:T(8,128)} collective-permute-done((f32[4,128,128]{2,1,0:T(8,128)}, f32[4,128,128]{2,1,0:T(8,128)}, u32[]{:S(2)}, u32[]{:S(2)}) %collective-permute-start.7) | collective-permute-done | bytes 262176 | tf_op jit(solution)/shard_map/ppermute | solution.py:27
  134.2 3.0 %collective-permute-done.8 = f32[4,128,128]{2,1,0:T(8,128)} collective-permute-done((f32[4,128,128]{2,1,0:T(8,128)}, f32[4,128,128]{2,1,0:T(8,128)}, u32[]{:S(2)}, u32[]{:S(2)}) %collective-permute-start.8) | collective-permute-done | bytes 262176 | tf_op jit(solution)/shard_map/ppermute | solution.py:27
  137.2 2.7 %collective-permute-done.9 = f32[4,128,128]{2,1,0:T(8,128)} collective-permute-done((f32[4,128,128]{2,1,0:T(8,128)}, f32[4,128,128]{2,1,0:T(8,128)}, u32[]{:S(2)}, u32[]{:S(2)}) %collective-permute-start.9) | collective-permute-done | bytes 262176 | tf_op jit(solution)/shard_map/ppermute | solution.py:27
  140.0 1.2 fusion.41
  141.4 0.5 multiply_reduce_fusion
  142.5 6.5 %convolution_convert_fusion = bf16[512,4096]{1,0:T(8,128)(2,1)} fusion(bf16[512,4096]{1,0:T(8,128)(2,1)} %bitcast.228, bf16[64,8,4,128]{3,2,1,0:T(4,128)(2,1)S(1)} %bitcast.287), kind=kOutput, calls=%fused_computation.1 | convolution fusion | flops 2149580800 | bytes 8912896 | tf_op jit(solution)/shard_map/dot_general | solution.py:117
  149.1 38.5 %reduce-scatter.2.cloned.1.call-done = bf16[512,512]{1,0:T(8,128)(2,1)} async-done(((bf16[512,4096]{1,0:T(8,128)(2,1)}), bf16[512,512]{1,0:T(8,128)(2,1)}) %reduce-scatter.2.cloned.1.call-update) | async-done | bytes 524304 | tf_op jit(solution)/shard_map/reduce_scatter | solution.py:118
  (89 shorter events, 1.6 us)
Async XLA Ops:
  6.5 1.6 slice-start
  6.5 40.1 %all-gather.2.cloned.1.call-start = ((), (), s32[]{:S(2)}) async-start(), calls=%async_computation.1 | async-start | bytes 4718592 | tf_op jit(solution)/shard_map/all_gather | solution.py:78
  7.3 180.3 %reduce-scatter.2.cloned.1.call-start = ((), (), s32[]{:S(2)}) async-start(), calls=%async_computation.2 | async-start | bytes 4718592 | tf_op jit(solution)/shard_map/reduce_scatter | solution.py:118
  7.5 3.3 %slice-start.1 = ((bf16[3,4,1024,128]{3,2,1,0:T(8,128)(2,1)}), bf16[1,4,1024,128]{3,2,1,0:T(8,128)(2,1)S(1)}, s32[]{:S(2)}) async-start(bf16[3,4,1024,128]{3,2,1,0:T(8,128)(2,1)} %param.6), calls=%async_computation.4 | async-start | bytes 2097152 | tf_op jit(solution)/shard_map/slice | solution.py:92
  7.5 4.6 %copy-start.14 = (f32[4,4,4,4]{3,2,1,0:T(4,128)S(1)}, f32[4,4,4,4]{3,2,1,0:T(4,128)}, u32[]{:S(2)}) copy-start(f32[4,4,4,4]{3,2,1,0:T(4,128)} %param.8) | copy-start | bytes 3076
  18.4 28.3 %copy-start = (bf16[2,4,1024,128]{2,3,1,0:T(8,128)(2,1)S(1)}, bf16[2,4,1024,128]{2,3,1,0:T(8,128)(2,1)}, u32[]{:S(2)}) copy-start(bf16[2,4,1024,128]{2,3,1,0:T(8,128)(2,1)} %copy.47) | copy-start | bytes 6291460
  64.7 3.2 %copy-start.9 = (f32[512,128]{1,0:T(8,128)S(1)}, f32[512,128]{1,0:T(8,128)}, u32[]{:S(2)}) copy-start(f32[512,128]{1,0:T(8,128)} %get-tuple-element.10) | copy-start | bytes 786436
  64.7 4.0 %copy-start.10 = (f32[512,128]{1,0:T(8,128)S(1)}, f32[512,128]{1,0:T(8,128)}, u32[]{:S(2)}) copy-start(f32[512,128]{1,0:T(8,128)} %get-tuple-element.18) | copy-start | bytes 786436
  64.7 4.9 %copy-start.11 = (f32[512,128]{1,0:T(8,128)S(1)}, f32[512,128]{1,0:T(8,128)}, u32[]{:S(2)}) copy-start(f32[512,128]{1,0:T(8,128)} %get-tuple-element.26) | copy-start | bytes 786436
  64.7 6.5 %copy-start.8 = (f32[512,128]{1,0:T(8,128)S(1)}, f32[512,128]{1,0:T(8,128)}, u32[]{:S(2)}) copy-start(f32[512,128]{1,0:T(8,128)} %get-tuple-element.9) | copy-start | bytes 786436
  64.7 12.8 %copy-start.7 = (f32[512,128]{1,0:T(8,128)S(1)}, f32[512,128]{1,0:T(8,128)}, u32[]{:S(2)}) copy-start(f32[512,128]{1,0:T(8,128)} %get-tuple-element.8) | copy-start | bytes 786436
  66.0 17.7 %copy-start.5 = (f32[4,128,128]{1,2,0:T(8,128)S(1)}, f32[4,128,128]{1,2,0:T(8,128)}, u32[]{:S(2)}) copy-start(f32[4,128,128]{1,2,0:T(8,128)} %copy.26) | copy-start | bytes 786436
  66.0 17.7 %copy-start.6 = (f32[4,128,128]{1,2,0:T(8,128)S(1)}, f32[4,128,128]{1,2,0:T(8,128)}, u32[]{:S(2)}) copy-start(f32[4,128,128]{1,2,0:T(8,128)} %copy.27) | copy-start | bytes 786436
  72.1 15.0 %copy-start.1 = (f32[512,128]{1,0:T(8,128)S(1)}, f32[512,128]{1,0:T(8,128)}, u32[]{:S(2)}) copy-start(f32[512,128]{1,0:T(8,128)} %get-tuple-element.20) | copy-start | bytes 786436
  72.1 15.0 %copy-start.2 = (f32[512,128]{1,0:T(8,128)S(1)}, f32[512,128]{1,0:T(8,128)}, u32[]{:S(2)}) copy-start(f32[512,128]{1,0:T(8,128)} %get-tuple-element.21) | copy-start | bytes 786436
  72.1 15.0 %copy-start.3 = (f32[512,128]{1,0:T(8,128)S(1)}, f32[512,128]{1,0:T(8,128)}, u32[]{:S(2)}) copy-start(f32[512,128]{1,0:T(8,128)} %get-tuple-element.22) | copy-start | bytes 786436
  72.1 15.0 %copy-start.4 = (f32[512,128]{1,0:T(8,128)S(1)}, f32[512,128]{1,0:T(8,128)}, u32[]{:S(2)}) copy-start(f32[512,128]{1,0:T(8,128)} %get-tuple-element.27) | copy-start | bytes 786436
  87.1 15.8 %copy-start.12 = (bf16[1,4,1024,128]{2,3,1,0:T(8,128)(2,1)S(1)}, bf16[1,4,1024,128]{2,3,1,0:T(8,128)(2,1)}, u32[]{:S(2)}) copy-start(bf16[1,4,1024,128]{2,3,1,0:T(8,128)(2,1)} %copy.48) | copy-start | bytes 3145732
  87.1 15.8 %copy-start.32 = (bf16[512,4096]{1,0:T(8,128)(2,1)S(1)}, bf16[512,4096]{1,0:T(8,128)(2,1)}, u32[]{:S(2)}) copy-start(bf16[512,4096]{1,0:T(8,128)(2,1)} %all-gather.2.cloned.1.call-done) | copy-start | bytes 12582916
  90.6 15.7 %collective-permute-start = (bf16[4,128,128]{2,1,0:T(8,128)(2,1)S(1)}, bf16[4,128,128]{2,1,0:T(8,128)(2,1)S(1)}, u32[]{:S(2)}, u32[]{:S(2)}) collective-permute-start(bf16[4,128,128]{2,1,0:T(8,128)(2,1)S(1)} %get-tuple-element.113), channel_id=1, source_target_pairs={{0,8},{8,16},{16,24},{24,32},{32,40},{40,48},{48,56},{56,0},{64,72... | collective-permute-start | bytes 393224 | tf_op jit(solution)/shard_map/ppermute | solution.py:27
  92.2 17.6 %collective-permute-start.1 = (bf16[4,128,128]{2,1,0:T(8,128)(2,1)S(1)}, bf16[4,128,128]{2,1,0:T(8,128)(2,1)S(1)}, u32[]{:S(2)}, u32[]{:S(2)}) collective-permute-start(bf16[4,128,128]{2,1,0:T(8,128)(2,1)S(1)} %get-tuple-element.113), channel_id=1, source_target_pairs={{0,16},{8,24},{16,32},{24,40},{32,48},{40,56},{48,0},{56,8},{64,80... | collective-permute-start | bytes 393224 | tf_op jit(solution)/shard_map/ppermute | solution.py:27
  94.8 17.9 %collective-permute-start.2 = (bf16[4,128,128]{2,1,0:T(8,128)(2,1)S(1)}, bf16[4,128,128]{2,1,0:T(8,128)(2,1)S(1)}, u32[]{:S(2)}, u32[]{:S(2)}) collective-permute-start(bf16[4,128,128]{2,1,0:T(8,128)(2,1)S(1)} %get-tuple-element.113), channel_id=1, source_target_pairs={{0,24},{8,32},{16,40},{24,48},{32,56},{40,0},{48,8},{56,16},{64,88... | collective-permute-start | bytes 393224 | tf_op jit(solution)/shard_map/ppermute | solution.py:27
  97.7 18.5 %collective-permute-start.3 = (bf16[4,128,128]{2,1,0:T(8,128)(2,1)S(1)}, bf16[4,128,128]{2,1,0:T(8,128)(2,1)S(1)}, u32[]{:S(2)}, u32[]{:S(2)}) collective-permute-start(bf16[4,128,128]{2,1,0:T(8,128)(2,1)S(1)} %get-tuple-element.113), channel_id=1, source_target_pairs={{0,32},{8,40},{16,48},{24,56},{32,0},{40,8},{48,16},{56,24},{64,96... | collective-permute-start | bytes 393224 | tf_op jit(solution)/shard_map/ppermute | solution.py:27
  99.7 19.3 %collective-permute-start.4 = (bf16[4,128,128]{2,1,0:T(8,128)(2,1)S(1)}, bf16[4,128,128]{2,1,0:T(8,128)(2,1)S(1)}, u32[]{:S(2)}, u32[]{:S(2)}) collective-permute-start(bf16[4,128,128]{2,1,0:T(8,128)(2,1)S(1)} %get-tuple-element.113), channel_id=1, source_target_pairs={{0,40},{8,48},{16,56},{24,0},{32,8},{40,16},{48,24},{56,32},{64,10... | collective-permute-start | bytes 393224 | tf_op jit(solution)/shard_map/ppermute | solution.py:27
  105.2 5.9 %copy-start.16 = (f32[4]{0:T(128)S(1)}, f32[4]{0:T(128)}, u32[]{:S(2)}) copy-start(f32[4]{0:T(128)} %get-tuple-element.77) | copy-start | bytes 52
  105.2 5.9 %copy-start.17 = (f32[4]{0:T(128)S(1)}, f32[4]{0:T(128)}, u32[]{:S(2)}) copy-start(f32[4]{0:T(128)} %get-tuple-element.78) | copy-start | bytes 52
  105.3 5.9 %copy-start.18 = (f32[4]{0:T(128)S(1)}, f32[4]{0:T(128)}, u32[]{:S(2)}) copy-start(f32[4]{0:T(128)} %get-tuple-element.79) | copy-start | bytes 52
  105.3 5.9 %copy-start.19 = (f32[4]{0:T(128)S(1)}, f32[4]{0:T(128)}, u32[]{:S(2)}) copy-start(f32[4]{0:T(128)} %get-tuple-element.80) | copy-start | bytes 52
  105.3 5.9 %copy-start.20 = (f32[4]{0:T(128)S(1)}, f32[4]{0:T(128)}, u32[]{:S(2)}) copy-start(f32[4]{0:T(128)} %get-tuple-element.81) | copy-start | bytes 52
  105.3 5.9 %copy-start.21 = (f32[4]{0:T(128)S(1)}, f32[4]{0:T(128)}, u32[]{:S(2)}) copy-start(f32[4]{0:T(128)} %get-tuple-element.82) | copy-start | bytes 52
  105.3 5.9 %copy-start.22 = (f32[4]{0:T(128)S(1)}, f32[4]{0:T(128)}, u32[]{:S(2)}) copy-start(f32[4]{0:T(128)} %get-tuple-element.83) | copy-start | bytes 52
  105.3 5.9 %copy-start.23 = (f32[4]{0:T(128)S(1)}, f32[4]{0:T(128)}, u32[]{:S(2)}) copy-start(f32[4]{0:T(128)} %get-tuple-element.84) | copy-start | bytes 52
  105.3 5.9 %copy-start.24 = (f32[4]{0:T(128)S(1)}, f32[4]{0:T(128)}, u32[]{:S(2)}) copy-start(f32[4]{0:T(128)} %get-tuple-element.85) | copy-start | bytes 52
  105.3 5.9 %copy-start.25 = (f32[4]{0:T(128)S(1)}, f32[4]{0:T(128)}, u32[]{:S(2)}) copy-start(f32[4]{0:T(128)} %get-tuple-element.86) | copy-start | bytes 52
  105.3 5.9 %copy-start.26 = (f32[4]{0:T(128)S(1)}, f32[4]{0:T(128)}, u32[]{:S(2)}) copy-start(f32[4]{0:T(128)} %get-tuple-element.87) | copy-start | bytes 52
  105.3 5.9 %copy-start.27 = (f32[4]{0:T(128)S(1)}, f32[4]{0:T(128)}, u32[]{:S(2)}) copy-start(f32[4]{0:T(128)} %get-tuple-element.88) | copy-start | bytes 52
  105.4 5.9 %copy-start.28 = (f32[4]{0:T(128)S(1)}, f32[4]{0:T(128)}, u32[]{:S(2)}) copy-start(f32[4]{0:T(128)} %get-tuple-element.89) | copy-start | bytes 52
  105.4 5.9 %copy-start.29 = (f32[4]{0:T(128)S(1)}, f32[4]{0:T(128)}, u32[]{:S(2)}) copy-start(f32[4]{0:T(128)} %get-tuple-element.90) | copy-start | bytes 52
  105.4 5.9 %copy-start.30 = (f32[4]{0:T(128)S(1)}, f32[4]{0:T(128)}, u32[]{:S(2)}) copy-start(f32[4]{0:T(128)} %get-tuple-element.91) | copy-start | bytes 52
  105.4 5.9 %copy-start.31 = (f32[4]{0:T(128)S(1)}, f32[4]{0:T(128)}, u32[]{:S(2)}) copy-start(f32[4]{0:T(128)} %get-tuple-element.92) | copy-start | bytes 52
  106.3 16.5 %collective-permute-start.5 = (bf16[4,128,128]{2,1,0:T(8,128)(2,1)S(1)}, bf16[4,128,128]{2,1,0:T(8,128)(2,1)S(1)}, u32[]{:S(2)}, u32[]{:S(2)}) collective-permute-start(bf16[4,128,128]{2,1,0:T(8,128)(2,1)S(1)} %get-tuple-element.113), channel_id=1, source_target_pairs={{0,48},{8,56},{16,0},{24,8},{32,16},{40,24},{48,32},{56,40},{64,11... | collective-permute-start | bytes 393224 | tf_op jit(solution)/shard_map/ppermute | solution.py:27
  109.8 14.1 %collective-permute-start.6 = (bf16[4,128,128]{2,1,0:T(8,128)(2,1)S(1)}, bf16[4,128,128]{2,1,0:T(8,128)(2,1)S(1)}, u32[]{:S(2)}, u32[]{:S(2)}) collective-permute-start(bf16[4,128,128]{2,1,0:T(8,128)(2,1)S(1)} %get-tuple-element.113), channel_id=1, source_target_pairs={{0,56},{8,0},{16,8},{24,16},{32,24},{40,32},{48,40},{56,48},{64,12... | collective-permute-start | bytes 393224 | tf_op jit(solution)/shard_map/ppermute | solution.py:27
  124.8 9.5 %collective-permute-start.7 = (f32[4,128,128]{2,1,0:T(8,128)}, f32[4,128,128]{2,1,0:T(8,128)}, u32[]{:S(2)}, u32[]{:S(2)}) collective-permute-start(f32[4,128,128]{2,1,0:T(8,128)} %convert_add_fusion), channel_id=1, source_target_pairs={{0,64},{8,72},{16,80},{24,88},{32,96},{40,104},{48,112},{56,120},{... | collective-permute-start | bytes 786440 | tf_op jit(solution)/shard_map/ppermute | solution.py:27
  126.2 11.0 %collective-permute-start.8 = (f32[4,128,128]{2,1,0:T(8,128)}, f32[4,128,128]{2,1,0:T(8,128)}, u32[]{:S(2)}, u32[]{:S(2)}) collective-permute-start(f32[4,128,128]{2,1,0:T(8,128)} %convert_add_fusion), channel_id=1, source_target_pairs={{0,128},{8,136},{16,144},{24,152},{32,160},{40,168},{48,176},{56,1... | collective-permute-start | bytes 786440 | tf_op jit(solution)/shard_map/ppermute | solution.py:27
  127.4 12.6 %collective-permute-start.9 = (f32[4,128,128]{2,1,0:T(8,128)}, f32[4,128,128]{2,1,0:T(8,128)}, u32[]{:S(2)}, u32[]{:S(2)}) collective-permute-start(f32[4,128,128]{2,1,0:T(8,128)} %convert_add_fusion), channel_id=1, source_target_pairs={{0,192},{8,200},{16,208},{24,216},{32,224},{40,232},{48,240},{56,2... | collective-permute-start | bytes 786440 | tf_op jit(solution)/shard_map/ppermute | solution.py:27
  131.1 10.3 %copy-start.13 = (f32[4,4,128,128]{3,2,1,0:T(8,128)S(1)}, f32[4,4,128,128]{3,2,1,0:T(8,128)}, u32[]{:S(2)}) copy-start(f32[4,4,128,128]{3,2,1,0:T(8,128)} %fusion.2) | copy-start | bytes 3145732
  141.2 0.8 copy-start.15
Sparse Core Ops, SparseCore 0:
  9.2 37.4 all-gather.1
  149.2 38.3 reduce-scatter.1

commit v7 on v6

--- a/solution.py
+++ b/solution.py
@@ -68,7 +68,7 @@
                 part = products[c][:, None, at:at + cols] * mixing[p, term_index, c][None, :, None]
                 summed = part if summed is None else summed + part
         outs.append(summed.astype(jnp.bfloat16).reshape(tok_rows, PHM * cols))
-    return outs
+    return lax.optimization_barrier(outs)
 
 
 def on_device(ctx_devices, ctx_row, tokens, qkv_blocks, out_blocks, mix_factors, head_gain):

time: 195 us -> 177 us (0.908); the launches traced: 194 us -> 174 us
  waiting for transfers between devices: 82 us -> 70.3 us
  local copies, waits for them, and re-layouts: 37.8 us -> 28.1 us
    mul x19 -> x76, local copies, waits for them, and re-layouts: 23.3 us -> 15.1 us  [project(): products[c][:, None, at:at + cols] * mixing[p, term_index, c][None, :, None]]
    all_gather x1, waiting for transfers between devices: 22.7 us -> 17.1 us  [on_device(): whole = lax.all_gather(tokens, 'tp', axis=1, tiled=True)]
    ppermute x10, waiting for transfers between devices: 20 us -> 14.8 us  [ring_gather(): got = lax.ppermute(value, axis, pairs).astype(jnp.float32)]
    slice x8, local copies, waits for them, and re-layouts: 5.14 us -> 0.89 us  [project(): products[c][:, None, at:at + cols] * mixing[p, term_index, c][None, :, None]]
    dot_general x8, matrix products: 13 us -> 10.9 us  [project(): jnp.dot(whole[:, c * rows:(c + 1) * rows], weights, preferred_element_typ...]
    unnamed x69 -> x49, local copies, waits for them, and re-layouts: 8.43 us -> 10.4 us
  transfers between devices with their start and end apart: 12 -> 12, of which waited for: 9 -> 8; matrix products, arithmetic and copies ran while one was open for 11% -> 19% of each run, Pallas kernels for 0% -> 0%
where the time goes in v7:
time: 177 us; the launch traced here: 174 us
  waiting for transfers between devices  70.3 us (40%)
  local copies, waits for them, and re-layouts  28.1 us (16%)
  starting transfers between devices  22.2 us (13%)
  matrix products  20.6 us (12%)
  other arithmetic  18.2 us (10%)
  between operations  14.9 us (8%)
    reduce_scatter x1, waiting for transfers between devices, on_device(): lax.psum_scatter(partial_value.astype(jnp.bfloat16), 'tp', scatter_dimens...  37.7 us
    ppermute x10, starting transfers between devices, ring_gather(): got = lax.ppermute(value, axis, pairs).astype(jnp.float32)  22.2 us
    all_gather x1, waiting for transfers between devices, on_device(): whole = lax.all_gather(tokens, 'tp', axis=1, tiled=True)  17.1 us
    mul x76, local copies, waits for them, and re-layouts, project(): products[c][:, None, at:at + cols] * mixing[p, term_index, c][None, :, None]  15.1 us
    ppermute x10, waiting for transfers between devices, ring_gather(): got = lax.ppermute(value, axis, pairs).astype(jnp.float32)  14.8 us
    dot_general x8, matrix products, project(): jnp.dot(whole[:, c * rows:(c + 1) * rows], weights, preferred_element_typ...  10.9 us
    unnamed x49, local copies, waits for them, and re-layouts  10.4 us
    convert_element_type x3, other arithmetic, project(): outs.append(summed.astype(jnp.bfloat16).reshape(tok_rows, PHM * cols))  7.75 us
  transfers between devices with their start and end apart: 12, of which 8 were waited for; matrix products, arithmetic and copies ran while one was open for 19% of the time, Pallas kernels for 0%

profile of v7, /device:TPU:8, one launch (start us, length us, event | category | flops | bytes accessed | tf_op | source)
XLA Modules:
  0.0 174.3 jit_solution(13066936621278353118)
XLA Ops:
  6.5 0.7 all-gather.2.cloned.1.call-update
  7.5 0.6 slice-done
  8.1 2.7 %copy.18 = bf16[2,4,1024,128]{2,3,1,0:T(8,128)(2,1)} copy(bf16[2,4,1024,128]{3,2,1,0:T(8,128)(2,1)S(1)} %slice-done) | data formatting | bytes 4194304
  10.8 1.3 copy.19
  12.1 1.4 bitcast_convert_fusion.3
  13.6 5.2 %add_convert_fusion = bf16[4,128,4,1024]{3,2,1,0:T(4,128)(2,1)S(1)} fusion(f32[128,1024]{1,0:T(8,128)S(1)} %get-tuple-element.63, f32[4,4]{1,0:T(4,128)S(1)} %get-tuple-element.115, f32[128,1024]{1,0:T(8,128)S(1)} %get-tuple-element.64, f32[4,4]{1,0:T(4,128)S(1)} %get-tuple-element.116, f32[128,1024]{1,0:T(8,128)S(1)} %get-tuple-element.62, ...), kind=kLoop, calls=%fused_computation | loop fusion | flops 16777216 | bytes 6291712 | tf_op jit(solution)/shard_map/convert_element_type | solution.py:76
  18.8 4.3 %copy.69 = bf16[64,8,4,1024]{3,1,2,0:T(8,128)(2,1)} copy(bf16[64,8,4,1024]{3,2,1,0:T(4,128)(2,1)S(1)} %bitcast.602) | data formatting | bytes 8388608
  24.3 0.7 broadcast_bitcast_fusion
  25.0 0.6 broadcast_bitcast_fusion.2
  25.6 0.6 broadcast_bitcast_fusion.4
  26.2 0.7 broadcast_bitcast_fusion.6
  26.9 0.7 broadcast_bitcast_fusion.8
  27.6 0.7 broadcast_bitcast_fusion.10
  28.2 0.6 broadcast_bitcast_fusion.12
  28.9 0.7 broadcast_bitcast_fusion.14
  29.5 17.1 %all-gather.2.cloned.1.call-done = bf16[512,4096]{1,0:T(8,128)(2,1)} async-done(((bf16[512,512]{1,0:T(8,128)(2,1)}), bf16[512,4096]{1,0:T(8,128)(2,1)}) %all-gather.2.cloned.1.call-update) | async-done | bytes 4194320 | tf_op jit(solution)/shard_map/all_gather | solution.py:78
  46.7 2.5 %fusion.71 = f32[512,1024]{1,0:T(8,128)S(1)} fusion(bf16[1024,1024]{0,1:T(8,128)(2,1)S(1)} %bitcast.654, bf16[512,4096]{1,0:T(8,128)(2,1)} %all-gather.2.cloned.1.call-done), kind=kOutput, calls=%fused_computation.127 | convolution fusion | flops 1073741824 | bytes 5242880 | tf_op jit(solution)/shard_map/dot_general | solution.py:59
  49.4 2.0 %copy-done.21 = bf16[512,4096]{1,0:T(8,128)(2,1)S(1)} copy-done((bf16[512,4096]{1,0:T(8,128)(2,1)S(1)}, bf16[512,4096]{1,0:T(8,128)(2,1)}, u32[]{:S(2)}) %copy-start.21) | copy-done | bytes 4194328
  51.4 1.3 fusion.67
  52.8 1.3 fusion.63
  54.3 1.3 fusion.59
  55.7 0.2 mul.1279
  55.9 0.2 mul.1286
  56.1 0.2 mul.1293
  56.3 0.2 mul.1300
  56.5 0.2 mul.1307
  56.6 0.2 mul.1314
  56.8 0.2 mul.1321
  57.0 0.2 mul.1328
  57.2 0.2 mul.1335
  57.4 0.2 mul.1342
  58.7 2.7 %fusion.20 = bf16[512,512]{1,0:T(8,128)(2,1)S(1)} fusion(f32[64,8,4,128]{3,2,1,0:T(4,128)S(1)} %bitcast.648, f32[64,8,4,128]{3,2,1,0:T(4,128)S(1)} %bitcast.647, f32[64,8,4,128]{3,2,1,0:T(4,128)S(1)} %bitcast.644, f32[64,8,4,128]{3,2,1,0:T(4,128)S(1)} %bitcast.643, f32[64,8,4,128]{3,2,1,0:T(4,128)S(1)} %bitcast.640, f32[64,8,4,128]{3,2,1,0:T(4,128)S(1)} %bitcast.639, ...), kind=kLoop, calls=%fused_computation.41 | loop fusion | flops 8388608 | bytes 17334272 | tf_op jit(solution)/shard_map/convert_element_type | solution.py:70
  64.5 2.5 %fusion.36 = bf16[512,512]{1,0:T(8,128)(2,1)S(1)} fusion(f32[64,8,4,128]{3,2,1,0:T(4,128)S(1)} %bitcast.649, f32[64,8,4,128]{3,2,1,0:T(4,128)S(1)} %bitcast.645, f32[64,8,4,128]{3,2,1,0:T(4,128)S(1)} %bitcast.641, f32[64,8,4,128]{3,2,1,0:T(4,128)S(1)} %bitcast.637, f32[64,8,4,128]{3,2,1,0:T(4,128)S(1)} %bitcast.633, f32[64,8,4,128]{3,2,1,0:T(4,128)S(1)} %bitcast.630, ...), kind=kLoop, calls=%fused_computation.73 | loop fusion | flops 8388608 | bytes 17334272 | tf_op jit(solution)/shard_map/convert_element_type | solution.py:70
  67.1 0.3 copy.11
  67.6 0.9 fusion.107
  68.5 1.6 collective-permute-start
  70.1 2.5 %collective-permute-start.1 = (bf16[4,128,128]{2,1,0:T(8,128)(2,1)}, bf16[4,128,128]{2,1,0:T(8,128)(2,1)S(1)}, u32[]{:S(2)}, u32[]{:S(2)}) collective-permute-start(bf16[4,128,128]{2,1,0:T(8,128)(2,1)} %get-tuple-element.117), channel_id=1, source_target_pairs={{0,16},{8,24},{16,32},{24,40},{32,48},{40,56},{48,0},{56,8},{64,80... | collective-permute-start | bytes 393224 | tf_op jit(solution)/shard_map/ppermute | solution.py:27
  72.7 2.9 %collective-permute-start.2 = (bf16[4,128,128]{2,1,0:T(8,128)(2,1)}, bf16[4,128,128]{2,1,0:T(8,128)(2,1)S(1)}, u32[]{:S(2)}, u32[]{:S(2)}) collective-permute-start(bf16[4,128,128]{2,1,0:T(8,128)(2,1)} %get-tuple-element.117), channel_id=1, source_target_pairs={{0,24},{8,32},{16,40},{24,48},{32,56},{40,0},{48,8},{56,16},{64,88... | collective-permute-start | bytes 393224 | tf_op jit(solution)/shard_map/ppermute | solution.py:27
  75.6 2.0 %collective-permute-start.3 = (bf16[4,128,128]{2,1,0:T(8,128)(2,1)}, bf16[4,128,128]{2,1,0:T(8,128)(2,1)}, u32[]{:S(2)}, u32[]{:S(2)}) collective-permute-start(bf16[4,128,128]{2,1,0:T(8,128)(2,1)} %get-tuple-element.117), channel_id=1, source_target_pairs={{0,32},{8,40},{16,48},{24,56},{32,0},{40,8},{48,16},{56,24},{64,96... | collective-permute-start | bytes 393224 | tf_op jit(solution)/shard_map/ppermute | solution.py:27
  77.6 3.3 %collective-permute-start.4 = (bf16[4,128,128]{2,1,0:T(8,128)(2,1)}, bf16[4,128,128]{2,1,0:T(8,128)(2,1)}, u32[]{:S(2)}, u32[]{:S(2)}) collective-permute-start(bf16[4,128,128]{2,1,0:T(8,128)(2,1)} %get-tuple-element.117), channel_id=1, source_target_pairs={{0,40},{8,48},{16,56},{24,0},{32,8},{40,16},{48,24},{56,32},{64,10... | collective-permute-start | bytes 393224 | tf_op jit(solution)/shard_map/ppermute | solution.py:27
  80.9 2.3 %fusion.69 = f32[512,512]{1,0:T(8,128)S(1)} fusion(bf16[1024,512]{0,1:T(8,128)(2,1)} %bitcast.658, bf16[512,4096]{1,0:T(8,128)(2,1)} %all-gather.2.cloned.1.call-done), kind=kOutput, calls=%fused_computation.125 | convolution fusion | flops 536870912 | bytes 3145728 | tf_op jit(solution)/shard_map/dot_general | solution.py:59
  83.3 0.7 fusion.65
  84.1 0.7 fusion.61
  84.9 0.7 fusion.57
  85.8 3.5 %collective-permute-start.5 = (bf16[4,128,128]{2,1,0:T(8,128)(2,1)}, bf16[4,128,128]{2,1,0:T(8,128)(2,1)}, u32[]{:S(2)}, u32[]{:S(2)}) collective-permute-start(bf16[4,128,128]{2,1,0:T(8,128)(2,1)} %get-tuple-element.117), channel_id=1, source_target_pairs={{0,48},{8,56},{16,0},{24,8},{32,16},{40,24},{48,32},{56,40},{64,11... | collective-permute-start | bytes 393224 | tf_op jit(solution)/shard_map/ppermute | solution.py:27
  89.2 1.4 collective-permute-start.6
  94.0 2.5 %fusion.4 = bf16[512,512]{1,0:T(8,128)(2,1)S(1)} fusion(f32[64,8,4,128]{3,2,1,0:T(4,128)S(1)} %bitcast.650, f32[64,8,4,128]{3,2,1,0:T(4,128)S(1)} %bitcast.646, f32[64,8,4,128]{3,2,1,0:T(4,128)S(1)} %bitcast.642, f32[64,8,4,128]{3,2,1,0:T(4,128)S(1)} %bitcast.638, f32[64,8,4,128]{3,2,1,0:T(4,128)S(1)} %bitcast.634, f32[64,8,4,128]{3,2,1,0:T(4,128)S(1)} %bitcast.631, ...), kind=kLoop, calls=%fused_computation.9 | loop fusion | flops 8388608 | bytes 17334272 | tf_op jit(solution)/shard_map/convert_element_type | solution.py:70
  96.8 0.3 collective-permute-done.4
  97.1 3.8 %collective-permute-done.5 = bf16[4,128,128]{2,1,0:T(8,128)(2,1)} collective-permute-done((bf16[4,128,128]{2,1,0:T(8,128)(2,1)}, bf16[4,128,128]{2,1,0:T(8,128)(2,1)}, u32[]{:S(2)}, u32[]{:S(2)}) %collective-permute-start.5) | collective-permute-done | bytes 131104 | tf_op jit(solution)/shard_map/ppermute | solution.py:27
  101.0 1.1 collective-permute-done.6
  102.1 2.0 %convert_add_fusion = f32[4,128,128]{2,1,0:T(8,128)} fusion(bf16[4,128,128]{2,1,0:T(8,128)(2,1)} %collective-permute-done.6, bf16[4,128,128]{2,1,0:T(8,128)(2,1)} %collective-permute-done.5, bf16[4,128,128]{2,1,0:T(8,128)(2,1)} %collective-permute-done.4, bf16[4,128,128]{2,1,0:T(8,128)(2,1)} %collective-permute-done.3, ...), kind=kLoop, calls=%fused_computation.137 | loop fusion | flops 983040 | bytes 1310720 | tf_op jit(solution)/shard_map/add | solution.py:29
  104.1 1.5 collective-permute-start.7
  105.6 1.1 collective-permute-start.8
  106.7 2.4 %collective-permute-start.9 = (f32[4,128,128]{2,1,0:T(8,128)}, f32[4,128,128]{2,1,0:T(8,128)}, u32[]{:S(2)}, u32[]{:S(2)}) collective-permute-start(f32[4,128,128]{2,1,0:T(8,128)} %convert_add_fusion), channel_id=1, source_target_pairs={{0,192},{8,200},{16,208},{24,216},{32,224},{40,232},{48,240},{56,2... | collective-permute-start | bytes 786440 | tf_op jit(solution)/shard_map/ppermute | solution.py:27
  109.1 1.7 fusion.2
  110.7 2.9 %collective-permute-done.7 = f32[4,128,128]{2,1,0:T(8,128)} collective-permute-done((f32[4,128,128]{2,1,0:T(8,128)}, f32[4,128,128]{2,1,0:T(8,128)}, u32[]{:S(2)}, u32[]{:S(2)}) %collective-permute-start.7) | collective-permute-done | bytes 262176 | tf_op jit(solution)/shard_map/ppermute | solution.py:27
  113.6 3.0 %collective-permute-done.8 = f32[4,128,128]{2,1,0:T(8,128)} collective-permute-done((f32[4,128,128]{2,1,0:T(8,128)}, f32[4,128,128]{2,1,0:T(8,128)}, u32[]{:S(2)}, u32[]{:S(2)}) %collective-permute-start.8) | collective-permute-done | bytes 262176 | tf_op jit(solution)/shard_map/ppermute | solution.py:27
  116.6 3.5 %collective-permute-done.9 = f32[4,128,128]{2,1,0:T(8,128)} collective-permute-done((f32[4,128,128]{2,1,0:T(8,128)}, f32[4,128,128]{2,1,0:T(8,128)}, u32[]{:S(2)}, u32[]{:S(2)}) %collective-permute-start.9) | collective-permute-done | bytes 262176 | tf_op jit(solution)/shard_map/ppermute | solution.py:27
  120.2 1.4 fusion.92
  121.9 0.5 multiply_reduce_fusion
  122.4 0.2 multiply_convert_fusion
  122.6 0.3 copy.16
  122.9 6.6 %convolution_convert_fusion = bf16[512,4096]{1,0:T(8,128)(2,1)} fusion(bf16[512,4096]{1,0:T(8,128)(2,1)} %bitcast.651, bf16[64,8,4,128]{3,2,1,0:T(4,128)(2,1)S(1)} %bitcast.662), kind=kOutput, calls=%fused_computation.1 | convolution fusion | flops 2149580800 | bytes 8912896 | tf_op jit(solution)/shard_map/dot_general | solution.py:117
  129.5 37.7 %reduce-scatter.2.cloned.1.call-done = bf16[512,512]{1,0:T(8,128)(2,1)} async-done(((bf16[512,4096]{1,0:T(8,128)(2,1)}), bf16[512,512]{1,0:T(8,128)(2,1)}) %reduce-scatter.2.cloned.1.call-update) | async-done | bytes 524304 | tf_op jit(solution)/shard_map/reduce_scatter | solution.py:118
  (131 shorter events, 9.9 us)
Async XLA Ops:
  6.5 1.6 slice-start
  6.5 40.1 %all-gather.2.cloned.1.call-start = ((), (), s32[]{:S(2)}) async-start(), calls=%async_computation.1 | async-start | bytes 4718592 | tf_op jit(solution)/shard_map/all_gather | solution.py:78
  7.3 160.0 %reduce-scatter.2.cloned.1.call-start = ((), (), s32[]{:S(2)}) async-start(), calls=%async_computation.2 | async-start | bytes 4718592 | tf_op jit(solution)/shard_map/reduce_scatter | solution.py:118
  7.5 3.3 %slice-start.1 = ((bf16[3,4,1024,128]{3,2,1,0:T(8,128)(2,1)}), bf16[1,4,1024,128]{3,2,1,0:T(8,128)(2,1)S(1)}, s32[]{:S(2)}) async-start(bf16[3,4,1024,128]{3,2,1,0:T(8,128)(2,1)} %param.6), calls=%async_computation.4 | async-start | bytes 2097152 | tf_op jit(solution)/shard_map/slice | solution.py:92
  8.1 5.4 %copy-start.3 = (f32[4,4,4,4]{3,2,1,0:T(4,128)S(1)}, f32[4,4,4,4]{3,2,1,0:T(4,128)}, u32[]{:S(2)}) copy-start(f32[4,4,4,4]{3,2,1,0:T(4,128)} %param.8) | copy-start | bytes 3076
  18.7 27.9 %copy-start = (bf16[2,4,1024,128]{2,3,1,0:T(8,128)(2,1)S(1)}, bf16[2,4,1024,128]{2,3,1,0:T(8,128)(2,1)}, u32[]{:S(2)}) copy-start(bf16[2,4,1024,128]{2,3,1,0:T(8,128)(2,1)} %copy.18) | copy-start | bytes 6291460
  49.2 2.2 %copy-start.21 = (bf16[512,4096]{1,0:T(8,128)(2,1)S(1)}, bf16[512,4096]{1,0:T(8,128)(2,1)}, u32[]{:S(2)}) copy-start(bf16[512,4096]{1,0:T(8,128)(2,1)} %all-gather.2.cloned.1.call-done) | copy-start | bytes 12582916
  67.6 15.7 %copy-start.1 = (bf16[1,4,1024,128]{2,3,1,0:T(8,128)(2,1)S(1)}, bf16[1,4,1024,128]{2,3,1,0:T(8,128)(2,1)}, u32[]{:S(2)}) copy-start(bf16[1,4,1024,128]{2,3,1,0:T(8,128)(2,1)} %copy.19) | copy-start | bytes 3145732
  67.6 15.7 %copy-start.22 = (bf16[512,4096]{1,0:T(8,128)(2,1)S(1)}, bf16[512,4096]{1,0:T(8,128)(2,1)}, u32[]{:S(2)}) copy-start(bf16[512,4096]{1,0:T(8,128)(2,1)} %all-gather.2.cloned.1.call-done) | copy-start | bytes 12582916
  68.5 17.2 %collective-permute-start = (bf16[4,128,128]{2,1,0:T(8,128)(2,1)}, bf16[4,128,128]{2,1,0:T(8,128)(2,1)S(1)}, u32[]{:S(2)}, u32[]{:S(2)}) collective-permute-start(bf16[4,128,128]{2,1,0:T(8,128)(2,1)} %get-tuple-element.117), channel_id=1, source_target_pairs={{0,8},{8,16},{16,24},{24,32},{32,40},{40,48},{48,56},{56,0},{64,72... | collective-permute-start | bytes 393224 | tf_op jit(solution)/shard_map/ppermute | solution.py:27
  70.1 19.1 %collective-permute-start.1 = (bf16[4,128,128]{2,1,0:T(8,128)(2,1)}, bf16[4,128,128]{2,1,0:T(8,128)(2,1)S(1)}, u32[]{:S(2)}, u32[]{:S(2)}) collective-permute-start(bf16[4,128,128]{2,1,0:T(8,128)(2,1)} %get-tuple-element.117), channel_id=1, source_target_pairs={{0,16},{8,24},{16,32},{24,40},{32,48},{40,56},{48,0},{56,8},{64,80... | collective-permute-start | bytes 393224 | tf_op jit(solution)/shard_map/ppermute | solution.py:27
  72.7 24.1 %collective-permute-start.2 = (bf16[4,128,128]{2,1,0:T(8,128)(2,1)}, bf16[4,128,128]{2,1,0:T(8,128)(2,1)S(1)}, u32[]{:S(2)}, u32[]{:S(2)}) collective-permute-start(bf16[4,128,128]{2,1,0:T(8,128)(2,1)} %get-tuple-element.117), channel_id=1, source_target_pairs={{0,24},{8,32},{16,40},{24,48},{32,56},{40,0},{48,8},{56,16},{64,88... | collective-permute-start | bytes 393224 | tf_op jit(solution)/shard_map/ppermute | solution.py:27
  75.6 21.2 %collective-permute-start.3 = (bf16[4,128,128]{2,1,0:T(8,128)(2,1)}, bf16[4,128,128]{2,1,0:T(8,128)(2,1)}, u32[]{:S(2)}, u32[]{:S(2)}) collective-permute-start(bf16[4,128,128]{2,1,0:T(8,128)(2,1)} %get-tuple-element.117), channel_id=1, source_target_pairs={{0,32},{8,40},{16,48},{24,56},{32,0},{40,8},{48,16},{56,24},{64,96... | collective-permute-start | bytes 393224 | tf_op jit(solution)/shard_map/ppermute | solution.py:27
  77.6 19.5 %collective-permute-start.4 = (bf16[4,128,128]{2,1,0:T(8,128)(2,1)}, bf16[4,128,128]{2,1,0:T(8,128)(2,1)}, u32[]{:S(2)}, u32[]{:S(2)}) collective-permute-start(bf16[4,128,128]{2,1,0:T(8,128)(2,1)} %get-tuple-element.117), channel_id=1, source_target_pairs={{0,40},{8,48},{16,56},{24,0},{32,8},{40,16},{48,24},{56,32},{64,10... | collective-permute-start | bytes 393224 | tf_op jit(solution)/shard_map/ppermute | solution.py:27
  85.8 15.2 %collective-permute-start.5 = (bf16[4,128,128]{2,1,0:T(8,128)(2,1)}, bf16[4,128,128]{2,1,0:T(8,128)(2,1)}, u32[]{:S(2)}, u32[]{:S(2)}) collective-permute-start(bf16[4,128,128]{2,1,0:T(8,128)(2,1)} %get-tuple-element.117), channel_id=1, source_target_pairs={{0,48},{8,56},{16,0},{24,8},{32,16},{40,24},{48,32},{56,40},{64,11... | collective-permute-start | bytes 393224 | tf_op jit(solution)/shard_map/ppermute | solution.py:27
  89.2 12.9 %collective-permute-start.6 = (bf16[4,128,128]{2,1,0:T(8,128)(2,1)}, bf16[4,128,128]{2,1,0:T(8,128)(2,1)}, u32[]{:S(2)}, u32[]{:S(2)}) collective-permute-start(bf16[4,128,128]{2,1,0:T(8,128)(2,1)} %get-tuple-element.117), channel_id=1, source_target_pairs={{0,56},{8,0},{16,8},{24,16},{32,24},{40,32},{48,40},{56,48},{64,12... | collective-permute-start | bytes 393224 | tf_op jit(solution)/shard_map/ppermute | solution.py:27
  92.6 1.3 copy-start.4
  92.6 1.3 copy-start.5
  92.6 1.3 copy-start.6
  92.6 1.3 copy-start.7
  92.6 1.3 copy-start.8
  92.6 1.3 copy-start.9
  92.6 1.3 copy-start.10
  92.6 1.3 copy-start.11
  92.6 1.3 copy-start.12
  92.6 1.3 copy-start.13
  92.7 1.3 copy-start.14
  92.7 1.3 copy-start.15
  92.7 1.3 copy-start.16
  92.7 1.3 copy-start.17
  92.7 1.3 copy-start.18
  92.7 1.3 copy-start.19
  104.1 9.5 %collective-permute-start.7 = (f32[4,128,128]{2,1,0:T(8,128)}, f32[4,128,128]{2,1,0:T(8,128)}, u32[]{:S(2)}, u32[]{:S(2)}) collective-permute-start(f32[4,128,128]{2,1,0:T(8,128)} %convert_add_fusion), channel_id=1, source_target_pairs={{0,64},{8,72},{16,80},{24,88},{32,96},{40,104},{48,112},{56,120},{... | collective-permute-start | bytes 786440 | tf_op jit(solution)/shard_map/ppermute | solution.py:27
  105.6 11.0 %collective-permute-start.8 = (f32[4,128,128]{2,1,0:T(8,128)}, f32[4,128,128]{2,1,0:T(8,128)}, u32[]{:S(2)}, u32[]{:S(2)}) collective-permute-start(f32[4,128,128]{2,1,0:T(8,128)} %convert_add_fusion), channel_id=1, source_target_pairs={{0,128},{8,136},{16,144},{24,152},{32,160},{40,168},{48,176},{56,1... | collective-permute-start | bytes 786440 | tf_op jit(solution)/shard_map/ppermute | solution.py:27
  106.7 13.5 %collective-permute-start.9 = (f32[4,128,128]{2,1,0:T(8,128)}, f32[4,128,128]{2,1,0:T(8,128)}, u32[]{:S(2)}, u32[]{:S(2)}) collective-permute-start(f32[4,128,128]{2,1,0:T(8,128)} %convert_add_fusion), channel_id=1, source_target_pairs={{0,192},{8,200},{16,208},{24,216},{32,224},{40,232},{48,240},{56,2... | collective-permute-start | bytes 786440 | tf_op jit(solution)/shard_map/ppermute | solution.py:27
  110.7 11.1 %copy-start.2 = (f32[4,4,128,128]{3,2,1,0:T(8,128)S(1)}, f32[4,4,128,128]{3,2,1,0:T(8,128)}, u32[]{:S(2)}) copy-start(f32[4,4,128,128]{3,2,1,0:T(8,128)} %fusion.2) | copy-start | bytes 3145732
  121.6 0.8 copy-start.20
Sparse Core Ops, SparseCore 0:
  9.2 37.4 all-gather.1
  129.6 37.5 reduce-scatter.1

commit v8 on v7

--- a/solution.py
+++ b/solution.py
@@ -31,11 +31,19 @@
     return total, earlier
 
 
+def earlier_rows(value, axis, devices, size, stride):
+    earlier = jnp.zeros_like(value)
+    for shift in range(1, size):
+        pairs = [(i, i + shift * stride) for i in range(devices) if (i // stride) % size + shift < size]
+        earlier = earlier + lax.ppermute(value, axis, pairs)
+    return earlier
+
+
 def exclusive_prefix(value, axis, devices, row):
     here = lax.axis_index(axis)
     pos, col = here % row, here // row
     row_total, before = ring_gather(value.astype(jnp.bfloat16), axis, devices, row, 1, pos)
-    _, rows_before = ring_gather(row_total, axis, devices, devices // row, row, col)
+    rows_before = earlier_rows(row_total, axis, devices, devices // row, row)
     return before + rows_before
 
 

time: 177 us -> 180 us (1.017)
  starting transfers between devices: 22.2 us -> 24.9 us
    ppermute x10 -> x7, waiting for transfers between devices: 14.8 us -> 5.33 us  [ring_gather(): got = lax.ppermute(value, axis, pairs).astype(jnp.float32)]
    ppermute x0 -> x3, starting transfers between devices: none -> 7.57 us  [earlier_rows(): earlier = earlier + lax.ppermute(value, axis, pairs)]
    reduce_scatter x1, waiting for transfers between devices: 37.7 us -> 44.8 us  [on_device(): lax.psum_scatter(partial_value.astype(jnp.bfloat16), 'tp', scatter_dimens...]
    ppermute x10 -> x7, starting transfers between devices: 22.2 us -> 17.2 us  [ring_gather(): got = lax.ppermute(value, axis, pairs).astype(jnp.float32)]
    ppermute x0 -> x3, waiting for transfers between devices: none -> 2.13 us  [earlier_rows(): earlier = earlier + lax.ppermute(value, axis, pairs)]
  transfers between devices with their start and end apart: 12 -> 12, of which waited for: 8 -> 6; matrix products, arithmetic and copies ran while one was open for 19% -> 19% of each run, Pallas kernels for 0% -> 0%
where the time goes in v8:
time: 180 us; the launch traced here: 177 us
  waiting for transfers between devices  70.1 us (39%)
  local copies, waits for them, and re-layouts  28.2 us (16%)
  starting transfers between devices  24.9 us (14%)
  matrix products  20.6 us (11%)
  other arithmetic  18.3 us (10%)
  between operations  14.8 us (8%)
    reduce_scatter x1, waiting for transfers between devices, on_device(): lax.psum_scatter(partial_value.astype(jnp.bfloat16), 'tp', scatter_dimens...  44.8 us
    ppermute x7, starting transfers between devices, ring_gather(): got = lax.ppermute(value, axis, pairs).astype(jnp.float32)  17.2 us
    all_gather x1, waiting for transfers between devices, on_device(): whole = lax.all_gather(tokens, 'tp', axis=1, tiled=True)  17.1 us
    mul x76, local copies, waits for them, and re-layouts, project(): products[c][:, None, at:at + cols] * mixing[p, term_index, c][None, :, None]  15.1 us
    dot_general x8, matrix products, project(): jnp.dot(whole[:, c * rows:(c + 1) * rows], weights, preferred_element_typ...  10.9 us
    unnamed x49, local copies, waits for them, and re-layouts  10.4 us
    convert_element_type x3, other arithmetic, project(): outs.append(summed.astype(jnp.bfloat16).reshape(tok_rows, PHM * cols))  7.75 us
    ppermute x3, starting transfers between devices, earlier_rows(): earlier = earlier + lax.ppermute(value, axis, pairs)  7.57 us
  transfers between devices with their start and end apart: 12, of which 6 were waited for; matrix products, arithmetic and copies ran while one was open for 19% of the time, Pallas kernels for 0%

profile of v8, /device:TPU:8, one launch (start us, length us, event | category | flops | bytes accessed | tf_op | source)
XLA Modules:
  0.0 176.9 jit_solution(7819105809712494587)
XLA Ops:
  6.5 0.7 all-gather.2.cloned.1.call-update
  7.4 0.7 slice-done
  8.1 2.7 %copy.18 = bf16[2,4,1024,128]{2,3,1,0:T(8,128)(2,1)} copy(bf16[2,4,1024,128]{3,2,1,0:T(8,128)(2,1)S(1)} %slice-done) | data formatting | bytes 4194304
  10.8 1.3 copy.19
  12.1 1.4 bitcast_convert_fusion.3
  13.6 5.2 %add_convert_fusion = bf16[4,128,4,1024]{3,2,1,0:T(4,128)(2,1)S(1)} fusion(f32[128,1024]{1,0:T(8,128)S(1)} %get-tuple-element.63, f32[4,4]{1,0:T(4,128)S(1)} %get-tuple-element.115, f32[128,1024]{1,0:T(8,128)S(1)} %get-tuple-element.64, f32[4,4]{1,0:T(4,128)S(1)} %get-tuple-element.116, f32[128,1024]{1,0:T(8,128)S(1)} %get-tuple-element.62, ...), kind=kLoop, calls=%fused_computation | loop fusion | flops 16777216 | bytes 6291712 | tf_op jit(solution)/shard_map/convert_element_type | solution.py:84
  18.8 4.3 %copy.69 = bf16[64,8,4,1024]{3,1,2,0:T(8,128)(2,1)} copy(bf16[64,8,4,1024]{3,2,1,0:T(4,128)(2,1)S(1)} %bitcast.602) | data formatting | bytes 8388608
  24.3 0.7 broadcast_bitcast_fusion
  25.0 0.6 broadcast_bitcast_fusion.2
  25.6 0.6 broadcast_bitcast_fusion.4
  26.2 0.7 broadcast_bitcast_fusion.6
  26.9 0.7 broadcast_bitcast_fusion.8
  27.6 0.7 broadcast_bitcast_fusion.10
  28.2 0.6 broadcast_bitcast_fusion.12
  28.9 0.7 broadcast_bitcast_fusion.14
  29.5 17.1 %all-gather.2.cloned.1.call-done = bf16[512,4096]{1,0:T(8,128)(2,1)} async-done(((bf16[512,512]{1,0:T(8,128)(2,1)}), bf16[512,4096]{1,0:T(8,128)(2,1)}) %all-gather.2.cloned.1.call-update) | async-done | bytes 4194320 | tf_op jit(solution)/shard_map/all_gather | solution.py:86
  46.7 2.5 %fusion.71 = f32[512,1024]{1,0:T(8,128)S(1)} fusion(bf16[1024,1024]{0,1:T(8,128)(2,1)S(1)} %bitcast.654, bf16[512,4096]{1,0:T(8,128)(2,1)} %all-gather.2.cloned.1.call-done), kind=kOutput, calls=%fused_computation.127 | convolution fusion | flops 1073741824 | bytes 5242880 | tf_op jit(solution)/shard_map/dot_general | solution.py:67
  49.4 2.0 %copy-done.21 = bf16[512,4096]{1,0:T(8,128)(2,1)S(1)} copy-done((bf16[512,4096]{1,0:T(8,128)(2,1)S(1)}, bf16[512,4096]{1,0:T(8,128)(2,1)}, u32[]{:S(2)}) %copy-start.21) | copy-done | bytes 4194328
  51.4 1.3 fusion.67
  52.8 1.3 fusion.63
  54.3 1.3 fusion.59
  55.7 0.2 mul.1279
  55.9 0.2 mul.1286
  56.1 0.2 mul.1293
  56.3 0.2 mul.1300
  56.5 0.2 mul.1307
  56.6 0.2 mul.1314
  56.8 0.2 mul.1321
  57.0 0.2 mul.1328
  57.2 0.2 mul.1335
  57.4 0.2 mul.1342
  57.6 0.2 mul.1349
  57.8 0.2 mul.1356
  58.7 2.7 %fusion.20 = bf16[512,512]{1,0:T(8,128)(2,1)S(1)} fusion(f32[64,8,4,128]{3,2,1,0:T(4,128)S(1)} %bitcast.648, f32[64,8,4,128]{3,2,1,0:T(4,128)S(1)} %bitcast.647, f32[64,8,4,128]{3,2,1,0:T(4,128)S(1)} %bitcast.644, f32[64,8,4,128]{3,2,1,0:T(4,128)S(1)} %bitcast.643, f32[64,8,4,128]{3,2,1,0:T(4,128)S(1)} %bitcast.640, f32[64,8,4,128]{3,2,1,0:T(4,128)S(1)} %bitcast.639, ...), kind=kLoop, calls=%fused_computation.41 | loop fusion | flops 8388608 | bytes 17334272 | tf_op jit(solution)/shard_map/convert_element_type | solution.py:78
  64.5 2.5 %fusion.36 = bf16[512,512]{1,0:T(8,128)(2,1)S(1)} fusion(f32[64,8,4,128]{3,2,1,0:T(4,128)S(1)} %bitcast.649, f32[64,8,4,128]{3,2,1,0:T(4,128)S(1)} %bitcast.645, f32[64,8,4,128]{3,2,1,0:T(4,128)S(1)} %bitcast.641, f32[64,8,4,128]{3,2,1,0:T(4,128)S(1)} %bitcast.637, f32[64,8,4,128]{3,2,1,0:T(4,128)S(1)} %bitcast.633, f32[64,8,4,128]{3,2,1,0:T(4,128)S(1)} %bitcast.630, ...), kind=kLoop, calls=%fused_computation.73 | loop fusion | flops 8388608 | bytes 17334272 | tf_op jit(solution)/shard_map/convert_element_type | solution.py:78
  67.1 0.3 copy.11
  67.6 0.9 fusion.107
  68.5 1.6 collective-permute-start
  70.1 2.5 %collective-permute-start.1 = (bf16[4,128,128]{2,1,0:T(8,128)(2,1)}, bf16[4,128,128]{2,1,0:T(8,128)(2,1)S(1)}, u32[]{:S(2)}, u32[]{:S(2)}) collective-permute-start(bf16[4,128,128]{2,1,0:T(8,128)(2,1)} %get-tuple-element.117), channel_id=1, source_target_pairs={{0,16},{8,24},{16,32},{24,40},{32,48},{40,56},{48,0},{56,8},{64,80... | collective-permute-start | bytes 393224 | tf_op jit(solution)/shard_map/ppermute | solution.py:27
  72.7 2.9 %collective-permute-start.2 = (bf16[4,128,128]{2,1,0:T(8,128)(2,1)}, bf16[4,128,128]{2,1,0:T(8,128)(2,1)S(1)}, u32[]{:S(2)}, u32[]{:S(2)}) collective-permute-start(bf16[4,128,128]{2,1,0:T(8,128)(2,1)} %get-tuple-element.117), channel_id=1, source_target_pairs={{0,24},{8,32},{16,40},{24,48},{32,56},{40,0},{48,8},{56,16},{64,88... | collective-permute-start | bytes 393224 | tf_op jit(solution)/shard_map/ppermute | solution.py:27
  75.6 2.0 %collective-permute-start.3 = (bf16[4,128,128]{2,1,0:T(8,128)(2,1)}, bf16[4,128,128]{2,1,0:T(8,128)(2,1)}, u32[]{:S(2)}, u32[]{:S(2)}) collective-permute-start(bf16[4,128,128]{2,1,0:T(8,128)(2,1)} %get-tuple-element.117), channel_id=1, source_target_pairs={{0,32},{8,40},{16,48},{24,56},{32,0},{40,8},{48,16},{56,24},{64,96... | collective-permute-start | bytes 393224 | tf_op jit(solution)/shard_map/ppermute | solution.py:27
  77.6 3.3 %collective-permute-start.4 = (bf16[4,128,128]{2,1,0:T(8,128)(2,1)}, bf16[4,128,128]{2,1,0:T(8,128)(2,1)}, u32[]{:S(2)}, u32[]{:S(2)}) collective-permute-start(bf16[4,128,128]{2,1,0:T(8,128)(2,1)} %get-tuple-element.117), channel_id=1, source_target_pairs={{0,40},{8,48},{16,56},{24,0},{32,8},{40,16},{48,24},{56,32},{64,10... | collective-permute-start | bytes 393224 | tf_op jit(solution)/shard_map/ppermute | solution.py:27
  80.9 2.3 %fusion.69 = f32[512,512]{1,0:T(8,128)S(1)} fusion(bf16[1024,512]{0,1:T(8,128)(2,1)} %bitcast.658, bf16[512,4096]{1,0:T(8,128)(2,1)} %all-gather.2.cloned.1.call-done), kind=kOutput, calls=%fused_computation.125 | convolution fusion | flops 536870912 | bytes 3145728 | tf_op jit(solution)/shard_map/dot_general | solution.py:67
  83.3 0.7 fusion.65
  84.1 0.7 fusion.61
  84.9 0.7 fusion.57
  85.8 3.5 %collective-permute-start.5 = (bf16[4,128,128]{2,1,0:T(8,128)(2,1)}, bf16[4,128,128]{2,1,0:T(8,128)(2,1)}, u32[]{:S(2)}, u32[]{:S(2)}) collective-permute-start(bf16[4,128,128]{2,1,0:T(8,128)(2,1)} %get-tuple-element.117), channel_id=1, source_target_pairs={{0,48},{8,56},{16,0},{24,8},{32,16},{40,24},{48,32},{56,40},{64,11... | collective-permute-start | bytes 393224 | tf_op jit(solution)/shard_map/ppermute | solution.py:27
  89.2 1.4 collective-permute-start.6
  94.0 2.5 %fusion.4 = bf16[512,512]{1,0:T(8,128)(2,1)S(1)} fusion(f32[64,8,4,128]{3,2,1,0:T(4,128)S(1)} %bitcast.650, f32[64,8,4,128]{3,2,1,0:T(4,128)S(1)} %bitcast.646, f32[64,8,4,128]{3,2,1,0:T(4,128)S(1)} %bitcast.642, f32[64,8,4,128]{3,2,1,0:T(4,128)S(1)} %bitcast.638, f32[64,8,4,128]{3,2,1,0:T(4,128)S(1)} %bitcast.634, f32[64,8,4,128]{3,2,1,0:T(4,128)S(1)} %bitcast.631, ...), kind=kLoop, calls=%fused_computation.9 | loop fusion | flops 8388608 | bytes 17334272 | tf_op jit(solution)/shard_map/convert_element_type | solution.py:78
  96.8 0.3 collective-permute-done.4
  97.1 3.8 %collective-permute-done.5 = bf16[4,128,128]{2,1,0:T(8,128)(2,1)} collective-permute-done((bf16[4,128,128]{2,1,0:T(8,128)(2,1)}, bf16[4,128,128]{2,1,0:T(8,128)(2,1)}, u32[]{:S(2)}, u32[]{:S(2)}) %collective-permute-start.5) | collective-permute-done | bytes 131104 | tf_op jit(solution)/shard_map/ppermute | solution.py:27
  101.0 1.1 collective-permute-done.6
  102.1 2.0 %convert_add_fusion = f32[4,128,128]{2,1,0:T(8,128)} fusion(bf16[4,128,128]{2,1,0:T(8,128)(2,1)} %collective-permute-done.6, bf16[4,128,128]{2,1,0:T(8,128)(2,1)} %collective-permute-done.5, bf16[4,128,128]{2,1,0:T(8,128)(2,1)} %collective-permute-done.4, bf16[4,128,128]{2,1,0:T(8,128)(2,1)} %collective-permute-done.3, ...), kind=kLoop, calls=%fused_computation.137 | loop fusion | flops 983040 | bytes 1310720 | tf_op jit(solution)/shard_map/add | solution.py:29
  104.1 3.4 %collective-permute-start.7 = (f32[4,128,128]{2,1,0:T(8,128)}, f32[4,128,128]{2,1,0:T(8,128)}, u32[]{:S(2)}, u32[]{:S(2)}) collective-permute-start(f32[4,128,128]{2,1,0:T(8,128)} %convert_add_fusion), channel_id=1, source_target_pairs={{0,64},{8,72},{16,80},{24,88},{32,96},{40,104},{48,112},{56,120},{... | collective-permute-start | bytes 786440 | tf_op jit(solution)/shard_map/ppermute | solution.py:38
  107.6 2.6 %collective-permute-start.8 = (f32[4,128,128]{2,1,0:T(8,128)}, f32[4,128,128]{2,1,0:T(8,128)}, u32[]{:S(2)}, u32[]{:S(2)}) collective-permute-start(f32[4,128,128]{2,1,0:T(8,128)} %convert_add_fusion), channel_id=1, source_target_pairs={{0,128},{8,136},{16,144},{24,152},{32,160},{40,168},{48,176},{56,1... | collective-permute-start | bytes 786440 | tf_op jit(solution)/shard_map/ppermute | solution.py:38
  110.1 1.6 collective-permute-start.9
  111.7 1.7 fusion.2
  113.4 2.1 %collective-permute-done.7 = f32[4,128,128]{2,1,0:T(8,128)} collective-permute-done((f32[4,128,128]{2,1,0:T(8,128)}, f32[4,128,128]{2,1,0:T(8,128)}, u32[]{:S(2)}, u32[]{:S(2)}) %collective-permute-start.7) | collective-permute-done | bytes 262176 | tf_op jit(solution)/shard_map/ppermute | solution.py:38
  115.5 1.5 fusion.92
  117.3 0.5 multiply_reduce_fusion
  117.9 0.2 multiply_convert_fusion
  118.1 0.3 copy.16
  118.4 6.6 %convolution_convert_fusion = bf16[512,4096]{1,0:T(8,128)(2,1)} fusion(bf16[512,4096]{1,0:T(8,128)(2,1)} %bitcast.651, bf16[64,8,4,128]{3,2,1,0:T(4,128)(2,1)S(1)} %bitcast.662), kind=kOutput, calls=%fused_computation.1 | convolution fusion | flops 2149580800 | bytes 8912896 | tf_op jit(solution)/shard_map/dot_general | solution.py:125
  125.0 44.8 %reduce-scatter.2.cloned.1.call-done = bf16[512,512]{1,0:T(8,128)(2,1)} async-done(((bf16[512,4096]{1,0:T(8,128)(2,1)}), bf16[512,512]{1,0:T(8,128)(2,1)}) %reduce-scatter.2.cloned.1.call-update) | async-done | bytes 524304 | tf_op jit(solution)/shard_map/reduce_scatter | solution.py:126
  (131 shorter events, 9.6 us)
Async XLA Ops:
  6.5 1.6 slice-start
  6.5 40.1 %all-gather.2.cloned.1.call-start = ((), (), s32[]{:S(2)}) async-start(), calls=%async_computation.1 | async-start | bytes 4718592 | tf_op jit(solution)/shard_map/all_gather | solution.py:86
  7.3 162.5 %reduce-scatter.2.cloned.1.call-start = ((), (), s32[]{:S(2)}) async-start(), calls=%async_computation.2 | async-start | bytes 4718592 | tf_op jit(solution)/shard_map/reduce_scatter | solution.py:126
  7.4 3.4 %slice-start.1 = ((bf16[3,4,1024,128]{3,2,1,0:T(8,128)(2,1)}), bf16[1,4,1024,128]{3,2,1,0:T(8,128)(2,1)S(1)}, s32[]{:S(2)}) async-start(bf16[3,4,1024,128]{3,2,1,0:T(8,128)(2,1)} %param.6), calls=%async_computation.4 | async-start | bytes 2097152 | tf_op jit(solution)/shard_map/slice | solution.py:100
  8.1 5.4 %copy-start.3 = (f32[4,4,4,4]{3,2,1,0:T(4,128)S(1)}, f32[4,4,4,4]{3,2,1,0:T(4,128)}, u32[]{:S(2)}) copy-start(f32[4,4,4,4]{3,2,1,0:T(4,128)} %param.8) | copy-start | bytes 3076
  18.7 27.9 %copy-start = (bf16[2,4,1024,128]{2,3,1,0:T(8,128)(2,1)S(1)}, bf16[2,4,1024,128]{2,3,1,0:T(8,128)(2,1)}, u32[]{:S(2)}) copy-start(bf16[2,4,1024,128]{2,3,1,0:T(8,128)(2,1)} %copy.18) | copy-start | bytes 6291460
  49.2 2.2 %copy-start.21 = (bf16[512,4096]{1,0:T(8,128)(2,1)S(1)}, bf16[512,4096]{1,0:T(8,128)(2,1)}, u32[]{:S(2)}) copy-start(bf16[512,4096]{1,0:T(8,128)(2,1)} %all-gather.2.cloned.1.call-done) | copy-start | bytes 12582916
  67.6 15.7 %copy-start.1 = (bf16[1,4,1024,128]{2,3,1,0:T(8,128)(2,1)S(1)}, bf16[1,4,1024,128]{2,3,1,0:T(8,128)(2,1)}, u32[]{:S(2)}) copy-start(bf16[1,4,1024,128]{2,3,1,0:T(8,128)(2,1)} %copy.19) | copy-start | bytes 3145732
  67.6 15.7 %copy-start.22 = (bf16[512,4096]{1,0:T(8,128)(2,1)S(1)}, bf16[512,4096]{1,0:T(8,128)(2,1)}, u32[]{:S(2)}) copy-start(bf16[512,4096]{1,0:T(8,128)(2,1)} %all-gather.2.cloned.1.call-done) | copy-start | bytes 12582916
  68.5 17.2 %collective-permute-start = (bf16[4,128,128]{2,1,0:T(8,128)(2,1)}, bf16[4,128,128]{2,1,0:T(8,128)(2,1)S(1)}, u32[]{:S(2)}, u32[]{:S(2)}) collective-permute-start(bf16[4,128,128]{2,1,0:T(8,128)(2,1)} %get-tuple-element.117), channel_id=1, source_target_pairs={{0,8},{8,16},{16,24},{24,32},{32,40},{40,48},{48,56},{56,0},{64,72... | collective-permute-start | bytes 393224 | tf_op jit(solution)/shard_map/ppermute | solution.py:27
  70.1 19.1 %collective-permute-start.1 = (bf16[4,128,128]{2,1,0:T(8,128)(2,1)}, bf16[4,128,128]{2,1,0:T(8,128)(2,1)S(1)}, u32[]{:S(2)}, u32[]{:S(2)}) collective-permute-start(bf16[4,128,128]{2,1,0:T(8,128)(2,1)} %get-tuple-element.117), channel_id=1, source_target_pairs={{0,16},{8,24},{16,32},{24,40},{32,48},{40,56},{48,0},{56,8},{64,80... | collective-permute-start | bytes 393224 | tf_op jit(solution)/shard_map/ppermute | solution.py:27
  72.7 24.1 %collective-permute-start.2 = (bf16[4,128,128]{2,1,0:T(8,128)(2,1)}, bf16[4,128,128]{2,1,0:T(8,128)(2,1)S(1)}, u32[]{:S(2)}, u32[]{:S(2)}) collective-permute-start(bf16[4,128,128]{2,1,0:T(8,128)(2,1)} %get-tuple-element.117), channel_id=1, source_target_pairs={{0,24},{8,32},{16,40},{24,48},{32,56},{40,0},{48,8},{56,16},{64,88... | collective-permute-start | bytes 393224 | tf_op jit(solution)/shard_map/ppermute | solution.py:27
  75.6 21.2 %collective-permute-start.3 = (bf16[4,128,128]{2,1,0:T(8,128)(2,1)}, bf16[4,128,128]{2,1,0:T(8,128)(2,1)}, u32[]{:S(2)}, u32[]{:S(2)}) collective-permute-start(bf16[4,128,128]{2,1,0:T(8,128)(2,1)} %get-tuple-element.117), channel_id=1, source_target_pairs={{0,32},{8,40},{16,48},{24,56},{32,0},{40,8},{48,16},{56,24},{64,96... | collective-permute-start | bytes 393224 | tf_op jit(solution)/shard_map/ppermute | solution.py:27
  77.6 19.5 %collective-permute-start.4 = (bf16[4,128,128]{2,1,0:T(8,128)(2,1)}, bf16[4,128,128]{2,1,0:T(8,128)(2,1)}, u32[]{:S(2)}, u32[]{:S(2)}) collective-permute-start(bf16[4,128,128]{2,1,0:T(8,128)(2,1)} %get-tuple-element.117), channel_id=1, source_target_pairs={{0,40},{8,48},{16,56},{24,0},{32,8},{40,16},{48,24},{56,32},{64,10... | collective-permute-start | bytes 393224 | tf_op jit(solution)/shard_map/ppermute | solution.py:27
  85.8 15.2 %collective-permute-start.5 = (bf16[4,128,128]{2,1,0:T(8,128)(2,1)}, bf16[4,128,128]{2,1,0:T(8,128)(2,1)}, u32[]{:S(2)}, u32[]{:S(2)}) collective-permute-start(bf16[4,128,128]{2,1,0:T(8,128)(2,1)} %get-tuple-element.117), channel_id=1, source_target_pairs={{0,48},{8,56},{16,0},{24,8},{32,16},{40,24},{48,32},{56,40},{64,11... | collective-permute-start | bytes 393224 | tf_op jit(solution)/shard_map/ppermute | solution.py:27
  89.2 12.9 %collective-permute-start.6 = (bf16[4,128,128]{2,1,0:T(8,128)(2,1)}, bf16[4,128,128]{2,1,0:T(8,128)(2,1)}, u32[]{:S(2)}, u32[]{:S(2)}) collective-permute-start(bf16[4,128,128]{2,1,0:T(8,128)(2,1)} %get-tuple-element.117), channel_id=1, source_target_pairs={{0,56},{8,0},{16,8},{24,16},{32,24},{40,32},{48,40},{56,48},{64,12... | collective-permute-start | bytes 393224 | tf_op jit(solution)/shard_map/ppermute | solution.py:27
  92.6 1.3 copy-start.4
  92.6 1.3 copy-start.5
  92.6 1.3 copy-start.6
  92.6 1.3 copy-start.7
  92.6 1.3 copy-start.8
  92.6 1.3 copy-start.9
  92.6 1.3 copy-start.10
  92.6 1.3 copy-start.11
  92.6 1.3 copy-start.12
  92.6 1.3 copy-start.13
  92.7 1.3 copy-start.14
  92.7 1.3 copy-start.15
  92.7 1.3 copy-start.16
  92.7 1.3 copy-start.17
  92.7 1.3 copy-start.18
  92.7 1.3 copy-start.19
  104.1 11.4 %collective-permute-start.7 = (f32[4,128,128]{2,1,0:T(8,128)}, f32[4,128,128]{2,1,0:T(8,128)}, u32[]{:S(2)}, u32[]{:S(2)}) collective-permute-start(f32[4,128,128]{2,1,0:T(8,128)} %convert_add_fusion), channel_id=1, source_target_pairs={{0,64},{8,72},{16,80},{24,88},{32,96},{40,104},{48,112},{56,120},{... | collective-permute-start | bytes 786440 | tf_op jit(solution)/shard_map/ppermute | solution.py:38
  107.6 7.9 %collective-permute-start.8 = (f32[4,128,128]{2,1,0:T(8,128)}, f32[4,128,128]{2,1,0:T(8,128)}, u32[]{:S(2)}, u32[]{:S(2)}) collective-permute-start(f32[4,128,128]{2,1,0:T(8,128)} %convert_add_fusion), channel_id=1, source_target_pairs={{0,128},{8,136},{16,144},{24,152},{32,160},{40,168},{48,176},{56,1... | collective-permute-start | bytes 786440 | tf_op jit(solution)/shard_map/ppermute | solution.py:38
  110.1 5.4 %collective-permute-start.9 = (f32[4,128,128]{2,1,0:T(8,128)}, f32[4,128,128]{2,1,0:T(8,128)}, u32[]{:S(2)}, u32[]{:S(2)}) collective-permute-start(f32[4,128,128]{2,1,0:T(8,128)} %convert_add_fusion), channel_id=1, source_target_pairs={{0,192},{8,200},{16,208},{24,216},{32,224},{40,232},{48,240},{56,2... | collective-permute-start | bytes 786440 | tf_op jit(solution)/shard_map/ppermute | solution.py:38
  113.4 3.9 %copy-start.2 = (f32[4,4,128,128]{3,2,1,0:T(8,128)S(1)}, f32[4,4,128,128]{3,2,1,0:T(8,128)}, u32[]{:S(2)}) copy-start(f32[4,4,128,128]{3,2,1,0:T(8,128)} %fusion.2) | copy-start | bytes 3145732
  117.1 0.8 copy-start.20
Sparse Core Ops, SparseCore 0:
  9.2 37.4 all-gather.1
  125.1 44.6 reduce-scatter.1

commit v9 on v7

--- a/solution.py
+++ b/solution.py
@@ -61,13 +61,16 @@
     ]
     outs = []
     for p in range(projections):
-        summed = None
-        for term_index in range(terms):
-            at = (p * terms + term_index) * cols
-            for c in range(PHM):
-                part = products[c][:, None, at:at + cols] * mixing[p, term_index, c][None, :, None]
-                summed = part if summed is None else summed + part
-        outs.append(summed.astype(jnp.bfloat16).reshape(tok_rows, PHM * cols))
+        blocks_out = []
+        for r in range(PHM):
+            summed = None
+            for term_index in range(terms):
+                at = (p * terms + term_index) * cols
+                for c in range(PHM):
+                    part = products[c][:, at:at + cols] * mixing[p, term_index, c, r]
+                    summed = part if summed is None else summed + part
+            blocks_out.append(summed.astype(jnp.bfloat16))
+        outs.append(jnp.concatenate(blocks_out, axis=1))
     return lax.optimization_barrier(outs)
 
 

time: 177 us -> 272 us (1.54)
  other arithmetic: 18.2 us -> 133 us
  waiting for transfers between devices: 70.3 us -> 60.6 us
  local copies, waits for them, and re-layouts: 28.1 us -> 20 us
    convert_element_type x3 -> x12, other arithmetic: 7.75 us -> 124 us  [project(): blocks_out.append(summed.astype(jnp.bfloat16))]
    mul x76 -> x0, local copies, waits for them, and re-layouts: 15.1 us -> none  [project(): products[c][:, None, at:at + cols] * mixing[p, term_index, c][None, :, None]]
    slice x8 -> x11, local copies, waits for them, and re-layouts: 0.89 us -> 7.7 us  [project(): part = products[c][:, at:at + cols] * mixing[p, term_index, c, r]]
    ppermute x10, waiting for transfers between devices: 14.8 us -> 8.1 us  [ring_gather(): got = lax.ppermute(value, axis, pairs).astype(jnp.float32)]
    unnamed x49 -> x19, local copies, waits for them, and re-layouts: 10.4 us -> 9.4 us
  transfers between devices with their start and end apart: 12 -> 12, of which waited for: 8 -> 5; matrix products, arithmetic and copies ran while one was open for 19% -> 26% of each run, Pallas kernels for 0% -> 0%
where the time goes in v9:
time: 272 us; the launch traced here: 270 us
  other arithmetic  133 us (49%)
  waiting for transfers between devices  60.6 us (22%)
  starting transfers between devices  21.8 us (8%)
  matrix products  20.4 us (7%)
  local copies, waits for them, and re-layouts  20 us (7%)
  between operations  14 us (5%)
    convert_element_type x12, other arithmetic, project(): blocks_out.append(summed.astype(jnp.bfloat16))  124 us
    reduce_scatter x1, waiting for transfers between devices, on_device(): lax.psum_scatter(partial_value.astype(jnp.bfloat16), 'tp', scatter_dimens...  35.3 us
    ppermute x10, starting transfers between devices, ring_gather(): got = lax.ppermute(value, axis, pairs).astype(jnp.float32)  21.8 us
    all_gather x1, waiting for transfers between devices, on_device(): whole = lax.all_gather(tokens, 'tp', axis=1, tiled=True)  16.5 us
    dot_general x8, matrix products, project(): jnp.dot(whole[:, c * rows:(c + 1) * rows], weights, preferred_element_typ...  10.7 us
    unnamed x19, local copies, waits for them, and re-layouts  9.4 us
    ppermute x10, waiting for transfers between devices, ring_gather(): got = lax.ppermute(value, axis, pairs).astype(jnp.float32)  8.1 us
    slice x11, local copies, waits for them, and re-layouts, project(): part = products[c][:, at:at + cols] * mixing[p, term_index, c, r]  7.7 us
  transfers between devices with their start and end apart: 12, of which 5 were waited for; matrix products, arithmetic and copies ran while one was open for 26% of the time, Pallas kernels for 0%

profile of v9, /device:TPU:8, one launch (start us, length us, event | category | flops | bytes accessed | tf_op | source)
XLA Modules:
  0.0 269.7 jit_solution(15784364006472150208)
XLA Ops:
  6.5 0.7 all-gather.2.cloned.1.call-update
  7.5 1.6 slice-done
  9.1 2.7 copy.22
  11.8 1.3 copy.23
  13.1 0.2 bitcast_convert_fusion.3
  13.3 4.8 %add_convert_fusion = bf16[4,128,4,1024]{3,2,1,0:T(4,128)(2,1)S(1)} fusion(f32[128,1024]{1,0:T(8,128)S(1)} %get-tuple-element.15, f32[4,4]{1,0:T(4,128)S(1)} %get-tuple-element.212, f32[128,1024]{1,0:T(8,128)S(1)} %get-tuple-element.16, f32[4,4]{1,0:T(4,128)S(1)} %get-tuple-element.211, f32[128,1024]{1,0:T(8,128)S(1)} %get-tuple-element.14, ...), kind=kLoop, calls=%fused_computation | loop fusion | flops 16777216 | bytes 6291712 | tf_op jit(solution)/shard_map/convert_element_type | solution.py:79
  18.1 4.3 %copy.25 = bf16[64,8,4,1024]{3,1,2,0:T(8,128)(2,1)} copy(bf16[64,8,4,1024]{3,2,1,0:T(4,128)(2,1)S(1)} %bitcast.275) | data formatting | bytes 8388608
  22.5 0.6 fusion.59
  23.1 0.6 fusion.57
  23.7 0.7 fusion.55
  24.4 0.7 fusion.56
  25.1 0.7 fusion.49
  25.9 0.7 fusion.53
  26.6 0.7 fusion.54
  27.3 0.7 fusion.50
  28.1 0.7 fusion.51
  28.8 0.7 fusion.52
  29.5 0.7 fusion.58
  30.2 16.5 %all-gather.2.cloned.1.call-done = bf16[512,4096]{1,0:T(8,128)(2,1)} async-done(((bf16[512,512]{1,0:T(8,128)(2,1)}), bf16[512,4096]{1,0:T(8,128)(2,1)}) %all-gather.2.cloned.1.call-update) | async-done | bytes 4194320 | tf_op jit(solution)/shard_map/all_gather | solution.py:81
  46.7 2.7 fusion.11
  49.3 1.3 fusion.15
  50.6 1.3 fusion.19
  51.9 1.3 fusion.23
  53.2 9.7 %add_convert_fusion.10 = bf16[512,128]{1,0:T(8,128)(2,1)S(1)} fusion(f32[512,1024]{1,0:T(8,128)S(1)} %fusion.11, f32[512,1024]{1,0:T(8,128)S(1)} %fusion.15, f32[512,1024]{1,0:T(8,128)S(1)} %fusion.19, f32[512,1024]{1,0:T(8,128)S(1)} %fusion.23, f32[]{:T(128)} %bitcast.50, f32[]{:T(128)} %bitcast.49, f32[]{:T(128)} %bitcast.48, f32[]{:T(128)} %bitcast.47, ...), kind=kLoop, calls=%fused_computation.85 | loop fusion | flops 2097152 | bytes 4325440 | tf_op jit(solution)/shard_map/convert_element_type | solution.py:72
  63.0 10.2 %add_convert_fusion.11 = bf16[512,128]{1,0:T(8,128)(2,1)S(1)} fusion(f32[512,1024]{1,0:T(8,128)S(1)} %fusion.11, f32[512,1024]{1,0:T(8,128)S(1)} %fusion.15, f32[512,1024]{1,0:T(8,128)S(1)} %fusion.19, f32[512,1024]{1,0:T(8,128)S(1)} %fusion.23, f32[]{:T(128)} %bitcast.34, f32[]{:T(128)} %bitcast.33, f32[]{:T(128)} %bitcast.32, f32[]{:T(128)} %bitcast.31, ...), kind=kLoop, calls=%fused_computation.86 | loop fusion | flops 2097152 | bytes 4325440 | tf_op jit(solution)/shard_map/convert_element_type | solution.py:72
  73.2 10.3 %add_convert_fusion.5 = bf16[512,128]{1,0:T(8,128)(2,1)S(1)} fusion(f32[512,1024]{1,0:T(8,128)S(1)} %fusion.11, f32[512,1024]{1,0:T(8,128)S(1)} %fusion.15, f32[512,1024]{1,0:T(8,128)S(1)} %fusion.19, f32[512,1024]{1,0:T(8,128)S(1)} %fusion.23, f32[]{:T(128)} %bitcast.130, f32[]{:T(128)} %bitcast.129, f32[]{:T(128)} %bitcast.128, f32[]{:T(128)} %bitcast.127, ...), kind=kLoop, calls=%fused_computation.80 | loop fusion | flops 2097152 | bytes 4325440 | tf_op jit(solution)/shard_map/convert_element_type | solution.py:72
  83.5 10.5 %add_convert_fusion.6 = bf16[512,128]{1,0:T(8,128)(2,1)S(1)} fusion(f32[512,1024]{1,0:T(8,128)S(1)} %fusion.11, f32[512,1024]{1,0:T(8,128)S(1)} %fusion.15, f32[512,1024]{1,0:T(8,128)S(1)} %fusion.19, f32[512,1024]{1,0:T(8,128)S(1)} %fusion.23, f32[]{:T(128)} %bitcast.114, f32[]{:T(128)} %bitcast.113, f32[]{:T(128)} %bitcast.112, f32[]{:T(128)} %bitcast.111, ...), kind=kLoop, calls=%fused_computation.81 | loop fusion | flops 2097152 | bytes 4325440 | tf_op jit(solution)/shard_map/convert_element_type | solution.py:72
  94.1 10.3 %add_convert_fusion.7 = bf16[512,128]{1,0:T(8,128)(2,1)S(1)} fusion(f32[512,1024]{1,0:T(8,128)S(1)} %fusion.11, f32[512,1024]{1,0:T(8,128)S(1)} %fusion.15, f32[512,1024]{1,0:T(8,128)S(1)} %fusion.19, f32[512,1024]{1,0:T(8,128)S(1)} %fusion.23, f32[]{:T(128)} %bitcast.98, f32[]{:T(128)} %bitcast.97, f32[]{:T(128)} %bitcast.96, f32[]{:T(128)} %bitcast.95, ...), kind=kLoop, calls=%fused_computation.82 | loop fusion | flops 2097152 | bytes 4325440 | tf_op jit(solution)/shard_map/convert_element_type | solution.py:72
  104.4 10.4 %add_convert_fusion.8 = bf16[512,128]{1,0:T(8,128)(2,1)S(1)} fusion(f32[512,1024]{1,0:T(8,128)S(1)} %fusion.11, f32[512,1024]{1,0:T(8,128)S(1)} %fusion.15, f32[512,1024]{1,0:T(8,128)S(1)} %fusion.19, f32[512,1024]{1,0:T(8,128)S(1)} %fusion.23, f32[]{:T(128)} %bitcast.82, f32[]{:T(128)} %bitcast.81, f32[]{:T(128)} %bitcast.80, f32[]{:T(128)} %bitcast.79, ...), kind=kLoop, calls=%fused_computation.83 | loop fusion | flops 2097152 | bytes 4325440 | tf_op jit(solution)/shard_map/convert_element_type | solution.py:72
  114.8 10.5 %add_convert_fusion.9 = bf16[512,128]{1,0:T(8,128)(2,1)S(1)} fusion(f32[512,1024]{1,0:T(8,128)S(1)} %fusion.11, f32[512,1024]{1,0:T(8,128)S(1)} %fusion.15, f32[512,1024]{1,0:T(8,128)S(1)} %fusion.19, f32[512,1024]{1,0:T(8,128)S(1)} %fusion.23, f32[]{:T(128)} %bitcast.66, f32[]{:T(128)} %bitcast.65, f32[]{:T(128)} %bitcast.64, f32[]{:T(128)} %bitcast.63, ...), kind=kLoop, calls=%fused_computation.84 | loop fusion | flops 2097152 | bytes 4325440 | tf_op jit(solution)/shard_map/convert_element_type | solution.py:72
  125.3 9.9 %add_convert_fusion.12 = bf16[512,128]{1,0:T(8,128)(2,1)S(1)} fusion(f32[512,1024]{1,0:T(8,128)S(1)} %fusion.11, f32[512,1024]{1,0:T(8,128)S(1)} %fusion.15, f32[512,1024]{1,0:T(8,128)S(1)} %fusion.19, f32[512,1024]{1,0:T(8,128)S(1)} %fusion.23, f32[]{:T(128)} %bitcast.18, f32[]{:T(128)} %bitcast.17, f32[]{:T(128)} %bitcast.16, f32[]{:T(128)} %bitcast.15, ...), kind=kLoop, calls=%fused_computation.87 | loop fusion | flops 2097152 | bytes 4325440 | tf_op jit(solution)/shard_map/convert_element_type | solution.py:72
  135.5 0.3 copy.15
  135.9 1.0 fusion.60
  136.9 1.6 collective-permute-start
  138.5 2.5 collective-permute-start.1
  141.0 2.9 %collective-permute-start.2 = (bf16[4,128,128]{2,1,0:T(8,128)(2,1)}, bf16[4,128,128]{2,1,0:T(8,128)(2,1)S(1)}, u32[]{:S(2)}, u32[]{:S(2)}) collective-permute-start(bf16[4,128,128]{2,1,0:T(8,128)(2,1)} %get-tuple-element.213), channel_id=1, source_target_pairs={{0,24},{8,32},{16,40},{24,48},{32,56},{40,0},{48,8},{56,16},{64,88... | collective-permute-start | bytes 393224 | tf_op jit(solution)/shard_map/ppermute | solution.py:27
  144.0 2.0 collective-permute-start.3
  145.9 3.1 %collective-permute-start.4 = (bf16[4,128,128]{2,1,0:T(8,128)(2,1)}, bf16[4,128,128]{2,1,0:T(8,128)(2,1)}, u32[]{:S(2)}, u32[]{:S(2)}) collective-permute-start(bf16[4,128,128]{2,1,0:T(8,128)(2,1)} %get-tuple-element.213), channel_id=1, source_target_pairs={{0,40},{8,48},{16,56},{24,0},{32,8},{40,16},{48,24},{56,32},{64,10... | collective-permute-start | bytes 393224 | tf_op jit(solution)/shard_map/ppermute | solution.py:27
  149.1 2.0 fusion.13
  151.1 0.7 fusion.17
  151.8 0.7 fusion.21
  152.6 0.7 fusion.9
  153.3 10.5 %add_convert_fusion.1 = bf16[512,128]{0,1:T(8,128)(2,1)S(1)} fusion(f32[512,512]{0,1:T(8,128)S(1)} %fusion.9, f32[512,512]{0,1:T(8,128)S(1)} %fusion.13, f32[512,512]{0,1:T(8,128)S(1)} %fusion.17, f32[512,512]{0,1:T(8,128)S(1)} %fusion.21, f32[]{:T(128)} %bitcast.197, f32[]{:T(128)} %bitcast.196, f32[]{:T(128)} %bitcast.195, f32[]{:T(128)} %bitcast.194, ...), kind=kLoop, calls=%fused_computation.76 | loop fusion | flops 2097152 | bytes 4325440 | tf_op jit(solution)/shard_map/convert_element_type | solution.py:72
  163.8 10.4 %add_convert_fusion.2 = bf16[512,128]{0,1:T(8,128)(2,1)S(1)} fusion(f32[512,512]{0,1:T(8,128)S(1)} %fusion.9, f32[512,512]{0,1:T(8,128)S(1)} %fusion.13, f32[512,512]{0,1:T(8,128)S(1)} %fusion.17, f32[512,512]{0,1:T(8,128)S(1)} %fusion.21, f32[]{:T(128)} %bitcast.181, f32[]{:T(128)} %bitcast.180, f32[]{:T(128)} %bitcast.179, f32[]{:T(128)} %bitcast.178, ...), kind=kLoop, calls=%fused_computation.77 | loop fusion | flops 2097152 | bytes 4325440 | tf_op jit(solution)/shard_map/convert_element_type | solution.py:72
  174.2 10.5 %add_convert_fusion.3 = bf16[512,128]{0,1:T(8,128)(2,1)S(1)} fusion(f32[512,512]{0,1:T(8,128)S(1)} %fusion.9, f32[512,512]{0,1:T(8,128)S(1)} %fusion.13, f32[512,512]{0,1:T(8,128)S(1)} %fusion.17, f32[512,512]{0,1:T(8,128)S(1)} %fusion.21, f32[]{:T(128)} %bitcast.165, f32[]{:T(128)} %bitcast.164, f32[]{:T(128)} %bitcast.163, f32[]{:T(128)} %bitcast.162, ...), kind=kLoop, calls=%fused_computation.78 | loop fusion | flops 2097152 | bytes 4325440 | tf_op jit(solution)/shard_map/convert_element_type | solution.py:72
  184.7 3.5 %collective-permute-start.5 = (bf16[4,128,128]{2,1,0:T(8,128)(2,1)}, bf16[4,128,128]{2,1,0:T(8,128)(2,1)}, u32[]{:S(2)}, u32[]{:S(2)}) collective-permute-start(bf16[4,128,128]{2,1,0:T(8,128)(2,1)} %get-tuple-element.213), channel_id=1, source_target_pairs={{0,48},{8,56},{16,0},{24,8},{32,16},{40,24},{48,32},{56,40},{64,11... | collective-permute-start | bytes 393224 | tf_op jit(solution)/shard_map/ppermute | solution.py:27
  188.2 1.4 collective-permute-start.6
  189.6 10.5 %add_convert_fusion.4 = bf16[512,128]{0,1:T(8,128)(2,1)S(1)} fusion(f32[512,512]{0,1:T(8,128)S(1)} %fusion.9, f32[512,512]{0,1:T(8,128)S(1)} %fusion.13, f32[512,512]{0,1:T(8,128)S(1)} %fusion.17, f32[512,512]{0,1:T(8,128)S(1)} %fusion.21, f32[]{:T(128)} %bitcast.149, f32[]{:T(128)} %bitcast.148, f32[]{:T(128)} %bitcast.147, f32[]{:T(128)} %bitcast.146, ...), kind=kLoop, calls=%fused_computation.79 | loop fusion | flops 2097152 | bytes 4325440 | tf_op jit(solution)/shard_map/convert_element_type | solution.py:72
  200.3 0.4 copy.18
  200.7 2.0 convert_add_fusion
  202.7 1.5 collective-permute-start.7
  204.2 1.1 collective-permute-start.8
  205.3 2.1 collective-permute-start.9
  207.5 1.6 fusion.2
  209.1 3.0 %collective-permute-done.7 = f32[4,128,128]{2,1,0:T(8,128)S(1)} collective-permute-done((f32[4,128,128]{2,1,0:T(8,128)}, f32[4,128,128]{2,1,0:T(8,128)S(1)}, u32[]{:S(2)}, u32[]{:S(2)}) %collective-permute-start.7) | collective-permute-done | bytes 262176 | tf_op jit(solution)/shard_map/ppermute | solution.py:27
  212.1 2.9 %collective-permute-done.8 = f32[4,128,128]{2,1,0:T(8,128)S(1)} collective-permute-done((f32[4,128,128]{2,1,0:T(8,128)}, f32[4,128,128]{2,1,0:T(8,128)S(1)}, u32[]{:S(2)}, u32[]{:S(2)}) %collective-permute-start.8) | collective-permute-done | bytes 262176 | tf_op jit(solution)/shard_map/ppermute | solution.py:27
  215.0 2.2 collective-permute-done.9
  217.2 1.3 fusion.44
  218.8 0.9 copy-done.3
  219.7 0.5 multiply_reduce_fusion
  220.4 0.2 multiply_convert_fusion
  220.6 0.3 copy.20
  220.9 6.6 %convolution_convert_fusion = bf16[512,4096]{1,0:T(8,128)(2,1)} fusion(bf16[512,4096]{1,0:T(8,128)(2,1)} %bitcast.276, bf16[64,8,4,128]{3,2,1,0:T(4,128)(2,1)S(1)} %bitcast.287), kind=kOutput, calls=%fused_computation.1 | convolution fusion | flops 2149580800 | bytes 8912896 | tf_op jit(solution)/shard_map/dot_general | solution.py:120
  227.5 35.3 %reduce-scatter.2.cloned.1.call-done = bf16[512,512]{1,0:T(8,128)(2,1)} async-done(((bf16[512,4096]{1,0:T(8,128)(2,1)}), bf16[512,512]{1,0:T(8,128)(2,1)}) %reduce-scatter.2.cloned.1.call-update) | async-done | bytes 524304 | tf_op jit(solution)/shard_map/reduce_scatter | solution.py:121
  (39 shorter events, 1.1 us)
Async XLA Ops:
  6.5 40.1 %all-gather.2.cloned.1.call-start = ((), (), s32[]{:S(2)}) async-start(), calls=%async_computation.1 | async-start | bytes 4718592 | tf_op jit(solution)/shard_map/all_gather | solution.py:81
  7.3 255.6 %reduce-scatter.2.cloned.1.call-start = ((), (), s32[]{:S(2)}) async-start(), calls=%async_computation.2 | async-start | bytes 4718592 | tf_op jit(solution)/shard_map/reduce_scatter | solution.py:121
  7.5 1.6 slice-start
  9.1 2.7 slice-start.1
  11.8 1.3 copy-start.4
  11.8 1.3 copy-start.1
  18.1 28.5 %copy-start = (bf16[2,4,1024,128]{2,3,1,0:T(8,128)(2,1)S(1)}, bf16[2,4,1024,128]{2,3,1,0:T(8,128)(2,1)}, u32[]{:S(2)}) copy-start(bf16[2,4,1024,128]{2,3,1,0:T(8,128)(2,1)} %copy.22) | copy-start | bytes 6291460
  46.7 2.7 copy-start.6
  135.5 13.6 %copy-start.2 = (bf16[1,4,1024,128]{2,3,1,0:T(8,128)(2,1)S(1)}, bf16[1,4,1024,128]{2,3,1,0:T(8,128)(2,1)}, u32[]{:S(2)}) copy-start(bf16[1,4,1024,128]{2,3,1,0:T(8,128)(2,1)} %copy.23) | copy-start | bytes 3145732
  135.9 15.1 %copy-start.7 = (bf16[512,4096]{1,0:T(8,128)(2,1)S(1)}, bf16[512,4096]{1,0:T(8,128)(2,1)}, u32[]{:S(2)}) copy-start(bf16[512,4096]{1,0:T(8,128)(2,1)} %all-gather.2.cloned.1.call-done) | copy-start | bytes 12582916
  136.9 47.8 %collective-permute-start = (bf16[4,128,128]{2,1,0:T(8,128)(2,1)}, bf16[4,128,128]{2,1,0:T(8,128)(2,1)S(1)}, u32[]{:S(2)}, u32[]{:S(2)}) collective-permute-start(bf16[4,128,128]{2,1,0:T(8,128)(2,1)} %get-tuple-element.213), channel_id=1, source_target_pairs={{0,8},{8,16},{16,24},{24,32},{32,40},{40,48},{48,56},{56,0},{64,72... | collective-permute-start | bytes 393224 | tf_op jit(solution)/shard_map/ppermute | solution.py:27
  138.5 49.7 %collective-permute-start.1 = (bf16[4,128,128]{2,1,0:T(8,128)(2,1)}, bf16[4,128,128]{2,1,0:T(8,128)(2,1)S(1)}, u32[]{:S(2)}, u32[]{:S(2)}) collective-permute-start(bf16[4,128,128]{2,1,0:T(8,128)(2,1)} %get-tuple-element.213), channel_id=1, source_target_pairs={{0,16},{8,24},{16,32},{24,40},{32,48},{40,56},{48,0},{56,8},{64,80... | collective-permute-start | bytes 393224 | tf_op jit(solution)/shard_map/ppermute | solution.py:27
  141.0 59.7 %collective-permute-start.2 = (bf16[4,128,128]{2,1,0:T(8,128)(2,1)}, bf16[4,128,128]{2,1,0:T(8,128)(2,1)S(1)}, u32[]{:S(2)}, u32[]{:S(2)}) collective-permute-start(bf16[4,128,128]{2,1,0:T(8,128)(2,1)} %get-tuple-element.213), channel_id=1, source_target_pairs={{0,24},{8,32},{16,40},{24,48},{32,56},{40,0},{48,8},{56,16},{64,88... | collective-permute-start | bytes 393224 | tf_op jit(solution)/shard_map/ppermute | solution.py:27
  144.0 56.7 %collective-permute-start.3 = (bf16[4,128,128]{2,1,0:T(8,128)(2,1)}, bf16[4,128,128]{2,1,0:T(8,128)(2,1)}, u32[]{:S(2)}, u32[]{:S(2)}) collective-permute-start(bf16[4,128,128]{2,1,0:T(8,128)(2,1)} %get-tuple-element.213), channel_id=1, source_target_pairs={{0,32},{8,40},{16,48},{24,56},{32,0},{40,8},{48,16},{56,24},{64,96... | collective-permute-start | bytes 393224 | tf_op jit(solution)/shard_map/ppermute | solution.py:27
  145.9 54.7 %collective-permute-start.4 = (bf16[4,128,128]{2,1,0:T(8,128)(2,1)}, bf16[4,128,128]{2,1,0:T(8,128)(2,1)}, u32[]{:S(2)}, u32[]{:S(2)}) collective-permute-start(bf16[4,128,128]{2,1,0:T(8,128)(2,1)} %get-tuple-element.213), channel_id=1, source_target_pairs={{0,40},{8,48},{16,56},{24,0},{32,8},{40,16},{48,24},{56,32},{64,10... | collective-permute-start | bytes 393224 | tf_op jit(solution)/shard_map/ppermute | solution.py:27
  184.7 16.0 %collective-permute-start.5 = (bf16[4,128,128]{2,1,0:T(8,128)(2,1)}, bf16[4,128,128]{2,1,0:T(8,128)(2,1)}, u32[]{:S(2)}, u32[]{:S(2)}) collective-permute-start(bf16[4,128,128]{2,1,0:T(8,128)(2,1)} %get-tuple-element.213), channel_id=1, source_target_pairs={{0,48},{8,56},{16,0},{24,8},{32,16},{40,24},{48,32},{56,40},{64,11... | collective-permute-start | bytes 393224 | tf_op jit(solution)/shard_map/ppermute | solution.py:27
  188.2 12.5 %collective-permute-start.6 = (bf16[4,128,128]{2,1,0:T(8,128)(2,1)}, bf16[4,128,128]{2,1,0:T(8,128)(2,1)}, u32[]{:S(2)}, u32[]{:S(2)}) collective-permute-start(bf16[4,128,128]{2,1,0:T(8,128)(2,1)} %get-tuple-element.213), channel_id=1, source_target_pairs={{0,56},{8,0},{16,8},{24,16},{32,24},{40,32},{48,40},{56,48},{64,12... | collective-permute-start | bytes 393224 | tf_op jit(solution)/shard_map/ppermute | solution.py:27
  202.7 9.4 %collective-permute-start.7 = (f32[4,128,128]{2,1,0:T(8,128)}, f32[4,128,128]{2,1,0:T(8,128)S(1)}, u32[]{:S(2)}, u32[]{:S(2)}) collective-permute-start(f32[4,128,128]{2,1,0:T(8,128)} %convert_add_fusion), channel_id=1, source_target_pairs={{0,64},{8,72},{16,80},{24,88},{32,96},{40,104},{48,112},{56,120},{... | collective-permute-start | bytes 786440 | tf_op jit(solution)/shard_map/ppermute | solution.py:27
  204.2 10.8 %collective-permute-start.8 = (f32[4,128,128]{2,1,0:T(8,128)}, f32[4,128,128]{2,1,0:T(8,128)S(1)}, u32[]{:S(2)}, u32[]{:S(2)}) collective-permute-start(f32[4,128,128]{2,1,0:T(8,128)} %convert_add_fusion), channel_id=1, source_target_pairs={{0,128},{8,136},{16,144},{24,152},{32,160},{40,168},{48,176},{56,1... | collective-permute-start | bytes 786440 | tf_op jit(solution)/shard_map/ppermute | solution.py:27
  205.3 11.9 %collective-permute-start.9 = (f32[4,128,128]{2,1,0:T(8,128)}, f32[4,128,128]{2,1,0:T(8,128)}, u32[]{:S(2)}, u32[]{:S(2)}) collective-permute-start(f32[4,128,128]{2,1,0:T(8,128)} %convert_add_fusion), channel_id=1, source_target_pairs={{0,192},{8,200},{16,208},{24,216},{32,224},{40,232},{48,240},{56,2... | collective-permute-start | bytes 786440 | tf_op jit(solution)/shard_map/ppermute | solution.py:27
  218.5 1.2 copy-start.3
  219.7 0.7 copy-start.5
Sparse Core Ops, SparseCore 0:
  9.2 37.4 all-gather.1
  227.6 35.1 reduce-scatter.1
